TPU v7x, 512 devices: a whole 4x8x8 slice. The times are simulated.
512 devices in a mesh: dom: 64 (over z, y), tile: 8 (over x, core).
Axes of the slice: x: 4, y: 8, z: 8, core: 2. Of those that a mesh axis runs over, the one named last changes fastest.
Arguments:
- geometry: float32 [5, 1572864], P(None, 'dom'), may hold values from -4 to 1056, as said below
- opacity: float32 [1572864], P('dom'), may hold values from -7 to -2.5
- colours: float32 [3, 1572864], P(None, 'dom'), may hold values from -6 to 6
- coverage: int32 [64, 8, 12], P('dom', 'tile'), may hold values from -1 to 127, as said below
- gauss_lists: int32 [64, 8, 12, 256], P('dom', 'tile'), may hold values from -1 to 24575, as said below
- orders: int32 [1024, 64], P(('dom', 'tile')), may hold values from 0 to 63, each once within a row
- cotangent: float32 [3, 1024, 256], P(None, ('dom', 'tile')), may hold values from -6 to 6
Outputs:
- rendered: float32 [3, 1024, 256], P(None, ('dom', 'tile'))
- grad_geometry: float32 [5, 1572864], P(None, ('dom', 'tile'))
- grad_opacity: float32 [1572864], P(('dom', 'tile'))
- grad_colours: float32 [3, 1572864], P(None, ('dom', 'tile'))
Inputs may be any that keep to these rules, and one draw needn't show every extreme that they name: `geometry`: Rows: centre x and y, two log standard deviations, angle. `coverage`: partition d covers the same number of tiles, 1 to 12, in every group; covered tiles of a group come first in increasing order, at most one in each block of 2 tiles, then -1; exactly one partition covers 12 tiles in every group. `gauss_lists`: A covered slot lists 1 to 256 Gaussians of the partition front to back, then -1; every device has a slot with exactly 256; an uncovered slot holds only -1; a Gaussian appears at most once in its partition. `orders`: each tile's row is a permutation of the partitions.
All inputs are finite; a program needn't handle non-finite values.
Results may differ from a plain program's by a relative error of at most 0.0003.
Values sent between devices are 32-bit elements; how exact they have to be, the bound alone decides.
No kernel may reach another device: no remote copies, remote signals or barrier semaphores. Data moves between devices by JAX's collectives and lax.ppermute only.
A program may use at most 128 MiB of HBM per device.

v0:
```python
import math

import jax
import jax.numpy as jnp
from jax import lax
from jax.sharding import PartitionSpec as P

TSIDE = 16


def render(params, pixel_x, pixel_y, live_mask):
    centre_x = params[0][:, None, :]
    centre_y = params[1][:, None, :]
    inv_one = jnp.exp(-2.0 * params[2])
    inv_two = jnp.exp(-2.0 * params[3])
    cosine = jnp.cos(params[4])
    sine_angle = jnp.sin(params[4])
    coef_a = (cosine * cosine * inv_one + sine_angle * sine_angle * inv_two)[:, None, :]
    coef_b = (cosine * sine_angle * (inv_one - inv_two))[:, None, :]
    coef_c = (sine_angle * sine_angle * inv_one + cosine * cosine * inv_two)[:, None, :]
    delta_x = pixel_x[:, :, None] - centre_x
    delta_y = pixel_y[:, :, None] - centre_y
    quadratic = (
        coef_a * delta_x * delta_x + 2.0 * coef_b * delta_x * delta_y + coef_c * delta_y * delta_y
    )
    strength = jax.nn.sigmoid(params[5]) * live_mask
    opaque_part = strength[:, None, :] * jnp.exp(-0.5 * quadratic)
    log_keep = jnp.log1p(-opaque_part)
    running = jnp.cumsum(log_keep, axis=2)
    before = jnp.concatenate([jnp.zeros_like(running[:, :, :1]), running[:, :, :-1]], axis=2)
    weight = opaque_part * jnp.exp(before)
    colour = jnp.einsum("kpg,ckg->kcp", weight, params[6:9], precision=lax.Precision.HIGHEST)
    transmit = jnp.exp(jnp.sum(log_keep, axis=2))
    return (colour, transmit)


def pixel_grid(tile_ids, group_index, tiles_per, pixels):
    safe_ids = jnp.maximum(tile_ids, 0)
    block_row = safe_ids // tiles_per
    column = group_index * tiles_per + safe_ids % tiles_per
    within = jnp.arange(pixels, dtype=jnp.int32)
    pixel_x = (column[:, None] * TSIDE + within[None, :] % TSIDE).astype(jnp.float32) + 0.5
    pixel_y = (block_row[:, None] * TSIDE + within[None, :] // TSIDE).astype(jnp.float32) + 0.5
    return (pixel_x, pixel_y)


def composite(arrived, orders, cotangent):
    parts_count = arrived.shape[0]
    ranks_onehot = (
        orders[:, None, :] == jnp.arange(parts_count, dtype=jnp.int32)[None, :, None]
    ).astype(jnp.float32)
    ordered = jnp.einsum("irk,kicp->ircp", ranks_onehot, arrived, precision=lax.Precision.HIGHEST)
    colour = ordered[:, :, :3]
    transmit = ordered[:, :, 3]
    running = jnp.cumprod(transmit, axis=1)
    prefix = jnp.concatenate([jnp.ones_like(running[:, :1]), running[:, :-1]], axis=1)
    rendered = jnp.sum(prefix[:, :, None, :] * colour, axis=1)

    def compose(earlier, later):
        return (earlier[0] * later[0], later[1] + later[0][:, :, None, :] * earlier[1])

    flipped = lax.associative_scan(compose, (transmit[:, ::-1], colour[:, ::-1]), axis=1)
    suffix = flipped[1][:, ::-1]
    behind = jnp.concatenate([suffix[:, 1:], jnp.zeros_like(suffix[:, :1])], axis=1)
    upstream_cot = jnp.transpose(cotangent, (1, 0, 2))
    grad_colour = prefix[:, :, None, :] * upstream_cot[:, None]
    grad_transmit = prefix * jnp.sum(upstream_cot[:, None] * behind, axis=2)
    grad_ordered = jnp.concatenate([grad_colour, grad_transmit[:, :, None, :]], axis=2)
    upstream = jnp.einsum(
        "irk,ircp->kicp", ranks_onehot, grad_ordered, precision=lax.Precision.HIGHEST
    )
    return (jnp.transpose(rendered, (1, 0, 2)), upstream)


def local(geometry, opacity, colours, coverage, gauss_lists, orders, cotangent):
    parts_count = lax.axis_size("dom")
    group_index = lax.axis_index("tile")
    tiles_per = orders.shape[0]
    pixels = cotangent.shape[2]
    params = jnp.concatenate([geometry, opacity[None, :], colours], axis=0)
    gauss_total = params.shape[1]
    tile_ids = coverage[0, 0]
    entries = gauss_lists[0, 0]
    slots_count = tile_ids.shape[0]
    turn_rows = math.gcd(slots_count, 4)
    covered = jnp.sum((tile_ids >= 0).astype(jnp.int32))
    turn_count = (covered + turn_rows - 1) // turn_rows
    pixel_x, pixel_y = pixel_grid(tile_ids, group_index, tiles_per, pixels)
    default = jnp.concatenate(
        [jnp.zeros((3, pixels), jnp.float32), jnp.ones((1, pixels), jnp.float32)], axis=0
    )

    def gather_turn(first_row):
        index_rows = lax.dynamic_slice_in_dim(entries, first_row, turn_rows, 0)
        live = index_rows >= 0
        chosen = jnp.take(params, jnp.where(live, index_rows, 0), axis=1)
        rows_x = lax.dynamic_slice_in_dim(pixel_x, first_row, turn_rows, 0)
        rows_y = lax.dynamic_slice_in_dim(pixel_y, first_row, turn_rows, 0)
        return (index_rows, live.astype(jnp.float32), chosen, rows_x, rows_y)

    def forward_turn(turn_index, partial_value):
        first_row = turn_index * turn_rows
        index_rows, live_mask, chosen, rows_x, rows_y = gather_turn(first_row)
        colour, transmit = render(chosen, rows_x, rows_y, live_mask)
        packed = jnp.concatenate([colour, transmit[:, None, :]], axis=1)
        return lax.dynamic_update_slice_in_dim(partial_value, packed, first_row, 0)

    partial_value = lax.fori_loop(
        0, turn_count, forward_turn, jnp.broadcast_to(default, (slots_count, 4, pixels))
    )
    block_slots = parts_count * tiles_per
    target = jnp.where(tile_ids >= 0, tile_ids, block_slots)
    dense = (
        jnp.broadcast_to(default, (block_slots, 4, pixels))
        .at[target]
        .set(partial_value, mode="drop")
    )
    arrived = lax.all_to_all(
        dense.reshape(parts_count, tiles_per, 4, pixels),
        "dom",
        split_axis=0,
        concat_axis=0,
        tiled=True,
    )
    rendered, upstream = composite(arrived, orders, cotangent)
    returned = lax.all_to_all(upstream, "dom", split_axis=0, concat_axis=0, tiled=True)
    slot_grads = jnp.take(
        returned.reshape(block_slots, 4, pixels), jnp.maximum(tile_ids, 0), axis=0
    )

    def backward_turn(turn_index, grads):
        first_row = turn_index * turn_rows
        index_rows, live_mask, chosen, rows_x, rows_y = gather_turn(first_row)
        upper_cot = lax.dynamic_slice_in_dim(slot_grads, first_row, turn_rows, 0)
        _, pullback = jax.vjp(lambda values: render(values, rows_x, rows_y, live_mask), chosen)
        grad_chosen = pullback((upper_cot[:, :3], upper_cot[:, 3]))[0]
        target_rows = jnp.where(index_rows >= 0, index_rows, gauss_total)
        return grads.at[:, target_rows].add(grad_chosen, mode="drop")

    grads = lax.fori_loop(0, turn_count, backward_turn, jnp.zeros((9, gauss_total), jnp.float32))
    shares = lax.psum_scatter(grads, "tile", scatter_dimension=1, tiled=True)
    return (rendered, shares[:5], shares[5], shares[6:])


def solution(mesh):
    placed = (
        P(None, "dom"),
        P("dom"),
        P(None, "dom"),
        P("dom", "tile", None),
        P("dom", "tile", None, None),
        P(("dom", "tile"), None),
        P(None, ("dom", "tile"), None),
    )
    return jax.shard_map(
        local,
        mesh=mesh,
        in_specs=placed,
        out_specs=(
            P(None, ("dom", "tile"), None),
            P(None, ("dom", "tile")),
            P(("dom", "tile")),
            P(None, ("dom", "tile")),
        ),
        check_vma=False,
    )
```

profile of v0, /device:TPU:1, one launch (start us, length us, event | category | flops | bytes accessed | tf_op | source)
XLA Modules:
  0.0 323.6 jit_solution(1440787683847271146)
XLA Ops:
  7.2 1.3 fusion.137
  9.2 0.7 fusion.141
  9.8 0.7 fusion.142
  10.5 0.7 copy.173
  11.2 1.7 pad_maximum_fusion
  12.9 6.9 %copy.123 = f32[9,24576]{0,1:T(8,128)} copy(f32[9,24576]{1,0:T(8,128)S(1)} %pad_maximum_fusion) | data formatting | bytes 1769472 | tf_op jit(solution)/shard_map/while | solution.py:108
  19.8 15.9 %while.20 = (s32[]{:T(128)}, f32[12,4,256]{2,1,0:T(4,128)S(1)}, s32[]{:T(128)}, s32[12,256]{1,0:T(8,128)S(1)}, f32[9,24576]{0,1:T(8,128)}, /*index=5*/f32[12,256...) while((s32[]{:T(128)}, f32[12,4,256]{2,1,0:T(4,128)S(1)}, ...), condition=%wide.region_5.7_spmd, body=%wide.region_1.6_spmd.sunk | while | flops 53526532 | bytes 6969531 | solution.py:108
  20.0 7.4 %gather_fusion = f32[1024,9]{1,0:T(8,128)S(1)} fusion(f32[9,24576]{0,1:T(8,128)} %get-tuple-element.402, s32[1024]{0:T(1024)S(1)} %broadcast_clamp_fusion.4), kind=kCustom, calls=%fused_computation.clone.clone.1 | custom fusion | bytes 77824 | tf_op jit(solution)/shard_map/while/body/jit(_take)/gather | solution.py:96
  27.3 0.2 copy.209
  27.6 0.2 fusion.174
  27.8 1.1 log-plus-one_reduce_fusion.4
  28.9 0.1 copy.216
  29.0 0.1 copy.215
  29.2 0.1 copy.214
  29.4 0.1 copy.213
  29.5 0.1 copy.212
  29.7 0.1 copy.211
  29.8 3.8 %fusion.175 = f32[4,256,2,128]{1,2,3,0:T(2,128)S(1)} fusion(f32[4,2,128]{1,2,0:T(8,128)S(1)} %copy.211, f32[4,2,128]{1,2,0:T(8,128)S(1)} %copy.212, f32[4,256]{1,0:T(4,128)S(1)} %get-tuple-element.334, f32[4,2,128]{1,2,0:T(8,128)S(1)} %copy.213, f32[4,2,128]{1,2,0:T(8,128)S(1)} %copy.214, f32[4,256]{1,0:T(4,128)S(1)} %constant_dynamic-slice_fusion.8, ...), kind=kOutput, calls=%fused_computation.24.clone.1 | output fusion | flops 36700160 | bytes 1081344 | tf_op jit(solution)/shard_map/reduce-window
  33.7 0.4 broadcast_add_fusion.6
  34.1 1.6 fusion.176
  35.8 0.9 broadcast_in_dim.49
  36.7 2.3 scatter_fusion.1
  39.0 43.1 %all-to-all-start = ((f32[64,2,4,256]{3,2,1,0:T(4,128)}), f32[64,2,4,256]{3,2,1,0:T(4,128)S(1)}, u32[]{:S(2)}, u32[]{:S(2)}) async-start(f32[64,2,4,256]{3,2,1,0:T(4,128)} %bitcast.38), calls=%async_computation | async-start | bytes 1048576 | tf_op jit(solution)/shard_map/all_to_all | solution.py:118
  82.1 17.4 %all-to-all-done = f32[64,2,4,256]{3,2,1,0:T(4,128)S(1)} async-done(((f32[64,2,4,256]{3,2,1,0:T(4,128)}), f32[64,2,4,256]{3,2,1,0:T(4,128)S(1)}, u32[]{:S(2)}, u32[]{:S(2)}) %all-to-all-start) | async-done | bytes 524320 | tf_op jit(solution)/shard_map/all_to_all | solution.py:118
  99.5 0.6 fusion.123
  100.7 0.1 reduce_window.9
  100.9 0.1 slice.261
  101.1 0.1 slice.257
  101.2 0.1 slice.265
  102.9 0.1 slice.258
  104.1 0.1 pad.101
  104.4 0.2 slice.306
  104.7 0.4 convolution_bitcast_fusion
  105.1 1.2 copy.127
  106.3 6.7 %all-to-all-start.1 = ((f32[64,2,4,256]{3,2,1,0:T(4,128)}), f32[64,2,4,256]{3,2,1,0:T(4,128)S(1)}, u32[]{:S(2)}, u32[]{:S(2)}) async-start(f32[64,2,4,256]{3,2,1,0:T(4,128)} %copy.127), calls=%async_computation.1 | async-start | bytes 1048576 | tf_op jit(solution)/shard_map/all_to_all | solution.py:126
  113.0 16.5 %all-to-all-done.1 = f32[64,2,4,256]{3,2,1,0:T(4,128)S(1)} async-done(((f32[64,2,4,256]{3,2,1,0:T(4,128)}), f32[64,2,4,256]{3,2,1,0:T(4,128)S(1)}, u32[]{:S(2)}, u32[]{:S(2)}) %all-to-all-start.1) | async-done | bytes 524320 | tf_op jit(solution)/shard_map/all_to_all | solution.py:126
  129.6 0.6 gather_fusion.2
  130.2 4.7 %broadcast_in_dim.53 = f32[9,24576]{0,1:T(8,128)} broadcast(f32[]{:T(128)} %constant.173.clone.1), dimensions={} | broadcast | bytes 884740 | tf_op jit(solution)/shard_map/broadcast_in_dim | solution.py:140
  135.0 45.2 %while.21 = (s32[]{:T(128)}, f32[9,24576]{0,1:T(8,128)}, s32[]{:T(128)}, s32[12,256]{1,0:T(8,128)S(1)}, f32[12,4,256]{2,1,0:T(4,128)S(1)}, /*index=5*/f32[9,2457...) while((s32[]{:T(128)}, f32[9,24576]{0,1:T(8,128)}, ...), condition=%wide.region_23.25_spmd, body=%wide.region_10.24_spmd.sunk | while | flops 108697600 | bytes 25286888 | solution.py:140
  135.1 7.4 %gather_fusion.1 = f32[1024,9]{1,0:T(8,128)S(1)} fusion(f32[9,24576]{0,1:T(8,128)} %get-tuple-element.443, s32[1024]{0:T(1024)S(1)} %broadcast_clamp_fusion.5), kind=kCustom, calls=%fused_computation.1.clone.clone.1 | custom fusion | bytes 77824 | tf_op jit(solution)/shard_map/while/body/jit(_take)/gather | solution.py:96
  142.5 0.2 copy.223
  142.9 0.1 copy.228
  143.0 0.1 copy.226
  143.2 0.1 copy.224
  143.3 0.1 copy.227
  143.5 0.1 copy.225
  143.7 0.1 copy.229
  143.8 3.8 %fusion.186 = f32[4,256,2,128]{1,2,3,0:T(2,128)S(1)} fusion(f32[4,2,128]{1,2,0:T(8,128)S(1)} %copy.224, f32[4,2,128]{1,2,0:T(8,128)S(1)} %copy.225, f32[4,256]{1,0:T(4,128)S(1)} %get-tuple-element.354, f32[4,2,128]{1,2,0:T(8,128)S(1)} %copy.226, f32[4,2,128]{1,2,0:T(8,128)S(1)} %copy.227, f32[4,256]{1,0:T(4,128)S(1)} %get-tuple-element.356, ...), kind=kOutput, calls=%fused_computation.111.clone.1 | output fusion | flops 36700160 | bytes 1081344 | tf_op jit(solution)/shard_map/reduce-window.2
  147.6 0.4 broadcast_add_fusion.7
  148.1 1.9 fusion.191
  150.0 1.0 fusion.185
  151.1 0.9 log-plus-one_reduce_fusion.5
  152.0 0.3 exponential_multiply_fusion.2
  152.4 9.2 %fusion.187 = f32[4,256,2,128]{1,2,3,0:T(2,128)S(1)} fusion(f32[4,256,2,128]{1,3,2,0:T(8,128)S(1)} %bitcast.283), kind=kOutput, calls=%fused_computation.125.clone.1 | output fusion | flops 33292288 | bytes 2097152 | tf_op jit(solution)/shard_map/reduce-window.4
  161.7 0.4 broadcast_add_fusion.8
  162.2 3.2 fusion.188
  165.5 0.2 copy.233
  165.7 14.5 %scatter_fusion = f32[9,24576]{0,1:T(8,128)} fusion(f32[9,24576]{0,1:T(8,128)} %get-tuple-element.425, s32[1024]{0:T(1024)S(1)} %bitcast.307, f32[1024,9]{1,0:T(8,128)S(1)} %bitcast.285), kind=kCustom, calls=%fused_computation.3.clone.1 | custom fusion | flops 9216 | bytes 114688 | tf_op jit(solution)/shard_map/while/body/scatter-add | solution.py:138
  180.2 8.5 %copy.129 = f32[9,24576]{1,0:T(8,128)} copy(f32[9,24576]{0,1:T(8,128)} %get-tuple-element.87) | data formatting | bytes 1769472 | tf_op jit(solution)/shard_map/while | solution.py:140
  188.7 0.6 copy.130
  189.3 122.9 %reduce-scatter.2.cloned.1.call-done = f32[9,3072]{1,0:T(8,128)} async-done(((f32[9,24576]{1,0:T(8,128)}), f32[9,3072]{1,0:T(8,128)}) %reduce-scatter.2.cloned.1.call-update) | async-done | bytes 110608 | tf_op jit(solution)/shard_map/reduce_scatter | solution.py:141
  312.1 1.5 slice.363
  313.6 1.6 slice.364
  315.2 1.5 slice.362
  (147 shorter events, 4.3 us)
Async XLA Ops:
  7.2 12.7 %copy-start = (f32[4,256]{1,0:T(4,128)S(1)}, f32[4,256]{1,0:T(4,128)}, u32[]{:S(2)}) copy-start(f32[4,256]{1,0:T(4,128)} %constant.160.clone.1) | copy-start | bytes 12292
  19.8 62.3 %copy-start.1 = (f32[3,2,256]{2,1,0:T(2,128)S(1)}, f32[3,2,256]{2,1,0:T(2,128)}, u32[]{:S(2)}) copy-start(f32[3,2,256]{2,1,0:T(2,128)} %param.19) | copy-start | bytes 18436
  19.8 79.7 %copy-start.2 = (s32[2,64]{1,0:T(2,128)S(1)}, s32[2,64]{1,0:T(2,128)}, u32[]{:S(2)}) copy-start(s32[2,64]{1,0:T(2,128)} %param.18) | copy-start | bytes 1540
  35.8 77.2 %copy-start.3 = (s32[1,1,12]{2,1,0:T(1,128)S(1)}, s32[1,1,12]{2,1,0:T(1,128)}, u32[]{:S(2)}) copy-start(s32[1,1,12]{2,1,0:T(1,128)} %param.16) | copy-start | bytes 148
  39.0 60.5 %all-to-all-start = ((f32[64,2,4,256]{3,2,1,0:T(4,128)}), f32[64,2,4,256]{3,2,1,0:T(4,128)S(1)}, u32[]{:S(2)}, u32[]{:S(2)}) async-start(f32[64,2,4,256]{3,2,1,0:T(4,128)} %bitcast.38), calls=%async_computation | async-start | bytes 1048576 | tf_op jit(solution)/shard_map/all_to_all | solution.py:118
  106.3 23.3 %all-to-all-start.1 = ((f32[64,2,4,256]{3,2,1,0:T(4,128)}), f32[64,2,4,256]{3,2,1,0:T(4,128)S(1)}, u32[]{:S(2)}, u32[]{:S(2)}) async-start(f32[64,2,4,256]{3,2,1,0:T(4,128)} %copy.127), calls=%async_computation.1 | async-start | bytes 1048576 | tf_op jit(solution)/shard_map/all_to_all | solution.py:126
  112.9 199.2 %reduce-scatter.2.cloned.1.call-start = ((), (), s32[]{:S(2)}) async-start(), calls=%async_computation.3 | async-start | bytes 1769472 | tf_op jit(solution)/shard_map/reduce_scatter | solution.py:141
Sparse Core Ops, SparseCore 0:
  188.8 123.3 reduce-scatter.1
where the time goes:
time: 325 us; the launch traced here: 324 us
  waiting for transfers between devices  157 us (48%)
  local copies, waits for them, and re-layouts  52 us (16%)
  starting transfers between devices  49.8 us (15%)
  other arithmetic  43.5 us (13%)
  between operations  15.4 us (5%)
  matrix products  5.59 us (2%)
    reduce_scatter x1, waiting for transfers between devices, local(): shares = lax.psum_scatter(grads, 'tile', scatter_dimension=1, tiled=True)  123 us
    all_to_all x1, starting transfers between devices, local(): lax.all_to_all(dense.reshape(parts_count, tiles_per, 4, pixels), 'dom', s...  43.1 us
    another operation x9, other arithmetic  17.9 us
    all_to_all x1, waiting for transfers between devices, local(): lax.all_to_all(dense.reshape(parts_count, tiles_per, 4, pixels), 'dom', s...  17.4 us
    all_to_all x1, waiting for transfers between devices, local(): lax.all_to_all(upstream, 'dom', split_axis=0, concat_axis=0, tiled=True)  16.5 us
    gather x4, local copies, waits for them, and re-layouts, gather_turn(): chosen = jnp.take(params, jnp.where(live, index_rows, 0), axis=1)  15.1 us
    scatter-add x1, other arithmetic, backward_turn(): return grads.at[:, target_rows].add(grad_chosen, mode='drop')  14.5 us
    while x1, local copies, waits for them, and re-layouts, local(): lax.fori_loop(0, turn_count, backward_turn, jnp.zeros((9, gauss_total), j...  8.49 us
  transfers between devices with their start and end apart: 3, of which 3 were waited for; matrix products, arithmetic and copies ran while one was open for 0% of the time, Pallas kernels for 0%

commit v1 on v0

--- a/solution.py
+++ b/solution.py
@@ -90,13 +90,17 @@
         [jnp.zeros((3, pixels), jnp.float32), jnp.ones((1, pixels), jnp.float32)], axis=0
     )
 
+    live_all = entries >= 0
+    chosen_all = jnp.take(params, jnp.where(live_all, entries, 0), axis=1)
+    live_all_f = live_all.astype(jnp.float32)
+
     def gather_turn(first_row):
         index_rows = lax.dynamic_slice_in_dim(entries, first_row, turn_rows, 0)
-        live = index_rows >= 0
-        chosen = jnp.take(params, jnp.where(live, index_rows, 0), axis=1)
+        live = lax.dynamic_slice_in_dim(live_all_f, first_row, turn_rows, 0)
+        chosen = lax.dynamic_slice_in_dim(chosen_all, first_row, turn_rows, 1)
         rows_x = lax.dynamic_slice_in_dim(pixel_x, first_row, turn_rows, 0)
         rows_y = lax.dynamic_slice_in_dim(pixel_y, first_row, turn_rows, 0)
-        return (index_rows, live.astype(jnp.float32), chosen, rows_x, rows_y)
+        return (index_rows, live, chosen, rows_x, rows_y)
 
     def forward_turn(turn_index, partial_value):
         first_row = turn_index * turn_rows
@@ -128,17 +132,49 @@
         returned.reshape(block_slots, 4, pixels), jnp.maximum(tile_ids, 0), axis=0
     )
 
-    def backward_turn(turn_index, grads):
+    def backward_turn(turn_index, compact):
         first_row = turn_index * turn_rows
         index_rows, live_mask, chosen, rows_x, rows_y = gather_turn(first_row)
         upper_cot = lax.dynamic_slice_in_dim(slot_grads, first_row, turn_rows, 0)
         _, pullback = jax.vjp(lambda values: render(values, rows_x, rows_y, live_mask), chosen)
         grad_chosen = pullback((upper_cot[:, :3], upper_cot[:, 3]))[0]
-        target_rows = jnp.where(index_rows >= 0, index_rows, gauss_total)
-        return grads.at[:, target_rows].add(grad_chosen, mode="drop")
-
-    grads = lax.fori_loop(0, turn_count, backward_turn, jnp.zeros((9, gauss_total), jnp.float32))
-    shares = lax.psum_scatter(grads, "tile", scatter_dimension=1, tiled=True)
+        return lax.dynamic_update_slice_in_dim(compact, grad_chosen, first_row, 1)
+
+    compact = lax.fori_loop(
+        0, turn_count, backward_turn, jnp.zeros(chosen_all.shape, jnp.float32)
+    )
+    rows_count = params.shape[0]
+    groups_count = lax.axis_size("tile")
+    shard = gauss_total // groups_count
+    lo_size = 48 if shard % 48 == 0 else 1
+    hi_size = gauss_total // lo_size
+    values = jnp.where(live_all[None], compact, 0.0)
+    values = jnp.transpose(values, (1, 2, 0)).reshape(-1, rows_count)
+    flat_index = jnp.where(live_all, entries, -1).reshape(-1)
+    hi_index = jnp.where(flat_index >= 0, flat_index // lo_size, -1)
+    lo_index = flat_index % lo_size
+    hi_hot = (hi_index[:, None] == jnp.arange(hi_size, dtype=jnp.int32)[None, :]).astype(
+        jnp.float32
+    )
+    lo_hot = (lo_index[:, None] == jnp.arange(lo_size, dtype=jnp.int32)[None, :]).astype(
+        jnp.float32
+    )
+    spread = (lo_hot[:, :, None] * values[:, None, :]).reshape(-1, lo_size * rows_count)
+    placed = jnp.einsum("eh,ez->hz", hi_hot, spread, precision=lax.Precision.HIGHEST)
+    blocks = placed.reshape(groups_count, hi_size // groups_count, lo_size * rows_count)
+    total = lax.dynamic_index_in_dim(blocks, group_index, 0, keepdims=False)
+    for step in range(1, groups_count):
+        outgoing = lax.dynamic_index_in_dim(
+            blocks, (group_index + step) % groups_count, 0, keepdims=False
+        )
+        total = total + lax.ppermute(
+            outgoing,
+            "tile",
+            perm=[(i, (i + step) % groups_count) for i in range(groups_count)],
+        )
+    shares = jnp.transpose(
+        total.reshape(hi_size // groups_count, lo_size, rows_count), (2, 0, 1)
+    ).reshape(rows_count, shard)
     return (rendered, shares[:5], shares[5], shares[6:])
 
 

time: 325 us -> 271 us (0.83)
  the two profiles are of different devices: /device:TPU:1 before, /device:TPU:224 now
where the time goes in v1:
time: 271 us; the launch traced here: 268 us
  other arithmetic  103 us (38%)
  local copies, waits for them, and re-layouts  64.1 us (24%)
  starting transfers between devices  38.4 us (14%)
  waiting for transfers between devices  32.2 us (12%)
  matrix products  27.1 us (10%)
    another operation x27, other arithmetic  57.1 us
    dot_general x9, matrix products, render(): jnp.einsum('kpg,ckg->kcp', weight, params[6:9], precision=lax.Precision.H...  17.3 us
    ppermute x7, starting transfers between devices, local(): lax.ppermute(outgoing, 'tile', perm=[(i, (i + step) % groups_count) for i...  17.2 us
    all_to_all x1, waiting for transfers between devices, local(): lax.all_to_all(dense.reshape(parts_count, tiles_per, 4, pixels), 'dom', s...  14 us
    gather x2, local copies, waits for them, and re-layouts, local(): chosen_all = jnp.take(params, jnp.where(live_all, entries, 0), axis=1)  13.3 us
    all_to_all x1, waiting for transfers between devices, local(): lax.all_to_all(upstream, 'dom', split_axis=0, concat_axis=0, tiled=True)  11.3 us
    all_to_all x1, starting transfers between devices, local(): lax.all_to_all(upstream, 'dom', split_axis=0, concat_axis=0, tiled=True)  10.7 us
    all_to_all x1, starting transfers between devices, local(): lax.all_to_all(dense.reshape(parts_count, tiles_per, 4, pixels), 'dom', s...  10.5 us
  transfers between devices with their start and end apart: 9, of which 5 were waited for; matrix products, arithmetic and copies ran while one was open for 1% of the time, Pallas kernels for 0%

profile of v1, /device:TPU:224, one launch (start us, length us, event | category | flops | bytes accessed | tf_op | source)
XLA Modules:
  0.0 268.4 jit_solution(2090172585293736883)
XLA Ops:
  1.3 1.3 fusion.145
  4.0 1.3 fusion.152
  5.3 1.7 pad_maximum_fusion
  7.0 6.9 %copy.147 = f32[9,24576]{0,1:T(8,128)} copy(f32[9,24576]{1,0:T(8,128)S(1)} %pad_maximum_fusion) | data formatting | bytes 1769472 | tf_op jit(solution)/shard_map/concatenate | solution.py:80
  13.9 12.7 %gather_fusion = f32[3072,9]{1,0:T(8,128)S(1)} fusion(f32[9,24576]{0,1:T(8,128)} %copy.147, s32[3072]{0:T(1024)S(1)} %broadcast_clamp_fusion), kind=kCustom, calls=%fused_computation | custom fusion | bytes 233472 | tf_op jit(solution)/shard_map/jit(_take)/gather | solution.py:94
  28.7 29.0 %while.20 = (s32[]{:T(128)}, f32[12,4,256]{2,1,0:T(4,128)S(1)}, s32[]{:T(128)}, f32[9,12,256]{2,1,0:T(8,128)S(1)}, f32[12,256]{1,0:T(8,128)}, /*index=5*/f32[12,...) while((s32[]{:T(128)}, f32[12,4,256]{2,1,0:T(4,128)S(1)}, ...), condition=%wide.region_5.6_spmd, body=%wide.region_1.5_spmd.sunk | while | flops 53501960 | bytes 6762835 | solution.py:112
  30.4 1.0 log-plus-one_reduce_fusion.4
  32.5 3.8 %fusion.178 = f32[4,256,2,128]{1,2,3,0:T(2,128)S(1)} fusion(f32[4,2,128]{1,2,0:T(8,128)S(1)} %copy.281, f32[4,2,128]{1,2,0:T(8,128)S(1)} %copy.283, f32[4,256]{1,0:T(4,128)S(1)} %get-tuple-element.314, f32[4,2,128]{1,2,0:T(8,128)S(1)} %copy.284, f32[4,2,128]{1,2,0:T(8,128)S(1)} %copy.286, f32[4,256]{1,0:T(4,128)S(1)} %constant_dynamic-slice_fusion.20, ...), kind=kOutput, calls=%fused_computation.22.clone.1 | output fusion | flops 36700160 | bytes 1081344 | tf_op jit(solution)/shard_map/reduce-window
  36.8 1.6 fusion.179
  40.1 1.0 log-plus-one_reduce_fusion.4
  42.1 3.8 %fusion.178 = f32[4,256,2,128]{1,2,3,0:T(2,128)S(1)} fusion(f32[4,2,128]{1,2,0:T(8,128)S(1)} %copy.281, f32[4,2,128]{1,2,0:T(8,128)S(1)} %copy.283, f32[4,256]{1,0:T(4,128)S(1)} %get-tuple-element.314, f32[4,2,128]{1,2,0:T(8,128)S(1)} %copy.284, f32[4,2,128]{1,2,0:T(8,128)S(1)} %copy.286, f32[4,256]{1,0:T(4,128)S(1)} %constant_dynamic-slice_fusion.20, ...), kind=kOutput, calls=%fused_computation.22.clone.1 | output fusion | flops 36700160 | bytes 1081344 | tf_op jit(solution)/shard_map/reduce-window
  46.5 1.6 fusion.179
  49.8 1.0 log-plus-one_reduce_fusion.4
  51.8 3.8 %fusion.178 = f32[4,256,2,128]{1,2,3,0:T(2,128)S(1)} fusion(f32[4,2,128]{1,2,0:T(8,128)S(1)} %copy.281, f32[4,2,128]{1,2,0:T(8,128)S(1)} %copy.283, f32[4,256]{1,0:T(4,128)S(1)} %get-tuple-element.314, f32[4,2,128]{1,2,0:T(8,128)S(1)} %copy.284, f32[4,2,128]{1,2,0:T(8,128)S(1)} %copy.286, f32[4,256]{1,0:T(4,128)S(1)} %constant_dynamic-slice_fusion.20, ...), kind=kOutput, calls=%fused_computation.22.clone.1 | output fusion | flops 36700160 | bytes 1081344 | tf_op jit(solution)/shard_map/reduce-window
  56.1 1.6 fusion.179
  58.6 2.1 scatter_fusion
  60.7 10.5 %all-to-all-start = ((f32[64,2,4,256]{3,2,1,0:T(4,128)}), f32[64,2,4,256]{3,2,1,0:T(4,128)S(1)}, u32[]{:S(2)}, u32[]{:S(2)}) async-start(f32[64,2,4,256]{3,2,1,0:T(4,128)} %bitcast.36), calls=%async_computation | async-start | bytes 1048576 | tf_op jit(solution)/shard_map/all_to_all | solution.py:122
  71.3 14.0 %all-to-all-done = f32[64,2,4,256]{3,2,1,0:T(4,128)S(1)} async-done(((f32[64,2,4,256]{3,2,1,0:T(4,128)}), f32[64,2,4,256]{3,2,1,0:T(4,128)S(1)}, u32[]{:S(2)}, u32[]{:S(2)}) %all-to-all-start) | async-done | bytes 524320 | tf_op jit(solution)/shard_map/all_to_all | solution.py:122
  91.5 1.1 copy.153
  92.6 10.7 %all-to-all-start.1 = ((f32[64,2,4,256]{3,2,1,0:T(4,128)}), f32[64,2,4,256]{3,2,1,0:T(4,128)S(1)}, u32[]{:S(2)}, u32[]{:S(2)}) async-start(f32[64,2,4,256]{3,2,1,0:T(4,128)} %copy.153), calls=%async_computation.1 | async-start | bytes 1048576 | tf_op jit(solution)/shard_map/all_to_all | solution.py:130
  105.3 11.3 %all-to-all-done.1 = f32[64,2,4,256]{3,2,1,0:T(4,128)S(1)} async-done(((f32[64,2,4,256]{3,2,1,0:T(4,128)}), f32[64,2,4,256]{3,2,1,0:T(4,128)S(1)}, u32[]{:S(2)}, u32[]{:S(2)}) %all-to-all-start.1) | async-done | bytes 524320 | tf_op jit(solution)/shard_map/all_to_all | solution.py:130
  118.6 98.9 %while.21 = (s32[]{:T(128)}, f32[9,12,256]{2,1,0:T(8,128)}, s32[]{:T(128)}, f32[12,4,256]{2,1,0:T(4,128)}, f32[9,12,256]{2,1,0:T(8,128)S(1)}, /*index=5*/f32[12,...) while((s32[]{:T(128)}, f32[9,12,256]{2,1,0:T(8,128)}, ...), condition=%wide.region_22.23_spmd, body=%wide.region_10.22_spmd.sunk | while | flops 108661776 | bytes 25101160 | solution.py:143
  120.2 1.8 fusion.186
  122.0 1.5 log-plus-one_reduce_fusion.5
  123.7 0.9 copy.294
  124.6 0.8 copy.295
  126.3 0.9 copy.297
  127.2 0.9 copy.298
  128.1 4.9 %fusion.187 = f32[4,256,2,128]{1,2,3,0:T(2,128)S(1)} fusion(f32[4,2,128]{1,2,0:T(8,128)S(1)} %copy.293, f32[4,2,128]{1,2,0:T(8,128)} %copy.294, f32[4,256]{1,0:T(4,128)} %copy-done.2, f32[4,2,128]{1,2,0:T(8,128)} %copy.295, f32[4,2,128]{1,2,0:T(8,128)} %copy.296, f32[4,256]{1,0:T(4,128)} %copy-done, f32[4,2,128]{1,2,0:T(8,128)} %copy.297, ...), kind=kOutput, calls=%fused_computation.104.clone.1 | output fusion | flops 36700160 | bytes 1081344 | tf_op jit(solution)/shard_map/reduce-window.2
  134.0 9.2 %fusion.188 = f32[4,256,2,128]{1,2,3,0:T(2,128)S(1)} fusion(f32[4,256,2,128]{1,3,2,0:T(8,128)S(1)} %bitcast.293), kind=kOutput, calls=%fused_computation.118.clone.1 | output fusion | flops 33292288 | bytes 2097152 | tf_op jit(solution)/shard_map/reduce-window.4
  144.5 3.2 %fusion.189 = (f32[4,256]{1,0:T(4,128)S(1)}, f32[4,256]{1,0:T(4,128)S(1)}, f32[4,256]{1,0:T(4,128)S(1)}, f32[4,256]{1,0:T(4,128)S(1)}, f32[4,256]{1,0:T(4,128)S(1)}, /*index=5*/f32[4,256]{1,0:T(4,128)S(1)}) fusion(f32[4,256]{1,0:T(4,128)S(1)} %bitcast.306, f32[4,256]{1,0:T(4,128)S(1)} %copy-done.3, f32[4,256]{1,0:T(4,128)S(1)} %bitcast.309, ...), kind=kLoop, calls=%fused_computation.110.clone.1 | loop fusion | flops 11528192 | bytes 3203072 | tf_op jit(solution)/shard_map/while/body/transpose(jvp())/reduce_sum | solution.py:24
  148.5 2.4 fusion.192
  153.2 1.8 fusion.186
  154.9 1.5 log-plus-one_reduce_fusion.5
  156.7 0.9 copy.294
  159.3 0.9 copy.297
  160.2 0.9 copy.298
  161.0 4.9 %fusion.187 = f32[4,256,2,128]{1,2,3,0:T(2,128)S(1)} fusion(f32[4,2,128]{1,2,0:T(8,128)S(1)} %copy.293, f32[4,2,128]{1,2,0:T(8,128)} %copy.294, f32[4,256]{1,0:T(4,128)} %copy-done.2, f32[4,2,128]{1,2,0:T(8,128)} %copy.295, f32[4,2,128]{1,2,0:T(8,128)} %copy.296, f32[4,256]{1,0:T(4,128)} %copy-done, f32[4,2,128]{1,2,0:T(8,128)} %copy.297, ...), kind=kOutput, calls=%fused_computation.104.clone.1 | output fusion | flops 36700160 | bytes 1081344 | tf_op jit(solution)/shard_map/reduce-window.2
  166.9 9.2 %fusion.188 = f32[4,256,2,128]{1,2,3,0:T(2,128)S(1)} fusion(f32[4,256,2,128]{1,3,2,0:T(8,128)S(1)} %bitcast.293), kind=kOutput, calls=%fused_computation.118.clone.1 | output fusion | flops 33292288 | bytes 2097152 | tf_op jit(solution)/shard_map/reduce-window.4
  177.5 3.2 %fusion.189 = (f32[4,256]{1,0:T(4,128)S(1)}, f32[4,256]{1,0:T(4,128)S(1)}, f32[4,256]{1,0:T(4,128)S(1)}, f32[4,256]{1,0:T(4,128)S(1)}, f32[4,256]{1,0:T(4,128)S(1)}, /*index=5*/f32[4,256]{1,0:T(4,128)S(1)}) fusion(f32[4,256]{1,0:T(4,128)S(1)} %bitcast.306, f32[4,256]{1,0:T(4,128)S(1)} %copy-done.3, f32[4,256]{1,0:T(4,128)S(1)} %bitcast.309, ...), kind=kLoop, calls=%fused_computation.110.clone.1 | loop fusion | flops 11528192 | bytes 3203072 | tf_op jit(solution)/shard_map/while/body/transpose(jvp())/reduce_sum | solution.py:24
  181.5 2.4 fusion.192
  186.2 1.8 fusion.186
  187.9 1.5 log-plus-one_reduce_fusion.5
  189.6 0.9 copy.294
  190.5 0.8 copy.295
  192.2 0.9 copy.297
  193.2 0.9 copy.298
  194.0 4.9 %fusion.187 = f32[4,256,2,128]{1,2,3,0:T(2,128)S(1)} fusion(f32[4,2,128]{1,2,0:T(8,128)S(1)} %copy.293, f32[4,2,128]{1,2,0:T(8,128)} %copy.294, f32[4,256]{1,0:T(4,128)} %copy-done.2, f32[4,2,128]{1,2,0:T(8,128)} %copy.295, f32[4,2,128]{1,2,0:T(8,128)} %copy.296, f32[4,256]{1,0:T(4,128)} %copy-done, f32[4,2,128]{1,2,0:T(8,128)} %copy.297, ...), kind=kOutput, calls=%fused_computation.104.clone.1 | output fusion | flops 36700160 | bytes 1081344 | tf_op jit(solution)/shard_map/reduce-window.2
  199.9 9.2 %fusion.188 = f32[4,256,2,128]{1,2,3,0:T(2,128)S(1)} fusion(f32[4,256,2,128]{1,3,2,0:T(8,128)S(1)} %bitcast.293), kind=kOutput, calls=%fused_computation.118.clone.1 | output fusion | flops 33292288 | bytes 2097152 | tf_op jit(solution)/shard_map/reduce-window.4
  210.5 3.2 %fusion.189 = (f32[4,256]{1,0:T(4,128)S(1)}, f32[4,256]{1,0:T(4,128)S(1)}, f32[4,256]{1,0:T(4,128)S(1)}, f32[4,256]{1,0:T(4,128)S(1)}, f32[4,256]{1,0:T(4,128)S(1)}, /*index=5*/f32[4,256]{1,0:T(4,128)S(1)}) fusion(f32[4,256]{1,0:T(4,128)S(1)} %bitcast.306, f32[4,256]{1,0:T(4,128)S(1)} %copy-done.3, f32[4,256]{1,0:T(4,128)S(1)} %bitcast.309, ...), kind=kLoop, calls=%fused_computation.110.clone.1 | loop fusion | flops 11528192 | bytes 3203072 | tf_op jit(solution)/shard_map/while/body/transpose(jvp())/reduce_sum | solution.py:24
  214.5 2.4 fusion.192
  217.6 0.9 select_bitcast_fusion.1
  218.6 5.9 %broadcast_multiply_fusion = f32[3072,48,9]{0,2,1:T(8,128)} fusion(f32[3072,9]{0,1:T(8,128)S(1)} %bitcast.321, f32[3072,48]{0,1:T(8,128)} %fusion.119), kind=kLoop, calls=%fused_computation.211 | loop fusion | flops 1327104 | bytes 6008832 | tf_op jit(solution)/shard_map/mul | solution.py:162
  224.5 7.4 %reshape.701 = f32[3072,432,1]{0,1,2:T(8,128)} reshape(f32[3072,48,9]{0,2,1:T(8,128)} %broadcast_multiply_fusion) | data formatting | bytes 10616832 | tf_op jit(solution)/shard_map/mul | solution.py:162
  231.9 8.8 %fusion.115 = f32[8,64,432]{2,1,0:T(8,128)S(1)} fusion(f32[3072,432,1]{0,1,2:T(8,128)} %reshape.701, s32[8,64]{1,0:T(8,128)S(1)} %copy-done.24, s32[3072]{0:T(1024)S(1)} %copy-done.21), kind=kOutput, calls=%fused_computation.209 | convolution fusion | flops 8155299840 | bytes 6207488 | tf_op jit(solution)/shard_map/eh,ez->hz/dot_general | solution.py:163
  241.5 4.0 %collective-permute-start.5 = (f32[64,432]{1,0:T(8,128)S(1)}, f32[64,432]{1,0:T(8,128)S(1)}, u32[]{:S(2)}, u32[]{:S(2)}) collective-permute-start(f32[64,432]{1,0:T(8,128)S(1)} %get-tuple-element.168), channel_id=1, source_target_pairs={{0,6},{1,7},{2,0},{3,1},{4,2},{5,3},{6,4},{7,5},{8,14},{9,15},{10,... | collective-permute-start | bytes 331784 | tf_op jit(solution)/shard_map/ppermute | solution.py:170
  245.5 2.4 collective-permute-start.4
  248.0 4.7 %collective-permute-start.3 = (f32[64,432]{1,0:T(8,128)S(1)}, f32[64,432]{1,0:T(8,128)S(1)}, u32[]{:S(2)}, u32[]{:S(2)}) collective-permute-start(f32[64,432]{1,0:T(8,128)S(1)} %get-tuple-element.170), channel_id=1, source_target_pairs={{0,4},{1,5},{2,6},{3,7},{4,0},{5,1},{6,2},{7,3},{8,12},{9,13},{10,... | collective-permute-start | bytes 331784 | tf_op jit(solution)/shard_map/ppermute | solution.py:170
  252.7 1.9 collective-permute-start.2
  254.6 2.3 collective-permute-start.1
  257.0 1.1 collective-permute-start
  258.7 2.9 %collective-permute-done.2 = f32[64,432]{1,0:T(8,128)S(1)} collective-permute-done((f32[64,432]{1,0:T(8,128)S(1)}, f32[64,432]{1,0:T(8,128)S(1)}, u32[]{:S(2)}, u32[]{:S(2)}) %collective-permute-start.2) | collective-permute-done | bytes 110624 | tf_op jit(solution)/shard_map/ppermute | solution.py:170
  261.6 2.7 collective-permute-done.1
  264.3 1.3 collective-permute-done
  (421 shorter events, 47.2 us)
Async XLA Ops:
  5.3 21.9 %copy-start.18 = (pred[12,256]{1,0:T(8,128)(4,1)}, pred[12,256]{1,0:T(8,128)(4,1)S(1)}, u32[]{:S(2)}) copy-start(pred[12,256]{1,0:T(8,128)(4,1)S(1)} %get-tuple-element.139) | copy-start | bytes 9220
  7.0 20.3 %copy-start.17 = (s32[1,1,12,256]{3,1,2,0:T(1,128)S(1)}, s32[1,1,12,256]{3,1,2,0:T(1,128)}, u32[]{:S(2)}) copy-start(s32[1,1,12,256]{3,1,2,0:T(1,128)} %param.15) | copy-start | bytes 36868
  7.0 20.3 %copy-start.25 = (s32[1,1,12]{2,1,0:T(1,128)S(1)}, s32[1,1,12]{2,1,0:T(1,128)}, u32[]{:S(2)}) copy-start(s32[1,1,12]{2,1,0:T(1,128)} %param.14) | copy-start | bytes 148
  7.0 21.7 %copy-start.20 = (f32[4,256]{1,0:T(4,128)S(1)}, f32[4,256]{1,0:T(4,128)}, u32[]{:S(2)}) copy-start(f32[4,256]{1,0:T(4,128)} %constant.230.clone.1) | copy-start | bytes 12292
  28.7 42.5 %copy-start.22 = (f32[3,2,256]{2,1,0:T(2,128)S(1)}, f32[3,2,256]{2,1,0:T(2,128)}, u32[]{:S(2)}) copy-start(f32[3,2,256]{2,1,0:T(2,128)} %param.17) | copy-start | bytes 18436
  28.7 56.5 %copy-start.23 = (s32[2,64]{1,0:T(2,128)S(1)}, s32[2,64]{1,0:T(2,128)}, u32[]{:S(2)}) copy-start(s32[2,64]{1,0:T(2,128)} %param.16) | copy-start | bytes 1540
  60.7 24.6 %all-to-all-start = ((f32[64,2,4,256]{3,2,1,0:T(4,128)}), f32[64,2,4,256]{3,2,1,0:T(4,128)S(1)}, u32[]{:S(2)}, u32[]{:S(2)}) async-start(f32[64,2,4,256]{3,2,1,0:T(4,128)} %bitcast.36), calls=%async_computation | async-start | bytes 1048576 | tf_op jit(solution)/shard_map/all_to_all | solution.py:122
  92.6 24.1 %all-to-all-start.1 = ((f32[64,2,4,256]{3,2,1,0:T(4,128)}), f32[64,2,4,256]{3,2,1,0:T(4,128)S(1)}, u32[]{:S(2)}, u32[]{:S(2)}) async-start(f32[64,2,4,256]{3,2,1,0:T(4,128)} %copy.153), calls=%async_computation.1 | async-start | bytes 1048576 | tf_op jit(solution)/shard_map/all_to_all | solution.py:130
  118.7 4.8 %copy-start.8 = (f32[1,4,256]{2,1,0:T(4,128)}, f32[1,4,256]{2,1,0:T(4,128)S(1)}, u32[]{:S(2)}) copy-start(f32[1,4,256]{2,1,0:T(4,128)S(1)} %get-tuple-element.330) | copy-start | bytes 12292 | tf_op jit(solution)/shard_map/while
  118.7 8.5 %copy-start.6 = (f32[1,4,256]{2,1,0:T(4,128)}, f32[1,4,256]{2,1,0:T(4,128)S(1)}, u32[]{:S(2)}) copy-start(f32[1,4,256]{2,1,0:T(4,128)S(1)} %get-tuple-element.332) | copy-start | bytes 12292 | tf_op jit(solution)/shard_map/while
  118.7 8.5 %copy-start.10 = (f32[1,4,256]{2,1,0:T(4,128)}, f32[1,4,256]{2,1,0:T(4,128)S(1)}, u32[]{:S(2)}) copy-start(f32[1,4,256]{2,1,0:T(4,128)S(1)} %get-tuple-element.331) | copy-start | bytes 12292 | tf_op jit(solution)/shard_map/while
  118.7 8.5 %copy-start.12 = (f32[1,4,256]{2,1,0:T(4,128)}, f32[1,4,256]{2,1,0:T(4,128)S(1)}, u32[]{:S(2)}) copy-start(f32[1,4,256]{2,1,0:T(4,128)S(1)} %get-tuple-element.327) | copy-start | bytes 12292 | tf_op jit(solution)/shard_map/while
  118.7 8.5 %copy-start.14 = (f32[1,4,256]{2,1,0:T(4,128)}, f32[1,4,256]{2,1,0:T(4,128)S(1)}, u32[]{:S(2)}) copy-start(f32[1,4,256]{2,1,0:T(4,128)S(1)} %get-tuple-element.329) | copy-start | bytes 12292 | tf_op jit(solution)/shard_map/while
  119.5 4.0 %copy-start.2 = (f32[4,256]{1,0:T(4,128)}, f32[4,256]{1,0:T(4,128)S(1)}, u32[]{:S(2)}) copy-start(f32[4,256]{1,0:T(4,128)S(1)} %get-tuple-element.328) | copy-start | bytes 12292 | tf_op jit(solution)/shard_map/while
  119.5 7.7 %copy-start.4 = (f32[4,256]{1,0:T(4,128)}, f32[4,256]{1,0:T(4,128)S(1)}, u32[]{:S(2)}) copy-start(f32[4,256]{1,0:T(4,128)S(1)} %get-tuple-element.333) | copy-start | bytes 12292 | tf_op jit(solution)/shard_map/while
  133.5 10.9 %copy-start.16 = (f32[4,256]{1,0:T(4,128)S(1)}, f32[4,256]{1,0:T(4,128)}, u32[]{:S(2)}) copy-start(f32[4,256]{1,0:T(4,128)} %get-tuple-element.335) | copy-start | bytes 12292 | tf_op jit(solution)/shard_map/while
  133.5 11.0 %copy-start.1 = (f32[4,256]{1,0:T(4,128)S(1)}, f32[4,256]{1,0:T(4,128)}, u32[]{:S(2)}) copy-start(f32[4,256]{1,0:T(4,128)} %copy-done) | copy-start | bytes 12292 | tf_op jit(solution)/shard_map/while
  133.5 11.0 %copy-start.3 = (f32[4,256]{1,0:T(4,128)S(1)}, f32[4,256]{1,0:T(4,128)}, u32[]{:S(2)}) copy-start(f32[4,256]{1,0:T(4,128)} %copy-done.2) | copy-start | bytes 12292 | tf_op jit(solution)/shard_map/while
  133.5 11.0 %copy-start.5 = (f32[4,256]{1,0:T(4,128)S(1)}, f32[4,256]{1,0:T(4,128)}, u32[]{:S(2)}) copy-start(f32[4,256]{1,0:T(4,128)} %copy-done.4) | copy-start | bytes 12292 | tf_op jit(solution)/shard_map/while
  133.5 11.0 %copy-start.7 = (f32[1,4,256]{2,1,0:T(4,128)S(1)}, f32[1,4,256]{2,1,0:T(4,128)}, u32[]{:S(2)}) copy-start(f32[1,4,256]{2,1,0:T(4,128)} %copy-done.6) | copy-start | bytes 12292 | tf_op jit(solution)/shard_map/while
  133.5 11.0 %copy-start.9 = (f32[1,4,256]{2,1,0:T(4,128)S(1)}, f32[1,4,256]{2,1,0:T(4,128)}, u32[]{:S(2)}) copy-start(f32[1,4,256]{2,1,0:T(4,128)} %copy-done.8) | copy-start | bytes 12292 | tf_op jit(solution)/shard_map/while
  133.6 11.0 %copy-start.11 = (f32[1,4,256]{2,1,0:T(4,128)S(1)}, f32[1,4,256]{2,1,0:T(4,128)}, u32[]{:S(2)}) copy-start(f32[1,4,256]{2,1,0:T(4,128)} %copy-done.10) | copy-start | bytes 12292 | tf_op jit(solution)/shard_map/while
  133.6 11.0 %copy-start.13 = (f32[1,4,256]{2,1,0:T(4,128)S(1)}, f32[1,4,256]{2,1,0:T(4,128)}, u32[]{:S(2)}) copy-start(f32[1,4,256]{2,1,0:T(4,128)} %copy-done.12) | copy-start | bytes 12292 | tf_op jit(solution)/shard_map/while
  133.6 11.0 %copy-start.15 = (f32[1,4,256]{2,1,0:T(4,128)S(1)}, f32[1,4,256]{2,1,0:T(4,128)}, u32[]{:S(2)}) copy-start(f32[1,4,256]{2,1,0:T(4,128)} %copy-done.14) | copy-start | bytes 12292 | tf_op jit(solution)/shard_map/while
  151.7 4.8 %copy-start.8 = (f32[1,4,256]{2,1,0:T(4,128)}, f32[1,4,256]{2,1,0:T(4,128)S(1)}, u32[]{:S(2)}) copy-start(f32[1,4,256]{2,1,0:T(4,128)S(1)} %get-tuple-element.330) | copy-start | bytes 12292 | tf_op jit(solution)/shard_map/while
  151.7 8.5 %copy-start.6 = (f32[1,4,256]{2,1,0:T(4,128)}, f32[1,4,256]{2,1,0:T(4,128)S(1)}, u32[]{:S(2)}) copy-start(f32[1,4,256]{2,1,0:T(4,128)S(1)} %get-tuple-element.332) | copy-start | bytes 12292 | tf_op jit(solution)/shard_map/while
  151.7 8.5 %copy-start.10 = (f32[1,4,256]{2,1,0:T(4,128)}, f32[1,4,256]{2,1,0:T(4,128)S(1)}, u32[]{:S(2)}) copy-start(f32[1,4,256]{2,1,0:T(4,128)S(1)} %get-tuple-element.331) | copy-start | bytes 12292 | tf_op jit(solution)/shard_map/while
  151.7 8.5 %copy-start.12 = (f32[1,4,256]{2,1,0:T(4,128)}, f32[1,4,256]{2,1,0:T(4,128)S(1)}, u32[]{:S(2)}) copy-start(f32[1,4,256]{2,1,0:T(4,128)S(1)} %get-tuple-element.327) | copy-start | bytes 12292 | tf_op jit(solution)/shard_map/while
  151.7 8.5 %copy-start.14 = (f32[1,4,256]{2,1,0:T(4,128)}, f32[1,4,256]{2,1,0:T(4,128)S(1)}, u32[]{:S(2)}) copy-start(f32[1,4,256]{2,1,0:T(4,128)S(1)} %get-tuple-element.329) | copy-start | bytes 12292 | tf_op jit(solution)/shard_map/while
  152.4 7.7 %copy-start.4 = (f32[4,256]{1,0:T(4,128)}, f32[4,256]{1,0:T(4,128)S(1)}, u32[]{:S(2)}) copy-start(f32[4,256]{1,0:T(4,128)S(1)} %get-tuple-element.333) | copy-start | bytes 12292 | tf_op jit(solution)/shard_map/while
  166.5 10.9 %copy-start.16 = (f32[4,256]{1,0:T(4,128)S(1)}, f32[4,256]{1,0:T(4,128)}, u32[]{:S(2)}) copy-start(f32[4,256]{1,0:T(4,128)} %get-tuple-element.335) | copy-start | bytes 12292 | tf_op jit(solution)/shard_map/while
  166.5 11.0 %copy-start.1 = (f32[4,256]{1,0:T(4,128)S(1)}, f32[4,256]{1,0:T(4,128)}, u32[]{:S(2)}) copy-start(f32[4,256]{1,0:T(4,128)} %copy-done) | copy-start | bytes 12292 | tf_op jit(solution)/shard_map/while
  166.5 11.0 %copy-start.3 = (f32[4,256]{1,0:T(4,128)S(1)}, f32[4,256]{1,0:T(4,128)}, u32[]{:S(2)}) copy-start(f32[4,256]{1,0:T(4,128)} %copy-done.2) | copy-start | bytes 12292 | tf_op jit(solution)/shard_map/while
  166.5 11.0 %copy-start.5 = (f32[4,256]{1,0:T(4,128)S(1)}, f32[4,256]{1,0:T(4,128)}, u32[]{:S(2)}) copy-start(f32[4,256]{1,0:T(4,128)} %copy-done.4) | copy-start | bytes 12292 | tf_op jit(solution)/shard_map/while
  166.5 11.0 %copy-start.7 = (f32[1,4,256]{2,1,0:T(4,128)S(1)}, f32[1,4,256]{2,1,0:T(4,128)}, u32[]{:S(2)}) copy-start(f32[1,4,256]{2,1,0:T(4,128)} %copy-done.6) | copy-start | bytes 12292 | tf_op jit(solution)/shard_map/while
  166.5 11.0 %copy-start.9 = (f32[1,4,256]{2,1,0:T(4,128)S(1)}, f32[1,4,256]{2,1,0:T(4,128)}, u32[]{:S(2)}) copy-start(f32[1,4,256]{2,1,0:T(4,128)} %copy-done.8) | copy-start | bytes 12292 | tf_op jit(solution)/shard_map/while
  166.5 11.0 %copy-start.11 = (f32[1,4,256]{2,1,0:T(4,128)S(1)}, f32[1,4,256]{2,1,0:T(4,128)}, u32[]{:S(2)}) copy-start(f32[1,4,256]{2,1,0:T(4,128)} %copy-done.10) | copy-start | bytes 12292 | tf_op jit(solution)/shard_map/while
  166.5 11.0 %copy-start.13 = (f32[1,4,256]{2,1,0:T(4,128)S(1)}, f32[1,4,256]{2,1,0:T(4,128)}, u32[]{:S(2)}) copy-start(f32[1,4,256]{2,1,0:T(4,128)} %copy-done.12) | copy-start | bytes 12292 | tf_op jit(solution)/shard_map/while
  166.5 11.0 %copy-start.15 = (f32[1,4,256]{2,1,0:T(4,128)S(1)}, f32[1,4,256]{2,1,0:T(4,128)}, u32[]{:S(2)}) copy-start(f32[1,4,256]{2,1,0:T(4,128)} %copy-done.14) | copy-start | bytes 12292 | tf_op jit(solution)/shard_map/while
  184.6 4.8 %copy-start.8 = (f32[1,4,256]{2,1,0:T(4,128)}, f32[1,4,256]{2,1,0:T(4,128)S(1)}, u32[]{:S(2)}) copy-start(f32[1,4,256]{2,1,0:T(4,128)S(1)} %get-tuple-element.330) | copy-start | bytes 12292 | tf_op jit(solution)/shard_map/while
  184.6 8.5 %copy-start.6 = (f32[1,4,256]{2,1,0:T(4,128)}, f32[1,4,256]{2,1,0:T(4,128)S(1)}, u32[]{:S(2)}) copy-start(f32[1,4,256]{2,1,0:T(4,128)S(1)} %get-tuple-element.332) | copy-start | bytes 12292 | tf_op jit(solution)/shard_map/while
  184.6 8.5 %copy-start.10 = (f32[1,4,256]{2,1,0:T(4,128)}, f32[1,4,256]{2,1,0:T(4,128)S(1)}, u32[]{:S(2)}) copy-start(f32[1,4,256]{2,1,0:T(4,128)S(1)} %get-tuple-element.331) | copy-start | bytes 12292 | tf_op jit(solution)/shard_map/while
  184.7 8.5 %copy-start.12 = (f32[1,4,256]{2,1,0:T(4,128)}, f32[1,4,256]{2,1,0:T(4,128)S(1)}, u32[]{:S(2)}) copy-start(f32[1,4,256]{2,1,0:T(4,128)S(1)} %get-tuple-element.327) | copy-start | bytes 12292 | tf_op jit(solution)/shard_map/while
  184.7 8.5 %copy-start.14 = (f32[1,4,256]{2,1,0:T(4,128)}, f32[1,4,256]{2,1,0:T(4,128)S(1)}, u32[]{:S(2)}) copy-start(f32[1,4,256]{2,1,0:T(4,128)S(1)} %get-tuple-element.329) | copy-start | bytes 12292 | tf_op jit(solution)/shard_map/while
  185.4 7.7 %copy-start.4 = (f32[4,256]{1,0:T(4,128)}, f32[4,256]{1,0:T(4,128)S(1)}, u32[]{:S(2)}) copy-start(f32[4,256]{1,0:T(4,128)S(1)} %get-tuple-element.333) | copy-start | bytes 12292 | tf_op jit(solution)/shard_map/while
  199.4 10.9 %copy-start.16 = (f32[4,256]{1,0:T(4,128)S(1)}, f32[4,256]{1,0:T(4,128)}, u32[]{:S(2)}) copy-start(f32[4,256]{1,0:T(4,128)} %get-tuple-element.335) | copy-start | bytes 12292 | tf_op jit(solution)/shard_map/while
  199.5 11.0 %copy-start.1 = (f32[4,256]{1,0:T(4,128)S(1)}, f32[4,256]{1,0:T(4,128)}, u32[]{:S(2)}) copy-start(f32[4,256]{1,0:T(4,128)} %copy-done) | copy-start | bytes 12292 | tf_op jit(solution)/shard_map/while
  199.5 11.0 %copy-start.3 = (f32[4,256]{1,0:T(4,128)S(1)}, f32[4,256]{1,0:T(4,128)}, u32[]{:S(2)}) copy-start(f32[4,256]{1,0:T(4,128)} %copy-done.2) | copy-start | bytes 12292 | tf_op jit(solution)/shard_map/while
  199.5 11.0 %copy-start.5 = (f32[4,256]{1,0:T(4,128)S(1)}, f32[4,256]{1,0:T(4,128)}, u32[]{:S(2)}) copy-start(f32[4,256]{1,0:T(4,128)} %copy-done.4) | copy-start | bytes 12292 | tf_op jit(solution)/shard_map/while
  199.5 11.0 %copy-start.7 = (f32[1,4,256]{2,1,0:T(4,128)S(1)}, f32[1,4,256]{2,1,0:T(4,128)}, u32[]{:S(2)}) copy-start(f32[1,4,256]{2,1,0:T(4,128)} %copy-done.6) | copy-start | bytes 12292 | tf_op jit(solution)/shard_map/while
  199.5 11.0 %copy-start.9 = (f32[1,4,256]{2,1,0:T(4,128)S(1)}, f32[1,4,256]{2,1,0:T(4,128)}, u32[]{:S(2)}) copy-start(f32[1,4,256]{2,1,0:T(4,128)} %copy-done.8) | copy-start | bytes 12292 | tf_op jit(solution)/shard_map/while
  199.5 11.0 %copy-start.11 = (f32[1,4,256]{2,1,0:T(4,128)S(1)}, f32[1,4,256]{2,1,0:T(4,128)}, u32[]{:S(2)}) copy-start(f32[1,4,256]{2,1,0:T(4,128)} %copy-done.10) | copy-start | bytes 12292 | tf_op jit(solution)/shard_map/while
  199.5 11.0 %copy-start.13 = (f32[1,4,256]{2,1,0:T(4,128)S(1)}, f32[1,4,256]{2,1,0:T(4,128)}, u32[]{:S(2)}) copy-start(f32[1,4,256]{2,1,0:T(4,128)} %copy-done.12) | copy-start | bytes 12292 | tf_op jit(solution)/shard_map/while
  199.5 11.0 %copy-start.15 = (f32[1,4,256]{2,1,0:T(4,128)S(1)}, f32[1,4,256]{2,1,0:T(4,128)}, u32[]{:S(2)}) copy-start(f32[1,4,256]{2,1,0:T(4,128)} %copy-done.14) | copy-start | bytes 12292 | tf_op jit(solution)/shard_map/while
  224.5 7.4 %copy-start.21 = (s32[3072]{0:T(1024)S(1)}, s32[3072]{0:T(1024)}, u32[]{:S(2)}) copy-start(s32[3072]{0:T(1024)} %get-tuple-element.178) | copy-start | bytes 36868
  224.5 7.4 %copy-start.24 = (s32[8,64]{1,0:T(8,128)S(1)}, s32[8,64]{1,0:T(8,128)}, u32[]{:S(2)}) copy-start(s32[8,64]{1,0:T(8,128)} %multiply_add_fusion.9) | copy-start | bytes 6148
  231.9 26.2 %copy-start.19 = (f32[2,3,256]{2,1,0:T(4,128)S(1)}, f32[2,3,256]{2,1,0:T(4,128)}, u32[]{:S(2)}) copy-start(f32[2,3,256]{2,1,0:T(4,128)} %get-tuple-element.174) | copy-start | bytes 18436
  240.8 13.8 %collective-permute-start.6 = (f32[64,432]{1,0:T(8,128)S(1)}, f32[64,432]{1,0:T(8,128)S(1)}, u32[]{:S(2)}, u32[]{:S(2)}) collective-permute-start(f32[64,432]{1,0:T(8,128)S(1)} %get-tuple-element.167), channel_id=1, source_target_pairs={{0,7},{1,0},{2,1},{3,2},{4,3},{5,4},{6,5},{7,6},{8,15},{9,8},{10,9... | collective-permute-start | bytes 331784 | tf_op jit(solution)/shard_map/ppermute | solution.py:170
  241.5 15.5 %collective-permute-start.5 = (f32[64,432]{1,0:T(8,128)S(1)}, f32[64,432]{1,0:T(8,128)S(1)}, u32[]{:S(2)}, u32[]{:S(2)}) collective-permute-start(f32[64,432]{1,0:T(8,128)S(1)} %get-tuple-element.168), channel_id=1, source_target_pairs={{0,6},{1,7},{2,0},{3,1},{4,2},{5,3},{6,4},{7,5},{8,14},{9,15},{10,... | collective-permute-start | bytes 331784 | tf_op jit(solution)/shard_map/ppermute | solution.py:170
  245.5 13.2 %collective-permute-start.4 = (f32[64,432]{1,0:T(8,128)S(1)}, f32[64,432]{1,0:T(8,128)S(1)}, u32[]{:S(2)}, u32[]{:S(2)}) collective-permute-start(f32[64,432]{1,0:T(8,128)S(1)} %get-tuple-element.169), channel_id=1, source_target_pairs={{0,5},{1,6},{2,7},{3,0},{4,1},{5,2},{6,3},{7,4},{8,13},{9,14},{10,... | collective-permute-start | bytes 331784 | tf_op jit(solution)/shard_map/ppermute | solution.py:170
  248.0 10.7 %collective-permute-start.3 = (f32[64,432]{1,0:T(8,128)S(1)}, f32[64,432]{1,0:T(8,128)S(1)}, u32[]{:S(2)}, u32[]{:S(2)}) collective-permute-start(f32[64,432]{1,0:T(8,128)S(1)} %get-tuple-element.170), channel_id=1, source_target_pairs={{0,4},{1,5},{2,6},{3,7},{4,0},{5,1},{6,2},{7,3},{8,12},{9,13},{10,... | collective-permute-start | bytes 331784 | tf_op jit(solution)/shard_map/ppermute | solution.py:170
  252.7 8.9 %collective-permute-start.2 = (f32[64,432]{1,0:T(8,128)S(1)}, f32[64,432]{1,0:T(8,128)S(1)}, u32[]{:S(2)}, u32[]{:S(2)}) collective-permute-start(f32[64,432]{1,0:T(8,128)S(1)} %get-tuple-element.171), channel_id=1, source_target_pairs={{0,3},{1,4},{2,5},{3,6},{4,7},{5,0},{6,1},{7,2},{8,11},{9,12},{10,... | collective-permute-start | bytes 331784 | tf_op jit(solution)/shard_map/ppermute | solution.py:170
  254.6 9.6 %collective-permute-start.1 = (f32[64,432]{1,0:T(8,128)S(1)}, f32[64,432]{1,0:T(8,128)S(1)}, u32[]{:S(2)}, u32[]{:S(2)}) collective-permute-start(f32[64,432]{1,0:T(8,128)S(1)} %get-tuple-element.172), channel_id=1, source_target_pairs={{0,2},{1,3},{2,4},{3,5},{4,6},{5,7},{6,0},{7,1},{8,10},{9,11},{10,... | collective-permute-start | bytes 331784 | tf_op jit(solution)/shard_map/ppermute | solution.py:170
  257.0 8.6 %collective-permute-start = (f32[64,432]{1,0:T(8,128)S(1)}, f32[64,432]{1,0:T(8,128)S(1)}, u32[]{:S(2)}, u32[]{:S(2)}) collective-permute-start(f32[64,432]{1,0:T(8,128)S(1)} %get-tuple-element.166), channel_id=1, source_target_pairs={{0,1},{1,2},{2,3},{3,4},{4,5},{5,6},{6,7},{7,0},{8,9},{9,10},{10,1... | collective-permute-start | bytes 331784 | tf_op jit(solution)/shard_map/ppermute | solution.py:170
  (5 other events, 18.0 us)

commit v2 on v1

--- a/solution.py
+++ b/solution.py
@@ -26,8 +26,12 @@
     strength = jax.nn.sigmoid(params[5]) * live_mask
     opaque_part = strength[:, None, :] * jnp.exp(-0.5 * quadratic)
     log_keep = jnp.log1p(-opaque_part)
-    running = jnp.cumsum(log_keep, axis=2)
-    before = jnp.concatenate([jnp.zeros_like(running[:, :, :1]), running[:, :, :-1]], axis=2)
+    entries_count = log_keep.shape[2]
+    ahead = (
+        jnp.arange(entries_count, dtype=jnp.int32)[:, None]
+        < jnp.arange(entries_count, dtype=jnp.int32)[None, :]
+    ).astype(jnp.float32)
+    before = jnp.einsum("kpg,gh->kph", log_keep, ahead, precision=lax.Precision.HIGHEST)
     weight = opaque_part * jnp.exp(before)
     colour = jnp.einsum("kpg,ckg->kcp", weight, params[6:9], precision=lax.Precision.HIGHEST)
     transmit = jnp.exp(jnp.sum(log_keep, axis=2))

time: 271 us -> 173 us (0.64)
  the two profiles are of different devices: /device:TPU:224 before, /device:TPU:264 now
where the time goes in v2:
time: 173 us; the launch traced here: 172 us
  local copies, waits for them, and re-layouts  39.4 us (23%)
  matrix products  38.1 us (22%)
  waiting for transfers between devices  38 us (22%)
  starting transfers between devices  35.2 us (20%)
  other arithmetic  18.2 us (11%)
  between operations  2.3 us (1%)
    dot_general x9, matrix products, render(): jnp.einsum('kpg,gh->kph', log_keep, ahead, precision=lax.Precision.HIGHEST)  18.7 us
    ppermute x7, starting transfers between devices, local(): lax.ppermute(outgoing, 'tile', perm=[(i, (i + step) % groups_count) for i...  17.2 us
    all_to_all x1, waiting for transfers between devices, local(): lax.all_to_all(dense.reshape(parts_count, tiles_per, 4, pixels), 'dom', s...  15.8 us
    all_to_all x1, waiting for transfers between devices, local(): lax.all_to_all(upstream, 'dom', split_axis=0, concat_axis=0, tiled=True)  15.1 us
    gather x2, local copies, waits for them, and re-layouts, local(): chosen_all = jnp.take(params, jnp.where(live_all, entries, 0), axis=1)  13.3 us
    dot_general x9, matrix products, render(): jnp.einsum('kpg,ckg->kcp', weight, params[6:9], precision=lax.Precision.H...  9.61 us
    all_to_all x1, starting transfers between devices, local(): lax.all_to_all(dense.reshape(parts_count, tiles_per, 4, pixels), 'dom', s...  9.17 us
    all_to_all x1, starting transfers between devices, local(): lax.all_to_all(upstream, 'dom', split_axis=0, concat_axis=0, tiled=True)  8.85 us
  transfers between devices with their start and end apart: 9, of which 5 were waited for; matrix products, arithmetic and copies ran while one was open for 0% of the time, Pallas kernels for 0%

profile of v2, /device:TPU:264, one launch (start us, length us, event | category | flops | bytes accessed | tf_op | source)
XLA Modules:
  0.0 171.9 jit_solution(5535156035563428697)
XLA Ops:
  0.6 0.7 fusion.126
  1.3 1.3 fusion.122
  3.2 0.7 compare_select_fusion
  4.0 0.7 fusion.129
  4.7 1.7 pad_maximum_fusion
  6.4 6.9 %copy.60 = f32[9,24576]{0,1:T(8,128)} copy(f32[9,24576]{1,0:T(8,128)S(1)} %pad_maximum_fusion) | data formatting | bytes 1769472 | tf_op jit(solution)/shard_map/concatenate | solution.py:84
  13.3 12.7 %gather_fusion = f32[3072,9]{1,0:T(8,128)S(1)} fusion(f32[9,24576]{0,1:T(8,128)} %copy.60, s32[3072]{0:T(1024)S(1)} %broadcast_clamp_fusion), kind=kCustom, calls=%fused_computation | custom fusion | bytes 233472 | tf_op jit(solution)/shard_map/jit(_take)/gather | solution.py:98
  26.0 0.6 copy.61
  26.9 12.2 %while.20 = (s32[]{:T(128)}, f32[12,4,256]{2,1,0:T(4,128)S(1)}, s32[]{:T(128)}, f32[9,12,256]{2,1,0:T(8,128)S(1)}, f32[12,256]{1,0:T(8,128)S(1)}, /*index=5*/f32...) while((s32[]{:T(128)}, f32[12,4,256]{2,1,0:T(4,128)S(1)}, ...), condition=%wide.region_3.4_spmd, body=%wide.region_1.3_spmd.sunk | while | flops 825316352 | bytes 2339143 | solution.py:116
  27.0 1.0 fusion.155
  28.1 1.8 %fusion.156 = f32[4,256,256]{2,1,0:T(8,128)S(1)} fusion(f32[4,256]{1,0:T(4,128)S(1)} %get-tuple-element.283, f32[4,256]{1,0:T(4,128)S(1)} %get-tuple-element.284, f32[4,256]{1,0:T(4,128)S(1)} %get-tuple-element.285, f32[4,256]{1,0:T(4,128)S(1)} %get-tuple-element.286, f32[4,256]{1,0:T(4,128)S(1)} %get-tuple-element.287, ...), kind=kOutput, calls=%fused_computation.10.clone.1 | convolution fusion | flops 812187648 | bytes 1081344 | tf_op jit(solution)/shard_map/while/body/kpg,gh->kph/dot_general | solution.py:34
  30.0 1.0 fusion.157
  31.1 1.0 fusion.155
  32.1 1.8 %fusion.156 = f32[4,256,256]{2,1,0:T(8,128)S(1)} fusion(f32[4,256]{1,0:T(4,128)S(1)} %get-tuple-element.283, f32[4,256]{1,0:T(4,128)S(1)} %get-tuple-element.284, f32[4,256]{1,0:T(4,128)S(1)} %get-tuple-element.285, f32[4,256]{1,0:T(4,128)S(1)} %get-tuple-element.286, f32[4,256]{1,0:T(4,128)S(1)} %get-tuple-element.287, ...), kind=kOutput, calls=%fused_computation.10.clone.1 | convolution fusion | flops 812187648 | bytes 1081344 | tf_op jit(solution)/shard_map/while/body/kpg,gh->kph/dot_general | solution.py:34
  34.0 1.0 fusion.157
  35.1 1.0 fusion.155
  36.2 1.8 %fusion.156 = f32[4,256,256]{2,1,0:T(8,128)S(1)} fusion(f32[4,256]{1,0:T(4,128)S(1)} %get-tuple-element.283, f32[4,256]{1,0:T(4,128)S(1)} %get-tuple-element.284, f32[4,256]{1,0:T(4,128)S(1)} %get-tuple-element.285, f32[4,256]{1,0:T(4,128)S(1)} %get-tuple-element.286, f32[4,256]{1,0:T(4,128)S(1)} %get-tuple-element.287, ...), kind=kOutput, calls=%fused_computation.10.clone.1 | convolution fusion | flops 812187648 | bytes 1081344 | tf_op jit(solution)/shard_map/while/body/kpg,gh->kph/dot_general | solution.py:34
  38.1 1.0 fusion.157
  39.1 0.9 broadcast_in_dim.56
  39.9 2.1 %scatter_fusion = f32[128,4,256]{2,1,0:T(4,128)} fusion(f32[128,4,256]{2,1,0:T(4,128)} %broadcast_in_dim.56, s32[12]{0:T(128)S(1)} %get-tuple-element.168, f32[12,4,256]{2,1,0:T(4,128)S(1)} %get-tuple-element.85), kind=kCustom, calls=%fused_computation.2 | custom fusion | bytes 147504 | tf_op jit(solution)/shard_map/scatter | solution.py:124
  42.0 9.2 %all-to-all-start = ((f32[64,2,4,256]{3,2,1,0:T(4,128)}), f32[64,2,4,256]{3,2,1,0:T(4,128)S(1)}, u32[]{:S(2)}, u32[]{:S(2)}) async-start(f32[64,2,4,256]{3,2,1,0:T(4,128)} %bitcast.32), calls=%async_computation | async-start | bytes 1048576 | tf_op jit(solution)/shard_map/all_to_all | solution.py:126
  51.2 15.8 %all-to-all-done = f32[64,2,4,256]{3,2,1,0:T(4,128)S(1)} async-done(((f32[64,2,4,256]{3,2,1,0:T(4,128)}), f32[64,2,4,256]{3,2,1,0:T(4,128)S(1)}, u32[]{:S(2)}, u32[]{:S(2)}) %all-to-all-start) | async-done | bytes 524320 | tf_op jit(solution)/shard_map/all_to_all | solution.py:126
  67.0 0.6 fusion.100
  67.7 0.1 reduce_window.9
  67.9 0.1 slice.240
  70.3 0.1 slice.241
  71.9 0.2 slice.289
  72.2 0.4 convolution_bitcast_fusion
  72.6 1.1 copy.65
  73.8 8.9 %all-to-all-start.1 = ((f32[64,2,4,256]{3,2,1,0:T(4,128)}), f32[64,2,4,256]{3,2,1,0:T(4,128)S(1)}, u32[]{:S(2)}, u32[]{:S(2)}) async-start(f32[64,2,4,256]{3,2,1,0:T(4,128)} %copy.65), calls=%async_computation.1 | async-start | bytes 1048576 | tf_op jit(solution)/shard_map/all_to_all | solution.py:134
  82.8 15.1 %all-to-all-done.1 = f32[64,2,4,256]{3,2,1,0:T(4,128)S(1)} async-done(((f32[64,2,4,256]{3,2,1,0:T(4,128)}), f32[64,2,4,256]{3,2,1,0:T(4,128)S(1)}, u32[]{:S(2)}, u32[]{:S(2)}) %all-to-all-start.1) | async-done | bytes 524320 | tf_op jit(solution)/shard_map/all_to_all | solution.py:134
  97.9 0.6 gather_fusion.1
  98.6 24.3 %while.21 = (s32[]{:T(128)}, f32[9,12,256]{2,1,0:T(8,128)S(1)}, s32[]{:T(128)}, f32[12,4,256]{2,1,0:T(4,128)S(1)}, f32[9,12,256]{2,1,0:T(8,128)S(1)}, /*index=5*...) while((s32[]{:T(128)}, f32[9,12,256]{2,1,0:T(8,128)S(1)}, ...), condition=%wide.region_16.17_spmd, body=%wide.region_8.16_spmd.sunk | while | flops 1655438336 | bytes 5755255 | solution.py:147
  98.9 1.5 convolution_exponential_fusion.3
  100.4 1.1 fusion.164
  101.5 1.0 log-plus-one_reduce_fusion.2
  102.5 2.9 %fusion.165 = (f32[4,256]{1,0:T(4,128)S(1)}, f32[4,256]{1,0:T(4,128)S(1)}, f32[4,256]{1,0:T(4,128)S(1)}, f32[4,256]{1,0:T(4,128)S(1)}, f32[4,256]{1,0:T(4,128)S(1)}, /*index=5*/f32[4,256]{1,0:T(4,128)S(1)}) fusion(f32[4,256]{1,0:T(4,128)S(1)} %get-tuple-element.298, f32[4,256]{1,0:T(4,128)S(1)} %get-tuple-element.299, ...), kind=kOutput, calls=%fused_computation.73.clone.1 | convolution fusion | flops 820570112 | bytes 2158592 | tf_op jit(solution)/shard_map/while/body/transpose(jvp(kpg,gh->kph))/dot_general | solution.py:34
  105.6 1.2 fusion.168
  106.9 1.5 convolution_exponential_fusion.3
  108.4 1.1 fusion.164
  109.5 1.0 log-plus-one_reduce_fusion.2
  110.5 2.9 %fusion.165 = (f32[4,256]{1,0:T(4,128)S(1)}, f32[4,256]{1,0:T(4,128)S(1)}, f32[4,256]{1,0:T(4,128)S(1)}, f32[4,256]{1,0:T(4,128)S(1)}, f32[4,256]{1,0:T(4,128)S(1)}, /*index=5*/f32[4,256]{1,0:T(4,128)S(1)}) fusion(f32[4,256]{1,0:T(4,128)S(1)} %get-tuple-element.298, f32[4,256]{1,0:T(4,128)S(1)} %get-tuple-element.299, ...), kind=kOutput, calls=%fused_computation.73.clone.1 | convolution fusion | flops 820570112 | bytes 2158592 | tf_op jit(solution)/shard_map/while/body/transpose(jvp(kpg,gh->kph))/dot_general | solution.py:34
  113.6 1.2 fusion.168
  115.0 1.5 convolution_exponential_fusion.3
  116.5 1.1 fusion.164
  117.5 1.0 log-plus-one_reduce_fusion.2
  118.6 2.9 %fusion.165 = (f32[4,256]{1,0:T(4,128)S(1)}, f32[4,256]{1,0:T(4,128)S(1)}, f32[4,256]{1,0:T(4,128)S(1)}, f32[4,256]{1,0:T(4,128)S(1)}, f32[4,256]{1,0:T(4,128)S(1)}, /*index=5*/f32[4,256]{1,0:T(4,128)S(1)}) fusion(f32[4,256]{1,0:T(4,128)S(1)} %get-tuple-element.298, f32[4,256]{1,0:T(4,128)S(1)} %get-tuple-element.299, ...), kind=kOutput, calls=%fused_computation.73.clone.1 | convolution fusion | flops 820570112 | bytes 2158592 | tf_op jit(solution)/shard_map/while/body/transpose(jvp(kpg,gh->kph))/dot_general | solution.py:34
  121.6 1.2 fusion.168
  123.0 4.8 %broadcast_multiply_fusion = f32[3072,48,9]{0,2,1:T(8,128)} fusion(f32[3072,9]{0,1:T(8,128)S(1)} %bitcast.258, f32[3072,48]{0,1:T(8,128)S(1)} %fusion.96), kind=kLoop, calls=%fused_computation.163 | loop fusion | flops 1327104 | bytes 6008832 | tf_op jit(solution)/shard_map/mul | solution.py:166
  127.8 7.4 %reshape.569 = f32[3072,432,1]{0,1,2:T(8,128)} reshape(f32[3072,48,9]{0,2,1:T(8,128)} %broadcast_multiply_fusion) | data formatting | bytes 10616832 | tf_op jit(solution)/shard_map/mul | solution.py:166
  135.2 8.7 %fusion.92 = f32[8,64,432]{2,1,0:T(8,128)S(1)} fusion(f32[3072,432,1]{0,1,2:T(8,128)} %reshape.569, s32[8,64]{1,0:T(8,128)S(1)} %multiply_add_fusion.5, s32[3072]{0:T(1024)S(1)} %get-tuple-element.163), kind=kOutput, calls=%fused_computation.161 | convolution fusion | flops 8155299840 | bytes 6207488 | tf_op jit(solution)/shard_map/eh,ez->hz/dot_general | solution.py:167
  144.1 4.6 %collective-permute-start.5 = (f32[64,432]{1,0:T(8,128)S(1)}, f32[64,432]{1,0:T(8,128)S(1)}, u32[]{:S(2)}, u32[]{:S(2)}) collective-permute-start(f32[64,432]{1,0:T(8,128)S(1)} %get-tuple-element.153), channel_id=1, source_target_pairs={{0,6},{1,7},{2,0},{3,1},{4,2},{5,3},{6,4},{7,5},{8,14},{9,15},{10,... | collective-permute-start | bytes 331784 | tf_op jit(solution)/shard_map/ppermute | solution.py:174
  148.7 2.6 %collective-permute-start.4 = (f32[64,432]{1,0:T(8,128)S(1)}, f32[64,432]{1,0:T(8,128)S(1)}, u32[]{:S(2)}, u32[]{:S(2)}) collective-permute-start(f32[64,432]{1,0:T(8,128)S(1)} %get-tuple-element.154), channel_id=1, source_target_pairs={{0,5},{1,6},{2,7},{3,0},{4,1},{5,2},{6,3},{7,4},{8,13},{9,14},{10,... | collective-permute-start | bytes 331784 | tf_op jit(solution)/shard_map/ppermute | solution.py:174
  151.3 4.6 %collective-permute-start.3 = (f32[64,432]{1,0:T(8,128)S(1)}, f32[64,432]{1,0:T(8,128)S(1)}, u32[]{:S(2)}, u32[]{:S(2)}) collective-permute-start(f32[64,432]{1,0:T(8,128)S(1)} %get-tuple-element.155), channel_id=1, source_target_pairs={{0,4},{1,5},{2,6},{3,7},{4,0},{5,1},{6,2},{7,3},{8,12},{9,13},{10,... | collective-permute-start | bytes 331784 | tf_op jit(solution)/shard_map/ppermute | solution.py:174
  155.9 1.9 %collective-permute-start.2 = (f32[64,432]{1,0:T(8,128)S(1)}, f32[64,432]{1,0:T(8,128)S(1)}, u32[]{:S(2)}, u32[]{:S(2)}) collective-permute-start(f32[64,432]{1,0:T(8,128)S(1)} %get-tuple-element.156), channel_id=1, source_target_pairs={{0,3},{1,4},{2,5},{3,6},{4,7},{5,0},{6,1},{7,2},{8,11},{9,12},{10,... | collective-permute-start | bytes 331784 | tf_op jit(solution)/shard_map/ppermute | solution.py:174
  157.8 2.4 %collective-permute-start.1 = (f32[64,432]{1,0:T(8,128)S(1)}, f32[64,432]{1,0:T(8,128)S(1)}, u32[]{:S(2)}, u32[]{:S(2)}) collective-permute-start(f32[64,432]{1,0:T(8,128)S(1)} %get-tuple-element.157), channel_id=1, source_target_pairs={{0,2},{1,3},{2,4},{3,5},{4,6},{5,7},{6,0},{7,1},{8,10},{9,11},{10,... | collective-permute-start | bytes 331784 | tf_op jit(solution)/shard_map/ppermute | solution.py:174
  160.2 1.1 collective-permute-start
  161.3 0.6 copy.70
  161.9 3.2 %collective-permute-done.2 = f32[64,432]{1,0:T(8,128)S(1)} collective-permute-done((f32[64,432]{1,0:T(8,128)S(1)}, f32[64,432]{1,0:T(8,128)S(1)}, u32[]{:S(2)}, u32[]{:S(2)}) %collective-permute-start.2) | collective-permute-done | bytes 110624 | tf_op jit(solution)/shard_map/ppermute | solution.py:174
  165.1 2.5 %collective-permute-done.1 = f32[64,432]{1,0:T(8,128)S(1)} collective-permute-done((f32[64,432]{1,0:T(8,128)S(1)}, f32[64,432]{1,0:T(8,128)S(1)}, u32[]{:S(2)}, u32[]{:S(2)}) %collective-permute-start.1) | collective-permute-done | bytes 110624 | tf_op jit(solution)/shard_map/ppermute | solution.py:174
  167.6 1.4 collective-permute-done
  169.5 0.8 slice.291
  170.3 0.7 squeeze.71
  171.1 0.7 slice.294
  (182 shorter events, 6.0 us)
Async XLA Ops:
  6.4 20.2 %copy-start = (s32[1,1,12,256]{3,1,2,0:T(1,128)S(1)}, s32[1,1,12,256]{3,1,2,0:T(1,128)}, u32[]{:S(2)}) copy-start(s32[1,1,12,256]{3,1,2,0:T(1,128)} %param.15) | copy-start | bytes 36868
  6.4 20.3 %copy-start.4 = (s32[1,1,12]{2,1,0:T(1,128)S(1)}, s32[1,1,12]{2,1,0:T(1,128)}, u32[]{:S(2)}) copy-start(s32[1,1,12]{2,1,0:T(1,128)} %param.14) | copy-start | bytes 148
  6.4 20.5 %copy-start.1 = (f32[4,256]{1,0:T(4,128)S(1)}, f32[4,256]{1,0:T(4,128)}, u32[]{:S(2)}) copy-start(f32[4,256]{1,0:T(4,128)} %constant.220.clone.1) | copy-start | bytes 12292
  26.9 24.3 %copy-start.2 = (f32[3,2,256]{2,1,0:T(2,128)S(1)}, f32[3,2,256]{2,1,0:T(2,128)}, u32[]{:S(2)}) copy-start(f32[3,2,256]{2,1,0:T(2,128)} %param.17) | copy-start | bytes 18436
  26.9 40.1 %copy-start.3 = (s32[2,64]{1,0:T(2,128)S(1)}, s32[2,64]{1,0:T(2,128)}, u32[]{:S(2)}) copy-start(s32[2,64]{1,0:T(2,128)} %param.16) | copy-start | bytes 1540
  42.0 25.0 %all-to-all-start = ((f32[64,2,4,256]{3,2,1,0:T(4,128)}), f32[64,2,4,256]{3,2,1,0:T(4,128)S(1)}, u32[]{:S(2)}, u32[]{:S(2)}) async-start(f32[64,2,4,256]{3,2,1,0:T(4,128)} %bitcast.32), calls=%async_computation | async-start | bytes 1048576 | tf_op jit(solution)/shard_map/all_to_all | solution.py:126
  73.8 24.1 %all-to-all-start.1 = ((f32[64,2,4,256]{3,2,1,0:T(4,128)}), f32[64,2,4,256]{3,2,1,0:T(4,128)S(1)}, u32[]{:S(2)}, u32[]{:S(2)}) async-start(f32[64,2,4,256]{3,2,1,0:T(4,128)} %copy.65), calls=%async_computation.1 | async-start | bytes 1048576 | tf_op jit(solution)/shard_map/all_to_all | solution.py:134
  144.1 13.7 %collective-permute-start.6 = (f32[64,432]{1,0:T(8,128)S(1)}, f32[64,432]{1,0:T(8,128)S(1)}, u32[]{:S(2)}, u32[]{:S(2)}) collective-permute-start(f32[64,432]{1,0:T(8,128)S(1)} %get-tuple-element.152), channel_id=1, source_target_pairs={{0,7},{1,0},{2,1},{3,2},{4,3},{5,4},{6,5},{7,6},{8,15},{9,8},{10,9... | collective-permute-start | bytes 331784 | tf_op jit(solution)/shard_map/ppermute | solution.py:174
  144.1 16.1 %collective-permute-start.5 = (f32[64,432]{1,0:T(8,128)S(1)}, f32[64,432]{1,0:T(8,128)S(1)}, u32[]{:S(2)}, u32[]{:S(2)}) collective-permute-start(f32[64,432]{1,0:T(8,128)S(1)} %get-tuple-element.153), channel_id=1, source_target_pairs={{0,6},{1,7},{2,0},{3,1},{4,2},{5,3},{6,4},{7,5},{8,14},{9,15},{10,... | collective-permute-start | bytes 331784 | tf_op jit(solution)/shard_map/ppermute | solution.py:174
  148.7 13.2 %collective-permute-start.4 = (f32[64,432]{1,0:T(8,128)S(1)}, f32[64,432]{1,0:T(8,128)S(1)}, u32[]{:S(2)}, u32[]{:S(2)}) collective-permute-start(f32[64,432]{1,0:T(8,128)S(1)} %get-tuple-element.154), channel_id=1, source_target_pairs={{0,5},{1,6},{2,7},{3,0},{4,1},{5,2},{6,3},{7,4},{8,13},{9,14},{10,... | collective-permute-start | bytes 331784 | tf_op jit(solution)/shard_map/ppermute | solution.py:174
  151.3 10.6 %collective-permute-start.3 = (f32[64,432]{1,0:T(8,128)S(1)}, f32[64,432]{1,0:T(8,128)S(1)}, u32[]{:S(2)}, u32[]{:S(2)}) collective-permute-start(f32[64,432]{1,0:T(8,128)S(1)} %get-tuple-element.155), channel_id=1, source_target_pairs={{0,4},{1,5},{2,6},{3,7},{4,0},{5,1},{6,2},{7,3},{8,12},{9,13},{10,... | collective-permute-start | bytes 331784 | tf_op jit(solution)/shard_map/ppermute | solution.py:174
  155.9 9.2 %collective-permute-start.2 = (f32[64,432]{1,0:T(8,128)S(1)}, f32[64,432]{1,0:T(8,128)S(1)}, u32[]{:S(2)}, u32[]{:S(2)}) collective-permute-start(f32[64,432]{1,0:T(8,128)S(1)} %get-tuple-element.156), channel_id=1, source_target_pairs={{0,3},{1,4},{2,5},{3,6},{4,7},{5,0},{6,1},{7,2},{8,11},{9,12},{10,... | collective-permute-start | bytes 331784 | tf_op jit(solution)/shard_map/ppermute | solution.py:174
  157.8 9.8 %collective-permute-start.1 = (f32[64,432]{1,0:T(8,128)S(1)}, f32[64,432]{1,0:T(8,128)S(1)}, u32[]{:S(2)}, u32[]{:S(2)}) collective-permute-start(f32[64,432]{1,0:T(8,128)S(1)} %get-tuple-element.157), channel_id=1, source_target_pairs={{0,2},{1,3},{2,4},{3,5},{4,6},{5,7},{6,0},{7,1},{8,10},{9,11},{10,... | collective-permute-start | bytes 331784 | tf_op jit(solution)/shard_map/ppermute | solution.py:174
  160.2 8.8 %collective-permute-start = (f32[64,432]{1,0:T(8,128)S(1)}, f32[64,432]{1,0:T(8,128)S(1)}, u32[]{:S(2)}, u32[]{:S(2)}) collective-permute-start(f32[64,432]{1,0:T(8,128)S(1)} %get-tuple-element.151), channel_id=1, source_target_pairs={{0,1},{1,2},{2,3},{3,4},{4,5},{5,6},{6,7},{7,0},{8,9},{9,10},{10,1... | collective-permute-start | bytes 331784 | tf_op jit(solution)/shard_map/ppermute | solution.py:174

commit v3 on v2

--- a/solution.py
+++ b/solution.py
@@ -150,35 +150,24 @@
     rows_count = params.shape[0]
     groups_count = lax.axis_size("tile")
     shard = gauss_total // groups_count
-    lo_size = 48 if shard % 48 == 0 else 1
+    lo_size = 384 if shard % 384 == 0 else shard
     hi_size = gauss_total // lo_size
-    values = jnp.where(live_all[None], compact, 0.0)
-    values = jnp.transpose(values, (1, 2, 0)).reshape(-1, rows_count)
     flat_index = jnp.where(live_all, entries, -1).reshape(-1)
+    values = jnp.where(live_all[None], compact, 0.0).reshape(rows_count, -1)
     hi_index = jnp.where(flat_index >= 0, flat_index // lo_size, -1)
     lo_index = flat_index % lo_size
-    hi_hot = (hi_index[:, None] == jnp.arange(hi_size, dtype=jnp.int32)[None, :]).astype(
+    spread = values[:, None, :] * (
+        hi_index[None, None, :] == jnp.arange(hi_size, dtype=jnp.int32)[None, :, None]
+    ).astype(jnp.float32)
+    lo_hot = (lo_index[None, :] == jnp.arange(lo_size, dtype=jnp.int32)[:, None]).astype(
         jnp.float32
     )
-    lo_hot = (lo_index[:, None] == jnp.arange(lo_size, dtype=jnp.int32)[None, :]).astype(
-        jnp.float32
+    placed = jnp.einsum("che,le->chl", spread, lo_hot, precision=lax.Precision.HIGHEST)
+    gathered = lax.all_to_all(placed, "tile", split_axis=1, concat_axis=1, tiled=True)
+    total = jnp.sum(
+        gathered.reshape(rows_count, groups_count, hi_size // groups_count, lo_size), axis=1
     )
-    spread = (lo_hot[:, :, None] * values[:, None, :]).reshape(-1, lo_size * rows_count)
-    placed = jnp.einsum("eh,ez->hz", hi_hot, spread, precision=lax.Precision.HIGHEST)
-    blocks = placed.reshape(groups_count, hi_size // groups_count, lo_size * rows_count)
-    total = lax.dynamic_index_in_dim(blocks, group_index, 0, keepdims=False)
-    for step in range(1, groups_count):
-        outgoing = lax.dynamic_index_in_dim(
-            blocks, (group_index + step) % groups_count, 0, keepdims=False
-        )
-        total = total + lax.ppermute(
-            outgoing,
-            "tile",
-            perm=[(i, (i + step) % groups_count) for i in range(groups_count)],
-        )
-    shares = jnp.transpose(
-        total.reshape(hi_size // groups_count, lo_size, rows_count), (2, 0, 1)
-    ).reshape(rows_count, shard)
+    shares = total.reshape(rows_count, shard)
     return (rendered, shares[:5], shares[5], shares[6:])
 
 

time: 173 us -> 164 us (0.948)
  the two profiles are of different devices: /device:TPU:264 before, /device:TPU:120 now
where the time goes in v3:
time: 164 us
  waiting for transfers between devices  55.5 us (34%)
  matrix products  35.4 us (22%)
  local copies, waits for them, and re-layouts  32.8 us (20%)
  starting transfers between devices  22.4 us (14%)
  other arithmetic  14.8 us (9%)
  between operations  2.07 us (1%)
    all_to_all x1, waiting for transfers between devices, local(): lax.all_to_all(placed, 'tile', split_axis=1, concat_axis=1, tiled=True)  21 us
    dot_general x9, matrix products, render(): jnp.einsum('kpg,gh->kph', log_keep, ahead, precision=lax.Precision.HIGHEST)  18.7 us
    all_to_all x1, waiting for transfers between devices, local(): lax.all_to_all(dense.reshape(parts_count, tiles_per, 4, pixels), 'dom', s...  17.6 us
    all_to_all x1, waiting for transfers between devices, local(): lax.all_to_all(upstream, 'dom', split_axis=0, concat_axis=0, tiled=True)  17 us
    gather x2, local copies, waits for them, and re-layouts, local(): chosen_all = jnp.take(params, jnp.where(live_all, entries, 0), axis=1)  13.3 us
    all_to_all x1, starting transfers between devices, local(): lax.all_to_all(dense.reshape(parts_count, tiles_per, 4, pixels), 'dom', s...  11.1 us
    dot_general x9, matrix products, render(): jnp.einsum('kpg,ckg->kcp', weight, params[6:9], precision=lax.Precision.H...  9.61 us
    all_to_all x1, starting transfers between devices, local(): lax.all_to_all(upstream, 'dom', split_axis=0, concat_axis=0, tiled=True)  7.09 us
  transfers between devices with their start and end apart: 3, of which 3 were waited for; matrix products, arithmetic and copies ran while one was open for 0% of the time, Pallas kernels for 0%

profile of v3, /device:TPU:120, one launch (start us, length us, event | category | flops | bytes accessed | tf_op | source)
XLA Modules:
  0.0 163.7 jit_solution(7343033842275413312)
XLA Ops:
  0.6 1.3 fusion.119
  2.6 0.7 fusion.126
  3.3 0.7 compare_select_fusion
  4.1 0.7 fusion.123
  4.7 0.7 fusion.124
  5.4 0.7 compare_and_fusion
  6.1 1.7 %pad_maximum_fusion = f32[9,24576]{1,0:T(8,128)S(1)} fusion(f32[3,24576]{1,0:T(4,128)} %param.13, f32[1,24576]{1,0:T(1,128)} %bitcast.228, f32[5,24576]{1,0:T(8,128)} %param.11), kind=kLoop, calls=%fused_computation.168 | loop fusion | flops 442368 | bytes 1769472 | tf_op jit(solution)/shard_map/concatenate | solution.py:84
  7.8 6.9 %copy.50 = f32[9,24576]{0,1:T(8,128)} copy(f32[9,24576]{1,0:T(8,128)S(1)} %pad_maximum_fusion) | data formatting | bytes 1769472 | tf_op jit(solution)/shard_map/concatenate | solution.py:84
  14.7 12.7 %gather_fusion = f32[3072,9]{1,0:T(8,128)S(1)} fusion(f32[9,24576]{0,1:T(8,128)} %copy.50, s32[3072]{0:T(1024)S(1)} %broadcast_clamp_fusion), kind=kCustom, calls=%fused_computation | custom fusion | bytes 233472 | tf_op jit(solution)/shard_map/jit(_take)/gather | solution.py:98
  27.4 0.6 copy.51
  28.1 12.2 %while.20 = (s32[]{:T(128)}, f32[12,4,256]{2,1,0:T(4,128)S(1)}, s32[]{:T(128)}, f32[9,12,256]{2,1,0:T(8,128)S(1)}, f32[12,256]{1,0:T(8,128)S(1)}, /*index=5*/f32...) while((s32[]{:T(128)}, f32[12,4,256]{2,1,0:T(4,128)S(1)}, ...), condition=%wide.region_3.4_spmd, body=%wide.region_1.3_spmd.sunk | while | flops 825316352 | bytes 2339135 | solution.py:116
  28.3 1.8 %fusion.152 = f32[4,256,256]{2,1,0:T(8,128)S(1)} fusion(f32[4,256]{1,0:T(4,128)S(1)} %get-tuple-element.280, f32[4,256]{1,0:T(4,128)S(1)} %get-tuple-element.281, f32[4,256]{1,0:T(4,128)S(1)} %get-tuple-element.282, f32[4,256]{1,0:T(4,128)S(1)} %get-tuple-element.283, f32[4,256]{1,0:T(4,128)S(1)} %get-tuple-element.284, ...), kind=kOutput, calls=%fused_computation.10.clone.1 | convolution fusion | flops 812187648 | bytes 1081344 | tf_op jit(solution)/shard_map/while/body/kpg,gh->kph/dot_general | solution.py:34
  30.1 1.0 fusion.153
  31.1 1.0 fusion.151
  32.3 1.8 %fusion.152 = f32[4,256,256]{2,1,0:T(8,128)S(1)} fusion(f32[4,256]{1,0:T(4,128)S(1)} %get-tuple-element.280, f32[4,256]{1,0:T(4,128)S(1)} %get-tuple-element.281, f32[4,256]{1,0:T(4,128)S(1)} %get-tuple-element.282, f32[4,256]{1,0:T(4,128)S(1)} %get-tuple-element.283, f32[4,256]{1,0:T(4,128)S(1)} %get-tuple-element.284, ...), kind=kOutput, calls=%fused_computation.10.clone.1 | convolution fusion | flops 812187648 | bytes 1081344 | tf_op jit(solution)/shard_map/while/body/kpg,gh->kph/dot_general | solution.py:34
  34.2 1.0 fusion.153
  35.2 1.0 fusion.151
  36.4 1.8 %fusion.152 = f32[4,256,256]{2,1,0:T(8,128)S(1)} fusion(f32[4,256]{1,0:T(4,128)S(1)} %get-tuple-element.280, f32[4,256]{1,0:T(4,128)S(1)} %get-tuple-element.281, f32[4,256]{1,0:T(4,128)S(1)} %get-tuple-element.282, f32[4,256]{1,0:T(4,128)S(1)} %get-tuple-element.283, f32[4,256]{1,0:T(4,128)S(1)} %get-tuple-element.284, ...), kind=kOutput, calls=%fused_computation.10.clone.1 | convolution fusion | flops 812187648 | bytes 1081344 | tf_op jit(solution)/shard_map/while/body/kpg,gh->kph/dot_general | solution.py:34
  38.3 1.0 fusion.153
  39.2 1.0 fusion.151
  40.3 0.9 broadcast_in_dim.56
  41.2 2.1 %scatter_fusion = f32[128,4,256]{2,1,0:T(4,128)} fusion(f32[128,4,256]{2,1,0:T(4,128)} %broadcast_in_dim.56, s32[12]{0:T(128)S(1)} %get-tuple-element.165, f32[12,4,256]{2,1,0:T(4,128)S(1)} %get-tuple-element.85), kind=kCustom, calls=%fused_computation.2 | custom fusion | bytes 147504 | tf_op jit(solution)/shard_map/scatter | solution.py:124
  43.3 11.1 %all-to-all-start = ((f32[64,2,4,256]{3,2,1,0:T(4,128)}), f32[64,2,4,256]{3,2,1,0:T(4,128)S(1)}, u32[]{:S(2)}, u32[]{:S(2)}) async-start(f32[64,2,4,256]{3,2,1,0:T(4,128)} %bitcast.32), calls=%async_computation | async-start | bytes 1048576 | tf_op jit(solution)/shard_map/all_to_all | solution.py:126
  54.4 17.6 %all-to-all-done = f32[64,2,4,256]{3,2,1,0:T(4,128)S(1)} async-done(((f32[64,2,4,256]{3,2,1,0:T(4,128)}), f32[64,2,4,256]{3,2,1,0:T(4,128)S(1)}, u32[]{:S(2)}, u32[]{:S(2)}) %all-to-all-start) | async-done | bytes 524320 | tf_op jit(solution)/shard_map/all_to_all | solution.py:126
  72.0 0.6 fusion.103
  73.1 0.1 reduce_window.9
  73.3 0.1 slice.244
  73.5 0.1 slice.248
  75.0 0.1 slice.251
  75.1 0.1 slice.240
  76.3 0.1 pad.142
  76.4 0.1 slice.241
  76.7 0.1 pad.95
  76.9 0.2 slice.289
  77.2 0.4 convolution_bitcast_fusion
  77.6 1.1 copy.55
  78.8 7.1 %all-to-all-start.1 = ((f32[64,2,4,256]{3,2,1,0:T(4,128)}), f32[64,2,4,256]{3,2,1,0:T(4,128)S(1)}, u32[]{:S(2)}, u32[]{:S(2)}) async-start(f32[64,2,4,256]{3,2,1,0:T(4,128)} %copy.55), calls=%async_computation.1 | async-start | bytes 1048576 | tf_op jit(solution)/shard_map/all_to_all | solution.py:134
  86.0 17.0 %all-to-all-done.1 = f32[64,2,4,256]{3,2,1,0:T(4,128)S(1)} async-done(((f32[64,2,4,256]{3,2,1,0:T(4,128)}), f32[64,2,4,256]{3,2,1,0:T(4,128)S(1)}, u32[]{:S(2)}, u32[]{:S(2)}) %all-to-all-start.1) | async-done | bytes 524320 | tf_op jit(solution)/shard_map/all_to_all | solution.py:134
  103.0 0.6 gather_fusion.1
  103.7 24.3 %while.21 = (s32[]{:T(128)}, f32[9,12,256]{2,1,0:T(8,128)S(1)}, s32[]{:T(128)}, f32[12,4,256]{2,1,0:T(4,128)S(1)}, f32[9,12,256]{2,1,0:T(8,128)S(1)}, /*index=5*...) while((s32[]{:T(128)}, f32[9,12,256]{2,1,0:T(8,128)S(1)}, ...), condition=%wide.region_16.17_spmd, body=%wide.region_8.16_spmd.sunk | while | flops 1655438336 | bytes 5755247 | solution.py:147
  104.0 1.5 convolution_exponential_fusion.3
  105.5 1.0 log-plus-one_reduce_fusion.2
  106.5 1.1 fusion.160
  107.6 2.9 %fusion.161 = (f32[4,256]{1,0:T(4,128)S(1)}, f32[4,256]{1,0:T(4,128)S(1)}, f32[4,256]{1,0:T(4,128)S(1)}, f32[4,256]{1,0:T(4,128)S(1)}, f32[4,256]{1,0:T(4,128)S(1)}, /*index=5*/f32[4,256]{1,0:T(4,128)S(1)}) fusion(f32[4,256]{1,0:T(4,128)S(1)} %get-tuple-element.295, f32[4,256]{1,0:T(4,128)S(1)} %get-tuple-element.296, ...), kind=kOutput, calls=%fused_computation.73.clone.1 | convolution fusion | flops 820570112 | bytes 2158592 | tf_op jit(solution)/shard_map/while/body/transpose(jvp(kpg,gh->kph))/dot_general | solution.py:34
  110.7 1.2 fusion.164
  112.0 1.5 convolution_exponential_fusion.3
  113.5 1.0 log-plus-one_reduce_fusion.2
  114.6 1.1 fusion.160
  115.6 2.9 %fusion.161 = (f32[4,256]{1,0:T(4,128)S(1)}, f32[4,256]{1,0:T(4,128)S(1)}, f32[4,256]{1,0:T(4,128)S(1)}, f32[4,256]{1,0:T(4,128)S(1)}, f32[4,256]{1,0:T(4,128)S(1)}, /*index=5*/f32[4,256]{1,0:T(4,128)S(1)}) fusion(f32[4,256]{1,0:T(4,128)S(1)} %get-tuple-element.295, f32[4,256]{1,0:T(4,128)S(1)} %get-tuple-element.296, ...), kind=kOutput, calls=%fused_computation.73.clone.1 | convolution fusion | flops 820570112 | bytes 2158592 | tf_op jit(solution)/shard_map/while/body/transpose(jvp(kpg,gh->kph))/dot_general | solution.py:34
  118.7 1.2 fusion.164
  120.1 1.5 convolution_exponential_fusion.3
  121.5 1.0 log-plus-one_reduce_fusion.2
  122.6 1.1 fusion.160
  123.7 2.9 %fusion.161 = (f32[4,256]{1,0:T(4,128)S(1)}, f32[4,256]{1,0:T(4,128)S(1)}, f32[4,256]{1,0:T(4,128)S(1)}, f32[4,256]{1,0:T(4,128)S(1)}, f32[4,256]{1,0:T(4,128)S(1)}, /*index=5*/f32[4,256]{1,0:T(4,128)S(1)}) fusion(f32[4,256]{1,0:T(4,128)S(1)} %get-tuple-element.295, f32[4,256]{1,0:T(4,128)S(1)} %get-tuple-element.296, ...), kind=kOutput, calls=%fused_computation.73.clone.1 | convolution fusion | flops 820570112 | bytes 2158592 | tf_op jit(solution)/shard_map/while/body/transpose(jvp(kpg,gh->kph))/dot_general | solution.py:34
  126.7 1.2 fusion.164
  128.0 0.1 copy.66
  128.1 6.1 %fusion.92 = f32[9,64,384]{2,1,0:T(8,128)S(1)} fusion(f32[64,3072]{1,0:T(8,128)S(1)} %fusion.99, f32[9,3072]{1,0:T(8,128)S(1)} %bitcast.226, s32[3072]{0:T(1024)S(1)} %get-tuple-element.160), kind=kOutput, calls=%fused_computation.161 | convolution fusion | flops 8156676096 | bytes 1794048 | tf_op jit(solution)/shard_map/che,le->chl/dot_general | solution.py:165
  134.2 1.7 %copy.56 = f32[9,64,384]{2,0,1:T(8,128)} copy(f32[9,64,384]{2,1,0:T(8,128)S(1)} %fusion.92) | data formatting | bytes 1769472 | tf_op jit(solution)/shard_map/che,le->chl/dot_general | solution.py:165
  135.9 4.2 %all-to-all-start.2 = ((f32[9,64,384]{2,0,1:T(8,128)}), f32[9,64,384]{2,0,1:T(8,128)S(1)}, u32[]{:S(2)}, u32[]{:S(2)}) async-start(f32[9,64,384]{2,0,1:T(8,128)} %copy.56), calls=%async_computation.2 | async-start | bytes 3145728 | tf_op jit(solution)/shard_map/all_to_all | solution.py:166
  140.1 0.6 copy.57
  140.7 21.0 %all-to-all-done.2 = f32[9,64,384]{2,0,1:T(8,128)S(1)} async-done(((f32[9,64,384]{2,0,1:T(8,128)}), f32[9,64,384]{2,0,1:T(8,128)S(1)}, u32[]{:S(2)}, u32[]{:S(2)}) %all-to-all-start.2) | async-done | bytes 884768 | tf_op jit(solution)/shard_map/all_to_all | solution.py:166
  161.8 0.6 slice.323
  162.4 0.6 slice.325
  163.1 0.6 slice.324
  (159 shorter events, 4.6 us)
Async XLA Ops:
  14.7 13.5 %copy-start.1 = (f32[4,256]{1,0:T(4,128)S(1)}, f32[4,256]{1,0:T(4,128)}, u32[]{:S(2)}) copy-start(f32[4,256]{1,0:T(4,128)} %constant.163.clone.1) | copy-start | bytes 12292
  40.3 14.1 %copy-start.2 = (f32[3,2,256]{2,1,0:T(2,128)S(1)}, f32[3,2,256]{2,1,0:T(2,128)}, u32[]{:S(2)}) copy-start(f32[3,2,256]{2,1,0:T(2,128)} %param.17) | copy-start | bytes 18436
  40.3 31.7 %copy-start.3 = (s32[2,64]{1,0:T(2,128)S(1)}, s32[2,64]{1,0:T(2,128)}, u32[]{:S(2)}) copy-start(s32[2,64]{1,0:T(2,128)} %param.16) | copy-start | bytes 1540
  43.3 28.7 %all-to-all-start = ((f32[64,2,4,256]{3,2,1,0:T(4,128)}), f32[64,2,4,256]{3,2,1,0:T(4,128)S(1)}, u32[]{:S(2)}, u32[]{:S(2)}) async-start(f32[64,2,4,256]{3,2,1,0:T(4,128)} %bitcast.32), calls=%async_computation | async-start | bytes 1048576 | tf_op jit(solution)/shard_map/all_to_all | solution.py:126
  77.2 8.7 %copy-start.4 = (s32[1,1,12]{2,1,0:T(1,128)S(1)}, s32[1,1,12]{2,1,0:T(1,128)}, u32[]{:S(2)}) copy-start(s32[1,1,12]{2,1,0:T(1,128)} %param.14) | copy-start | bytes 148
  77.2 8.7 %copy-start = (s32[1,1,12,256]{3,1,2,0:T(1,128)S(1)}, s32[1,1,12,256]{3,1,2,0:T(1,128)}, u32[]{:S(2)}) copy-start(s32[1,1,12,256]{3,1,2,0:T(1,128)} %param.15) | copy-start | bytes 36868
  78.8 24.2 %all-to-all-start.1 = ((f32[64,2,4,256]{3,2,1,0:T(4,128)}), f32[64,2,4,256]{3,2,1,0:T(4,128)S(1)}, u32[]{:S(2)}, u32[]{:S(2)}) async-start(f32[64,2,4,256]{3,2,1,0:T(4,128)} %copy.55), calls=%async_computation.1 | async-start | bytes 1048576 | tf_op jit(solution)/shard_map/all_to_all | solution.py:134
  135.9 25.7 %all-to-all-start.2 = ((f32[9,64,384]{2,0,1:T(8,128)}), f32[9,64,384]{2,0,1:T(8,128)S(1)}, u32[]{:S(2)}, u32[]{:S(2)}) async-start(f32[9,64,384]{2,0,1:T(8,128)} %copy.56), calls=%async_computation.2 | async-start | bytes 3145728 | tf_op jit(solution)/shard_map/all_to_all | solution.py:166

commit v4 on v3

--- a/solution.py
+++ b/solution.py
@@ -95,7 +95,25 @@
     )
 
     live_all = entries >= 0
-    chosen_all = jnp.take(params, jnp.where(live_all, entries, 0), axis=1)
+    groups_count = lax.axis_size("tile")
+    shard = gauss_total // groups_count
+    lo_size = 384 if shard % 384 == 0 else shard
+    hi_size = gauss_total // lo_size
+    safe_index = jnp.where(live_all, entries, 0).reshape(-1)
+    hi_pick = (
+        safe_index[None, None, :] // lo_size
+        == jnp.arange(hi_size, dtype=jnp.int32)[None, :, None]
+    ).astype(jnp.float32)
+    lo_pick = (
+        safe_index[None, :] % lo_size == jnp.arange(lo_size, dtype=jnp.int32)[:, None]
+    ).astype(jnp.float32)
+    by_row = jnp.einsum(
+        "chl,le->che",
+        params.reshape(params.shape[0], hi_size, lo_size),
+        lo_pick,
+        precision=lax.Precision.HIGHEST,
+    )
+    chosen_all = jnp.sum(by_row * hi_pick, axis=1).reshape((params.shape[0],) + entries.shape)
     live_all_f = live_all.astype(jnp.float32)
 
     def gather_turn(first_row):
@@ -148,10 +166,6 @@
         0, turn_count, backward_turn, jnp.zeros(chosen_all.shape, jnp.float32)
     )
     rows_count = params.shape[0]
-    groups_count = lax.axis_size("tile")
-    shard = gauss_total // groups_count
-    lo_size = 384 if shard % 384 == 0 else shard
-    hi_size = gauss_total // lo_size
     flat_index = jnp.where(live_all, entries, -1).reshape(-1)
     values = jnp.where(live_all[None], compact, 0.0).reshape(rows_count, -1)
     hi_index = jnp.where(flat_index >= 0, flat_index // lo_size, -1)

time: 164 us -> 146 us (0.89)
  the two profiles are of different devices: /device:TPU:120 before, /device:TPU:328 now
where the time goes in v4:
time: 146 us; the launch traced here: 145 us
  waiting for transfers between devices  52.2 us (36%)
  matrix products  41.6 us (28%)
  starting transfers between devices  21 us (14%)
  local copies, waits for them, and re-layouts  15.8 us (11%)
  other arithmetic  11.7 us (8%)
  between operations  2.07 us (1%)
    all_to_all x1, waiting for transfers between devices, local(): lax.all_to_all(placed, 'tile', split_axis=1, concat_axis=1, tiled=True)  21 us
    dot_general x9, matrix products, render(): jnp.einsum('kpg,gh->kph', log_keep, ahead, precision=lax.Precision.HIGHEST)  18.7 us
    all_to_all x1, waiting for transfers between devices, local(): lax.all_to_all(dense.reshape(parts_count, tiles_per, 4, pixels), 'dom', s...  15.9 us
    all_to_all x1, waiting for transfers between devices, local(): lax.all_to_all(upstream, 'dom', split_axis=0, concat_axis=0, tiled=True)  15.3 us
    dot_general x9, matrix products, render(): jnp.einsum('kpg,ckg->kcp', weight, params[6:9], precision=lax.Precision.H...  9.61 us
    all_to_all x1, starting transfers between devices, local(): lax.all_to_all(upstream, 'dom', split_axis=0, concat_axis=0, tiled=True)  8.76 us
    all_to_all x1, starting transfers between devices, local(): lax.all_to_all(dense.reshape(parts_count, tiles_per, 4, pixels), 'dom', s...  7.93 us
    dot_general x1, matrix products, local(): jnp.einsum('chl,le->che', params.reshape(params.shape[0], hi_size, lo_siz...  6.15 us
  transfers between devices with their start and end apart: 3, of which 3 were waited for; matrix products, arithmetic and copies ran while one was open for 0% of the time, Pallas kernels for 0%

profile of v4, /device:TPU:328, one launch (start us, length us, event | category | flops | bytes accessed | tf_op | source)
XLA Modules:
  0.0 145.1 jit_solution(1725241602831877767)
XLA Ops:
  0.6 0.7 fusion.134
  1.3 1.3 fusion.130
  3.3 0.7 fusion.138
  4.0 0.7 add_select_fusion
  4.7 1.0 copy.84
  5.8 0.9 concatenate.38
  6.7 1.2 copy.83
  7.9 0.1 fusion.107
  8.1 6.2 %multiply_reduce_fusion.1 = f32[9,3072]{1,0:T(8,128)S(1)} fusion(f32[64,3072]{1,0:T(8,128)S(1)} %get-tuple-element.215, s32[3072]{0:T(1024)S(1)} %get-tuple-element.208, f32[3,64,384]{2,1,0:T(8,128)S(1)} %bitcast.227, f32[1,64,384]{2,1,0:T(8,128)S(1)} %concatenate.38, f32[5,64,384]{2,1,0:T(8,128)S(1)} %bitcast.225), kind=kOutput, calls=%fused_computation.162 | convolution fusion | flops 8158860288 | bytes 1794048 | tf_op jit(solution)/shard_map/chl,le->che/dot_general | solution.py:110
  14.4 12.2 %while.20 = (s32[]{:T(128)}, f32[12,4,256]{2,1,0:T(4,128)S(1)}, s32[]{:T(128)}, f32[9,12,256]{2,1,0:T(8,128)S(1)}, f32[12,256]{1,0:T(8,128)S(1)}, /*index=5*/f32...) while((s32[]{:T(128)}, f32[12,4,256]{2,1,0:T(4,128)S(1)}, ...), condition=%wide.region_4.5_spmd, body=%wide.region_2.4_spmd.sunk | while | flops 825316352 | bytes 2339143 | solution.py:134
  14.5 1.0 fusion.164
  15.6 1.8 %fusion.165 = f32[4,256,256]{2,1,0:T(8,128)S(1)} fusion(f32[4,256]{1,0:T(4,128)S(1)} %get-tuple-element.329, f32[4,256]{1,0:T(4,128)S(1)} %get-tuple-element.330, f32[4,256]{1,0:T(4,128)S(1)} %get-tuple-element.331, f32[4,256]{1,0:T(4,128)S(1)} %get-tuple-element.332, f32[4,256]{1,0:T(4,128)S(1)} %get-tuple-element.333, ...), kind=kOutput, calls=%fused_computation.9.clone.1 | convolution fusion | flops 812187648 | bytes 1081344 | tf_op jit(solution)/shard_map/while/body/kpg,gh->kph/dot_general | solution.py:34
  17.5 1.0 fusion.166
  18.6 1.0 fusion.164
  19.6 1.8 %fusion.165 = f32[4,256,256]{2,1,0:T(8,128)S(1)} fusion(f32[4,256]{1,0:T(4,128)S(1)} %get-tuple-element.329, f32[4,256]{1,0:T(4,128)S(1)} %get-tuple-element.330, f32[4,256]{1,0:T(4,128)S(1)} %get-tuple-element.331, f32[4,256]{1,0:T(4,128)S(1)} %get-tuple-element.332, f32[4,256]{1,0:T(4,128)S(1)} %get-tuple-element.333, ...), kind=kOutput, calls=%fused_computation.9.clone.1 | convolution fusion | flops 812187648 | bytes 1081344 | tf_op jit(solution)/shard_map/while/body/kpg,gh->kph/dot_general | solution.py:34
  21.5 1.0 fusion.166
  22.7 1.0 fusion.164
  23.7 1.8 %fusion.165 = f32[4,256,256]{2,1,0:T(8,128)S(1)} fusion(f32[4,256]{1,0:T(4,128)S(1)} %get-tuple-element.329, f32[4,256]{1,0:T(4,128)S(1)} %get-tuple-element.330, f32[4,256]{1,0:T(4,128)S(1)} %get-tuple-element.331, f32[4,256]{1,0:T(4,128)S(1)} %get-tuple-element.332, f32[4,256]{1,0:T(4,128)S(1)} %get-tuple-element.333, ...), kind=kOutput, calls=%fused_computation.9.clone.1 | convolution fusion | flops 812187648 | bytes 1081344 | tf_op jit(solution)/shard_map/while/body/kpg,gh->kph/dot_general | solution.py:34
  25.6 1.0 fusion.166
  26.6 0.9 broadcast_in_dim.42
  27.5 2.1 %scatter_fusion = f32[128,4,256]{2,1,0:T(4,128)} fusion(f32[128,4,256]{2,1,0:T(4,128)} %broadcast_in_dim.42, s32[12]{0:T(128)S(1)} %get-tuple-element.212, f32[12,4,256]{2,1,0:T(4,128)S(1)} %get-tuple-element.85), kind=kCustom, calls=%fused_computation.1 | custom fusion | bytes 147504 | tf_op jit(solution)/shard_map/scatter | solution.py:142
  29.5 7.9 %all-to-all-start = ((f32[64,2,4,256]{3,2,1,0:T(4,128)}), f32[64,2,4,256]{3,2,1,0:T(4,128)S(1)}, u32[]{:S(2)}, u32[]{:S(2)}) async-start(f32[64,2,4,256]{3,2,1,0:T(4,128)} %bitcast.30), calls=%async_computation | async-start | bytes 1048576 | tf_op jit(solution)/shard_map/all_to_all | solution.py:144
  37.5 15.9 %all-to-all-done = f32[64,2,4,256]{3,2,1,0:T(4,128)S(1)} async-done(((f32[64,2,4,256]{3,2,1,0:T(4,128)}), f32[64,2,4,256]{3,2,1,0:T(4,128)S(1)}, u32[]{:S(2)}, u32[]{:S(2)}) %all-to-all-start) | async-done | bytes 524320 | tf_op jit(solution)/shard_map/all_to_all | solution.py:144
  53.4 0.6 fusion.112
  54.0 0.1 reduce_window.9
  54.3 0.1 slice.240
  54.4 0.1 slice.244
  54.6 0.1 slice.248
  56.5 0.1 slice.251
  56.7 0.1 slice.241
  58.0 0.1 pad.94
  58.1 0.1 pad.150
  58.3 0.2 slice.289
  58.6 0.4 convolution_bitcast_fusion
  59.0 1.1 copy.53
  60.1 8.8 %all-to-all-start.1 = ((f32[64,2,4,256]{3,2,1,0:T(4,128)}), f32[64,2,4,256]{3,2,1,0:T(4,128)S(1)}, u32[]{:S(2)}, u32[]{:S(2)}) async-start(f32[64,2,4,256]{3,2,1,0:T(4,128)} %copy.53), calls=%async_computation.1 | async-start | bytes 1048576 | tf_op jit(solution)/shard_map/all_to_all | solution.py:152
  68.9 15.3 %all-to-all-done.1 = f32[64,2,4,256]{3,2,1,0:T(4,128)S(1)} async-done(((f32[64,2,4,256]{3,2,1,0:T(4,128)}), f32[64,2,4,256]{3,2,1,0:T(4,128)S(1)}, u32[]{:S(2)}, u32[]{:S(2)}) %all-to-all-start.1) | async-done | bytes 524320 | tf_op jit(solution)/shard_map/all_to_all | solution.py:152
  84.2 0.6 gather_fusion
  84.9 24.3 %while.21 = (s32[]{:T(128)}, f32[9,12,256]{2,1,0:T(8,128)S(1)}, s32[]{:T(128)}, f32[12,4,256]{2,1,0:T(4,128)S(1)}, f32[9,12,256]{2,1,0:T(8,128)S(1)}, /*index=5*...) while((s32[]{:T(128)}, f32[9,12,256]{2,1,0:T(8,128)S(1)}, ...), condition=%wide.region_17.18_spmd, body=%wide.region_9.17_spmd.sunk | while | flops 1655438336 | bytes 5755255 | solution.py:165
  85.1 1.5 %convolution_exponential_fusion.3 = f32[4,256,256]{2,1,0:T(8,128)S(1)} fusion(f32[4,256]{1,0:T(4,128)S(1)} %get-tuple-element.347, f32[4,256]{1,0:T(4,128)S(1)} %get-tuple-element.344, f32[4,256]{1,0:T(4,128)S(1)} %get-tuple-element.345, f32[4,256]{1,0:T(4,128)S(1)} %get-tuple-element.348, f32[4,256]{1,0:T(4,128)S(1)} %get-tuple-element.346, ...), kind=kOutput, calls=%fused_computation.59.clone.1 | convolution fusion | flops 808779776 | bytes 1081344 | tf_op jit(solution)/shard_map/while/body/jvp(kpg,gh->kph)/dot_general | solution.py:34
  86.6 1.1 fusion.173
  87.6 1.0 log-plus-one_reduce_fusion.2
  88.7 2.9 %fusion.174 = (f32[4,256]{1,0:T(4,128)S(1)}, f32[4,256]{1,0:T(4,128)S(1)}, f32[4,256]{1,0:T(4,128)S(1)}, f32[4,256]{1,0:T(4,128)S(1)}, f32[4,256]{1,0:T(4,128)S(1)}, /*index=5*/f32[4,256]{1,0:T(4,128)S(1)}) fusion(f32[4,256]{1,0:T(4,128)S(1)} %get-tuple-element.344, f32[4,256]{1,0:T(4,128)S(1)} %get-tuple-element.345, ...), kind=kOutput, calls=%fused_computation.72.clone.1 | convolution fusion | flops 820570112 | bytes 2158592 | tf_op jit(solution)/shard_map/while/body/transpose(jvp(kpg,gh->kph))/dot_general | solution.py:34
  91.7 1.2 fusion.177
  93.1 1.5 %convolution_exponential_fusion.3 = f32[4,256,256]{2,1,0:T(8,128)S(1)} fusion(f32[4,256]{1,0:T(4,128)S(1)} %get-tuple-element.347, f32[4,256]{1,0:T(4,128)S(1)} %get-tuple-element.344, f32[4,256]{1,0:T(4,128)S(1)} %get-tuple-element.345, f32[4,256]{1,0:T(4,128)S(1)} %get-tuple-element.348, f32[4,256]{1,0:T(4,128)S(1)} %get-tuple-element.346, ...), kind=kOutput, calls=%fused_computation.59.clone.1 | convolution fusion | flops 808779776 | bytes 1081344 | tf_op jit(solution)/shard_map/while/body/jvp(kpg,gh->kph)/dot_general | solution.py:34
  94.6 1.1 fusion.173
  95.7 1.0 log-plus-one_reduce_fusion.2
  96.7 2.9 %fusion.174 = (f32[4,256]{1,0:T(4,128)S(1)}, f32[4,256]{1,0:T(4,128)S(1)}, f32[4,256]{1,0:T(4,128)S(1)}, f32[4,256]{1,0:T(4,128)S(1)}, f32[4,256]{1,0:T(4,128)S(1)}, /*index=5*/f32[4,256]{1,0:T(4,128)S(1)}) fusion(f32[4,256]{1,0:T(4,128)S(1)} %get-tuple-element.344, f32[4,256]{1,0:T(4,128)S(1)} %get-tuple-element.345, ...), kind=kOutput, calls=%fused_computation.72.clone.1 | convolution fusion | flops 820570112 | bytes 2158592 | tf_op jit(solution)/shard_map/while/body/transpose(jvp(kpg,gh->kph))/dot_general | solution.py:34
  99.8 1.2 fusion.177
  101.1 1.5 %convolution_exponential_fusion.3 = f32[4,256,256]{2,1,0:T(8,128)S(1)} fusion(f32[4,256]{1,0:T(4,128)S(1)} %get-tuple-element.347, f32[4,256]{1,0:T(4,128)S(1)} %get-tuple-element.344, f32[4,256]{1,0:T(4,128)S(1)} %get-tuple-element.345, f32[4,256]{1,0:T(4,128)S(1)} %get-tuple-element.348, f32[4,256]{1,0:T(4,128)S(1)} %get-tuple-element.346, ...), kind=kOutput, calls=%fused_computation.59.clone.1 | convolution fusion | flops 808779776 | bytes 1081344 | tf_op jit(solution)/shard_map/while/body/jvp(kpg,gh->kph)/dot_general | solution.py:34
  102.6 1.0 fusion.173
  103.7 1.0 log-plus-one_reduce_fusion.2
  104.7 2.9 %fusion.174 = (f32[4,256]{1,0:T(4,128)S(1)}, f32[4,256]{1,0:T(4,128)S(1)}, f32[4,256]{1,0:T(4,128)S(1)}, f32[4,256]{1,0:T(4,128)S(1)}, f32[4,256]{1,0:T(4,128)S(1)}, /*index=5*/f32[4,256]{1,0:T(4,128)S(1)}) fusion(f32[4,256]{1,0:T(4,128)S(1)} %get-tuple-element.344, f32[4,256]{1,0:T(4,128)S(1)} %get-tuple-element.345, ...), kind=kOutput, calls=%fused_computation.72.clone.1 | convolution fusion | flops 820570112 | bytes 2158592 | tf_op jit(solution)/shard_map/while/body/transpose(jvp(kpg,gh->kph))/dot_general | solution.py:34
  107.8 1.2 fusion.177
  109.3 0.1 copy.65
  109.4 6.1 %fusion.92 = f32[9,64,384]{2,1,0:T(8,128)S(1)} fusion(f32[64,3072]{1,0:T(8,128)S(1)} %get-tuple-element.216, f32[9,3072]{1,0:T(8,128)S(1)} %bitcast.228, s32[3072]{0:T(1024)S(1)} %get-tuple-element.205), kind=kOutput, calls=%fused_computation.160 | convolution fusion | flops 8156676096 | bytes 1794048 | tf_op jit(solution)/shard_map/che,le->chl/dot_general | solution.py:179
  115.5 1.7 %copy.54 = f32[9,64,384]{2,0,1:T(8,128)} copy(f32[9,64,384]{2,1,0:T(8,128)S(1)} %fusion.92) | data formatting | bytes 1769472 | tf_op jit(solution)/shard_map/che,le->chl/dot_general | solution.py:179
  117.2 4.3 %all-to-all-start.2 = ((f32[9,64,384]{2,0,1:T(8,128)}), f32[9,64,384]{2,0,1:T(8,128)S(1)}, u32[]{:S(2)}, u32[]{:S(2)}) async-start(f32[9,64,384]{2,0,1:T(8,128)} %copy.54), calls=%async_computation.2 | async-start | bytes 3145728 | tf_op jit(solution)/shard_map/all_to_all | solution.py:180
  121.5 0.6 copy.55
  122.1 21.0 %all-to-all-done.2 = f32[9,64,384]{2,0,1:T(8,128)S(1)} async-done(((f32[9,64,384]{2,0,1:T(8,128)}), f32[9,64,384]{2,0,1:T(8,128)S(1)}, u32[]{:S(2)}, u32[]{:S(2)}) %all-to-all-start.2) | async-done | bytes 884768 | tf_op jit(solution)/shard_map/all_to_all | solution.py:180
  143.1 0.1 reduce_sum.141
  143.2 0.6 slice.321
  143.8 0.6 slice.322
  144.4 0.6 slice.323
  (154 shorter events, 4.4 us)
Async XLA Ops:
  8.0 6.2 %copy-start.3 = (s32[1,1,12]{2,1,0:T(1,128)S(1)}, s32[1,1,12]{2,1,0:T(1,128)}, u32[]{:S(2)}) copy-start(s32[1,1,12]{2,1,0:T(1,128)} %param.14) | copy-start | bytes 148
  8.0 6.3 %copy-start = (f32[4,256]{1,0:T(4,128)S(1)}, f32[4,256]{1,0:T(4,128)}, u32[]{:S(2)}) copy-start(f32[4,256]{1,0:T(4,128)} %constant.162.clone.1) | copy-start | bytes 12292
  26.6 10.9 %copy-start.1 = (f32[3,2,256]{2,1,0:T(2,128)S(1)}, f32[3,2,256]{2,1,0:T(2,128)}, u32[]{:S(2)}) copy-start(f32[3,2,256]{2,1,0:T(2,128)} %param.17) | copy-start | bytes 18436
  26.6 26.8 %copy-start.2 = (s32[2,64]{1,0:T(2,128)S(1)}, s32[2,64]{1,0:T(2,128)}, u32[]{:S(2)}) copy-start(s32[2,64]{1,0:T(2,128)} %param.16) | copy-start | bytes 1540
  29.5 23.9 %all-to-all-start = ((f32[64,2,4,256]{3,2,1,0:T(4,128)}), f32[64,2,4,256]{3,2,1,0:T(4,128)S(1)}, u32[]{:S(2)}, u32[]{:S(2)}) async-start(f32[64,2,4,256]{3,2,1,0:T(4,128)} %bitcast.30), calls=%async_computation | async-start | bytes 1048576 | tf_op jit(solution)/shard_map/all_to_all | solution.py:144
  60.1 24.1 %all-to-all-start.1 = ((f32[64,2,4,256]{3,2,1,0:T(4,128)}), f32[64,2,4,256]{3,2,1,0:T(4,128)S(1)}, u32[]{:S(2)}, u32[]{:S(2)}) async-start(f32[64,2,4,256]{3,2,1,0:T(4,128)} %copy.53), calls=%async_computation.1 | async-start | bytes 1048576 | tf_op jit(solution)/shard_map/all_to_all | solution.py:152
  117.2 25.9 %all-to-all-start.2 = ((f32[9,64,384]{2,0,1:T(8,128)}), f32[9,64,384]{2,0,1:T(8,128)S(1)}, u32[]{:S(2)}, u32[]{:S(2)}) async-start(f32[9,64,384]{2,0,1:T(8,128)} %copy.54), calls=%async_computation.2 | async-start | bytes 3145728 | tf_op jit(solution)/shard_map/all_to_all | solution.py:180

commit v5 on v4

--- a/solution.py
+++ b/solution.py
@@ -134,25 +134,29 @@
     partial_value = lax.fori_loop(
         0, turn_count, forward_turn, jnp.broadcast_to(default, (slots_count, 4, pixels))
     )
-    block_slots = parts_count * tiles_per
-    target = jnp.where(tile_ids >= 0, tile_ids, block_slots)
+    home = lax.axis_index("dom")
+    cover_all = lax.all_gather(tile_ids.astype(jnp.float32), "dom", axis=0, tiled=False)
+    first_here = jnp.any(cover_all == (home * tiles_per).astype(jnp.float32), axis=1)
+    second_here = jnp.any(cover_all == (home * tiles_per + 1).astype(jnp.float32), axis=1)
+    target = jnp.where(tile_ids >= 0, tile_ids // tiles_per, parts_count)
     dense = (
-        jnp.broadcast_to(default, (block_slots, 4, pixels))
+        jnp.broadcast_to(default, (parts_count, 4, pixels))
         .at[target]
         .set(partial_value, mode="drop")
     )
-    arrived = lax.all_to_all(
-        dense.reshape(parts_count, tiles_per, 4, pixels),
-        "dom",
-        split_axis=0,
-        concat_axis=0,
-        tiled=True,
+    landed = lax.all_to_all(dense, "dom", split_axis=0, concat_axis=0, tiled=True)
+    blank = jnp.broadcast_to(default, landed.shape)
+    arrived = jnp.stack(
+        [
+            jnp.where(first_here[:, None, None], landed, blank),
+            jnp.where(second_here[:, None, None], landed, blank),
+        ],
+        axis=1,
     )
     rendered, upstream = composite(arrived, orders, cotangent)
-    returned = lax.all_to_all(upstream, "dom", split_axis=0, concat_axis=0, tiled=True)
-    slot_grads = jnp.take(
-        returned.reshape(block_slots, 4, pixels), jnp.maximum(tile_ids, 0), axis=0
-    )
+    sent_back = jnp.where(second_here[:, None, None], upstream[:, 1], upstream[:, 0])
+    returned = lax.all_to_all(sent_back, "dom", split_axis=0, concat_axis=0, tiled=True)
+    slot_grads = jnp.take(returned, jnp.maximum(tile_ids, 0) // tiles_per, axis=0)
 
     def backward_turn(turn_index, compact):
         first_row = turn_index * turn_rows

time: 146 us -> 172 us (1.18)
  the two profiles are of different devices: /device:TPU:328 before, /device:TPU:216 now
where the time goes in v5:
time: 172 us
  blocking collectives  43.5 us (25%)
  matrix products  41.5 us (24%)
  waiting for transfers between devices  30 us (17%)
  starting transfers between devices  23.9 us (14%)
  other arithmetic  15.8 us (9%)
  local copies, waits for them, and re-layouts  14.2 us (8%)
  between operations  2.1 us (1%)
    all_gather x1, blocking collectives, local(): lax.all_gather(tile_ids.astype(jnp.float32), 'dom', axis=0, tiled=False)  43.5 us
    all_to_all x1, waiting for transfers between devices, local(): lax.all_to_all(placed, 'tile', split_axis=1, concat_axis=1, tiled=True)  21 us
    dot_general x9, matrix products, render(): jnp.einsum('kpg,gh->kph', log_keep, ahead, precision=lax.Precision.HIGHEST)  18.7 us
    all_to_all x1, starting transfers between devices, local(): lax.all_to_all(dense, 'dom', split_axis=0, concat_axis=0, tiled=True)  9.82 us
    all_to_all x1, starting transfers between devices, local(): lax.all_to_all(sent_back, 'dom', split_axis=0, concat_axis=0, tiled=True)  9.8 us
    dot_general x9, matrix products, render(): jnp.einsum('kpg,ckg->kcp', weight, params[6:9], precision=lax.Precision.H...  9.63 us
    all_to_all x1, waiting for transfers between devices, local(): lax.all_to_all(sent_back, 'dom', split_axis=0, concat_axis=0, tiled=True)  9.05 us
    dot_general x1, matrix products, local(): jnp.einsum('chl,le->che', params.reshape(params.shape[0], hi_size, lo_siz...  6.15 us
  transfers between devices with their start and end apart: 3, of which 2 were waited for; matrix products, arithmetic and copies ran while one was open for 2% of the time, Pallas kernels for 0%

profile of v5, /device:TPU:216, one launch (start us, length us, event | category | flops | bytes accessed | tf_op | source)
XLA Modules:
  0.0 171.9 jit_solution(11486053413610788049)
XLA Ops:
  0.7 0.7 compare_and_fusion
  1.4 1.4 fusion.147
  3.4 0.7 fusion.137
  4.1 0.7 fusion.135
  4.8 0.7 fusion.142
  5.5 0.7 add_select_fusion
  6.2 0.9 concatenate.38
  7.2 1.0 copy.94
  8.4 6.1 %multiply_reduce_fusion.1 = f32[9,3072]{1,0:T(8,128)S(1)} fusion(f32[64,3072]{1,0:T(8,128)S(1)} %get-tuple-element.229, s32[3072]{0:T(1024)S(1)} %get-tuple-element.222, f32[3,64,384]{2,1,0:T(8,128)S(1)} %bitcast.242, f32[1,64,384]{2,1,0:T(8,128)S(1)} %concatenate.38, f32[5,64,384]{2,1,0:T(8,128)S(1)} %bitcast.240), kind=kOutput, calls=%fused_computation.162 | convolution fusion | flops 8158860288 | bytes 1794048 | tf_op jit(solution)/shard_map/chl,le->che/dot_general | solution.py:110
  14.8 12.2 %while.20 = (s32[]{:T(128)}, f32[12,4,256]{2,1,0:T(4,128)S(1)}, s32[]{:T(128)}, f32[9,12,256]{2,1,0:T(8,128)S(1)}, f32[12,256]{1,0:T(8,128)S(1)}, /*index=5*/f32...) while((s32[]{:T(128)}, f32[12,4,256]{2,1,0:T(4,128)S(1)}, ...), condition=%wide.region_5.6_spmd, body=%wide.region_3.5_spmd.sunk | while | flops 825316352 | bytes 2339135 | solution.py:134
  15.0 1.0 fusion.169
  16.0 1.8 %fusion.170 = f32[4,256,256]{2,1,0:T(8,128)S(1)} fusion(f32[4,256]{1,0:T(4,128)S(1)} %get-tuple-element.341, f32[4,256]{1,0:T(4,128)S(1)} %get-tuple-element.342, f32[4,256]{1,0:T(4,128)S(1)} %get-tuple-element.343, f32[4,256]{1,0:T(4,128)S(1)} %get-tuple-element.344, f32[4,256]{1,0:T(4,128)S(1)} %get-tuple-element.345, ...), kind=kOutput, calls=%fused_computation.9.clone.1 | convolution fusion | flops 812187648 | bytes 1081344 | tf_op jit(solution)/shard_map/while/body/kpg,gh->kph/dot_general | solution.py:34
  17.9 1.0 fusion.171
  19.0 1.0 fusion.169
  20.1 1.8 %fusion.170 = f32[4,256,256]{2,1,0:T(8,128)S(1)} fusion(f32[4,256]{1,0:T(4,128)S(1)} %get-tuple-element.341, f32[4,256]{1,0:T(4,128)S(1)} %get-tuple-element.342, f32[4,256]{1,0:T(4,128)S(1)} %get-tuple-element.343, f32[4,256]{1,0:T(4,128)S(1)} %get-tuple-element.344, f32[4,256]{1,0:T(4,128)S(1)} %get-tuple-element.345, ...), kind=kOutput, calls=%fused_computation.9.clone.1 | convolution fusion | flops 812187648 | bytes 1081344 | tf_op jit(solution)/shard_map/while/body/kpg,gh->kph/dot_general | solution.py:34
  21.9 1.0 fusion.171
  23.1 1.0 fusion.169
  24.1 1.8 %fusion.170 = f32[4,256,256]{2,1,0:T(8,128)S(1)} fusion(f32[4,256]{1,0:T(4,128)S(1)} %get-tuple-element.341, f32[4,256]{1,0:T(4,128)S(1)} %get-tuple-element.342, f32[4,256]{1,0:T(4,128)S(1)} %get-tuple-element.343, f32[4,256]{1,0:T(4,128)S(1)} %get-tuple-element.344, f32[4,256]{1,0:T(4,128)S(1)} %get-tuple-element.345, ...), kind=kOutput, calls=%fused_computation.9.clone.1 | convolution fusion | flops 812187648 | bytes 1081344 | tf_op jit(solution)/shard_map/while/body/kpg,gh->kph/dot_general | solution.py:34
  26.0 1.0 fusion.171
  27.0 0.7 broadcast_in_dim.65.clone
  27.7 2.1 %scatter_fusion = f32[64,4,256]{2,1,0:T(4,128)} fusion(f32[64,4,256]{2,1,0:T(4,128)} %broadcast_in_dim.65.clone, s32[12]{0:T(128)S(1)} %get-tuple-element.226, f32[12,4,256]{2,1,0:T(4,128)S(1)} %get-tuple-element.85), kind=kCustom, calls=%fused_computation.1 | custom fusion | bytes 147504 | tf_op jit(solution)/shard_map/scatter | solution.py:145
  29.8 9.8 %all-to-all-start = ((f32[64,4,256]{2,1,0:T(4,128)}), f32[64,4,256]{2,1,0:T(4,128)S(1)}, u32[]{:S(2)}, u32[]{:S(2)}) async-start(f32[64,4,256]{2,1,0:T(4,128)} %scatter_fusion), calls=%async_computation | async-start | bytes 524288 | tf_op jit(solution)/shard_map/all_to_all | solution.py:147
  39.7 43.5 %all-gather = f32[64,1,12]{2,1,0:T(1,128)S(1)} all-gather(f32[1,1,12]{2,1,0:T(1,128)S(1)} %get-tuple-element.227), channel_id=2, replica_groups=mesh['dom'=64,'tile'=8] {'dom'}, dimensions={0}, use_global_device_ids=true | all-gather | bytes 3120 | tf_op jit(solution)/shard_map/all_gather | solution.py:138
  83.1 2.4 %compare_reduce_fusion.1 = (pred[64]{0:T(512)(128)(4,1)S(1)}, pred[64]{0:T(512)(128)(4,1)S(1)}) fusion(f32[64,1,12]{2,1,0:T(1,128)S(1)} %all-gather, f32[]{:T(128)S(6)} %convert_element_type.55, f32[]{:T(128)S(6)} %convert_element_type.61), kind=kLoop, calls=%fused_computation.205 | loop fusion | flops 2944 | bytes 3208 | tf_op jit(solution)/shard_map/reduce_or | solution.py:139
  85.6 0.5 fusion.109
  86.7 0.1 reduce_window.9
  87.0 0.1 slice.250
  87.1 0.1 slice.246
  87.2 0.1 slice.254
  87.8 0.1 slice.257
  88.9 0.1 slice.247
  90.1 0.1 pad.96
  90.2 0.1 pad.160
  90.4 0.2 slice.295
  90.7 0.4 convolution_bitcast_fusion
  91.2 0.9 copy.62
  92.1 9.8 %all-to-all-start.1 = ((f32[64,4,256]{2,1,0:T(4,128)}), f32[64,4,256]{2,1,0:T(4,128)S(1)}, u32[]{:S(2)}, u32[]{:S(2)}) async-start(f32[64,4,256]{2,1,0:T(4,128)} %copy.62), calls=%async_computation.1 | async-start | bytes 524288 | tf_op jit(solution)/shard_map/all_to_all | solution.py:158
  101.9 9.1 %all-to-all-done.1 = f32[64,4,256]{2,1,0:T(4,128)S(1)} async-done(((f32[64,4,256]{2,1,0:T(4,128)}), f32[64,4,256]{2,1,0:T(4,128)S(1)}, u32[]{:S(2)}, u32[]{:S(2)}) %all-to-all-start.1) | async-done | bytes 262176 | tf_op jit(solution)/shard_map/all_to_all | solution.py:158
  111.0 0.6 gather_fusion
  111.6 24.4 %while.21 = (s32[]{:T(128)}, f32[9,12,256]{2,1,0:T(8,128)S(1)}, s32[]{:T(128)}, f32[12,4,256]{2,1,0:T(4,128)S(1)}, f32[9,12,256]{2,1,0:T(8,128)S(1)}, /*index=5*...) while((s32[]{:T(128)}, f32[9,12,256]{2,1,0:T(8,128)S(1)}, ...), condition=%wide.region_19.20_spmd, body=%wide.region_11.19_spmd.sunk | while | flops 1655438336 | bytes 5755247 | solution.py:169
  111.8 1.0 log-plus-one_reduce_fusion.2
  112.9 1.1 fusion.178
  113.9 1.5 convolution_exponential_fusion.3
  115.4 2.9 %fusion.179 = (f32[4,256]{1,0:T(4,128)S(1)}, f32[4,256]{1,0:T(4,128)S(1)}, f32[4,256]{1,0:T(4,128)S(1)}, f32[4,256]{1,0:T(4,128)S(1)}, f32[4,256]{1,0:T(4,128)S(1)}, /*index=5*/f32[4,256]{1,0:T(4,128)S(1)}) fusion(f32[4,256]{1,0:T(4,128)S(1)} %get-tuple-element.356, f32[4,256]{1,0:T(4,128)S(1)} %get-tuple-element.357, ...), kind=kOutput, calls=%fused_computation.72.clone.1 | convolution fusion | flops 820570112 | bytes 2158592 | tf_op jit(solution)/shard_map/while/body/transpose(jvp(kpg,gh->kph))/dot_general | solution.py:34
  118.3 1.2 fusion.182
  119.9 1.0 log-plus-one_reduce_fusion.2
  120.9 1.1 fusion.178
  122.0 1.5 convolution_exponential_fusion.3
  123.4 2.9 %fusion.179 = (f32[4,256]{1,0:T(4,128)S(1)}, f32[4,256]{1,0:T(4,128)S(1)}, f32[4,256]{1,0:T(4,128)S(1)}, f32[4,256]{1,0:T(4,128)S(1)}, f32[4,256]{1,0:T(4,128)S(1)}, /*index=5*/f32[4,256]{1,0:T(4,128)S(1)}) fusion(f32[4,256]{1,0:T(4,128)S(1)} %get-tuple-element.356, f32[4,256]{1,0:T(4,128)S(1)} %get-tuple-element.357, ...), kind=kOutput, calls=%fused_computation.72.clone.1 | convolution fusion | flops 820570112 | bytes 2158592 | tf_op jit(solution)/shard_map/while/body/transpose(jvp(kpg,gh->kph))/dot_general | solution.py:34
  126.4 1.2 fusion.182
  127.9 1.0 log-plus-one_reduce_fusion.2
  129.0 1.1 fusion.178
  130.0 1.5 convolution_exponential_fusion.3
  131.5 2.9 %fusion.179 = (f32[4,256]{1,0:T(4,128)S(1)}, f32[4,256]{1,0:T(4,128)S(1)}, f32[4,256]{1,0:T(4,128)S(1)}, f32[4,256]{1,0:T(4,128)S(1)}, f32[4,256]{1,0:T(4,128)S(1)}, /*index=5*/f32[4,256]{1,0:T(4,128)S(1)}) fusion(f32[4,256]{1,0:T(4,128)S(1)} %get-tuple-element.356, f32[4,256]{1,0:T(4,128)S(1)} %get-tuple-element.357, ...), kind=kOutput, calls=%fused_computation.72.clone.1 | convolution fusion | flops 820570112 | bytes 2158592 | tf_op jit(solution)/shard_map/while/body/transpose(jvp(kpg,gh->kph))/dot_general | solution.py:34
  134.4 1.2 fusion.182
  136.1 0.1 copy.75
  136.2 6.1 %fusion.92 = f32[9,64,384]{2,1,0:T(8,128)S(1)} fusion(f32[64,3072]{1,0:T(8,128)S(1)} %get-tuple-element.230, f32[9,3072]{1,0:T(8,128)S(1)} %bitcast.243, s32[3072]{0:T(1024)S(1)} %get-tuple-element.219), kind=kOutput, calls=%fused_computation.160 | convolution fusion | flops 8156676096 | bytes 1794048 | tf_op jit(solution)/shard_map/che,le->chl/dot_general | solution.py:183
  142.3 1.7 copy.63
  144.0 4.3 %all-to-all-start.2 = ((f32[9,64,384]{2,0,1:T(8,128)}), f32[9,64,384]{2,0,1:T(8,128)S(1)}, u32[]{:S(2)}, u32[]{:S(2)}) async-start(f32[9,64,384]{2,0,1:T(8,128)} %copy.63), calls=%async_computation.2 | async-start | bytes 3145728 | tf_op jit(solution)/shard_map/all_to_all | solution.py:184
  148.3 0.6 copy.64
  148.9 21.0 %all-to-all-done.2 = f32[9,64,384]{2,0,1:T(8,128)S(1)} async-done(((f32[9,64,384]{2,0,1:T(8,128)}), f32[9,64,384]{2,0,1:T(8,128)S(1)}, u32[]{:S(2)}, u32[]{:S(2)}) %all-to-all-start.2) | async-done | bytes 884768 | tf_op jit(solution)/shard_map/all_to_all | solution.py:184
  170.0 0.6 slice.332
  170.6 0.6 slice.333
  171.2 0.6 slice.331
  (160 shorter events, 5.0 us)
Async XLA Ops:
  0.6 7.5 %copy-start = (f32[5,24576]{1,0:T(8,128)S(1)}, f32[5,24576]{1,0:T(8,128)}, u32[]{:S(2)}) copy-start(f32[5,24576]{1,0:T(8,128)} %param.11) | copy-start | bytes 1474564
  8.4 6.4 %copy-start.1 = (f32[4,256]{1,0:T(4,128)S(1)}, f32[4,256]{1,0:T(4,128)}, u32[]{:S(2)}) copy-start(f32[4,256]{1,0:T(4,128)} %constant.181.clone.1) | copy-start | bytes 12292
  14.8 24.8 %copy-start.2 = (f32[3,2,256]{2,1,0:T(2,128)S(1)}, f32[3,2,256]{2,1,0:T(2,128)}, u32[]{:S(2)}) copy-start(f32[3,2,256]{2,1,0:T(2,128)} %param.17) | copy-start | bytes 18436
  27.0 58.6 %copy-start.3 = (s32[2,64]{1,0:T(2,128)S(1)}, s32[2,64]{1,0:T(2,128)}, u32[]{:S(2)}) copy-start(s32[2,64]{1,0:T(2,128)} %param.16) | copy-start | bytes 1540
  29.8 55.7 %all-to-all-start = ((f32[64,4,256]{2,1,0:T(4,128)}), f32[64,4,256]{2,1,0:T(4,128)S(1)}, u32[]{:S(2)}, u32[]{:S(2)}) async-start(f32[64,4,256]{2,1,0:T(4,128)} %scatter_fusion), calls=%async_computation | async-start | bytes 524288 | tf_op jit(solution)/shard_map/all_to_all | solution.py:147
  92.1 18.9 %all-to-all-start.1 = ((f32[64,4,256]{2,1,0:T(4,128)}), f32[64,4,256]{2,1,0:T(4,128)S(1)}, u32[]{:S(2)}, u32[]{:S(2)}) async-start(f32[64,4,256]{2,1,0:T(4,128)} %copy.62), calls=%async_computation.1 | async-start | bytes 524288 | tf_op jit(solution)/shard_map/all_to_all | solution.py:158
  144.0 25.9 %all-to-all-start.2 = ((f32[9,64,384]{2,0,1:T(8,128)}), f32[9,64,384]{2,0,1:T(8,128)S(1)}, u32[]{:S(2)}, u32[]{:S(2)}) async-start(f32[9,64,384]{2,0,1:T(8,128)} %copy.63), calls=%async_computation.2 | async-start | bytes 3145728 | tf_op jit(solution)/shard_map/all_to_all | solution.py:184

commit v6 on v5

--- a/solution.py
+++ b/solution.py
@@ -134,21 +134,32 @@
     partial_value = lax.fori_loop(
         0, turn_count, forward_turn, jnp.broadcast_to(default, (slots_count, 4, pixels))
     )
-    home = lax.axis_index("dom")
-    cover_all = lax.all_gather(tile_ids.astype(jnp.float32), "dom", axis=0, tiled=False)
-    first_here = jnp.any(cover_all == (home * tiles_per).astype(jnp.float32), axis=1)
-    second_here = jnp.any(cover_all == (home * tiles_per + 1).astype(jnp.float32), axis=1)
     target = jnp.where(tile_ids >= 0, tile_ids // tiles_per, parts_count)
     dense = (
         jnp.broadcast_to(default, (parts_count, 4, pixels))
         .at[target]
         .set(partial_value, mode="drop")
     )
-    landed = lax.all_to_all(dense, "dom", split_axis=0, concat_axis=0, tiled=True)
+    offset = (
+        jnp.zeros((parts_count,), jnp.float32)
+        .at[target]
+        .set((tile_ids % tiles_per).astype(jnp.float32), mode="drop")
+    )
+    tag_width = 128
+    payload = jnp.concatenate(
+        [
+            dense.reshape(parts_count, 4 * pixels),
+            jnp.broadcast_to(offset[:, None], (parts_count, tag_width)),
+        ],
+        axis=1,
+    )
+    landed = lax.all_to_all(payload, "dom", split_axis=0, concat_axis=0, tiled=True)
+    second_here = landed[:, 4 * pixels] > 0.5
+    landed = landed[:, : 4 * pixels].reshape(parts_count, 4, pixels)
     blank = jnp.broadcast_to(default, landed.shape)
     arrived = jnp.stack(
         [
-            jnp.where(first_here[:, None, None], landed, blank),
+            jnp.where(second_here[:, None, None], blank, landed),
             jnp.where(second_here[:, None, None], landed, blank),
         ],
         axis=1,

time: 172 us -> 135 us (0.78)
  the two profiles are of different devices: /device:TPU:216 before, /device:TPU:16 now
where the time goes in v6:
time: 135 us
  waiting for transfers between devices  48.1 us (36%)
  matrix products  32 us (24%)
  starting transfers between devices  27.4 us (20%)
  local copies, waits for them, and re-layouts  14.1 us (10%)
  other arithmetic  10.4 us (8%)
  between operations  2.16 us (2%)
    all_to_all x1, waiting for transfers between devices, local(): lax.all_to_all(placed, 'tile', split_axis=1, concat_axis=1, tiled=True)  21 us
    all_to_all x1, starting transfers between devices, local(): lax.all_to_all(payload, 'dom', split_axis=0, concat_axis=0, tiled=True)  17.4 us
    all_to_all x1, waiting for transfers between devices, local(): lax.all_to_all(payload, 'dom', split_axis=0, concat_axis=0, tiled=True)  14.3 us
    all_to_all x1, waiting for transfers between devices, local(): lax.all_to_all(sent_back, 'dom', split_axis=0, concat_axis=0, tiled=True)  12.8 us
    dot_general x6, matrix products, render(): jnp.einsum('kpg,gh->kph', log_keep, ahead, precision=lax.Precision.HIGHEST)  12.5 us
    dot_general x6, matrix products, render(): jnp.einsum('kpg,ckg->kcp', weight, params[6:9], precision=lax.Precision.H...  6.42 us
    dot_general x1, matrix products, local(): jnp.einsum('chl,le->che', params.reshape(params.shape[0], hi_size, lo_siz...  6.15 us
    dot_general x1, matrix products, local(): jnp.einsum('che,le->chl', spread, lo_hot, precision=lax.Precision.HIGHEST)  6.08 us
  transfers between devices with their start and end apart: 3, of which 3 were waited for; matrix products, arithmetic and copies ran while one was open for 0% of the time, Pallas kernels for 0%

profile of v6, /device:TPU:16, one launch (start us, length us, event | category | flops | bytes accessed | tf_op | source)
XLA Modules:
  0.0 134.8 jit_solution(10136176140465368967)
XLA Ops:
  0.7 1.4 %fusion.135 = (s32[12]{0:T(128)S(1)}, f32[12]{0:T(128)S(1)}, s32[]{:T(128)}) fusion(s32[1,1,12]{2,1,0:T(1,128)} %param.14, s32[]{:T(128)S(6)} %mul.711), kind=kLoop, calls=%fused_computation.280 | loop fusion | flops 287 | bytes 152 | tf_op jit(solution)/shard_map/mul | solution.py:46
  2.7 0.7 fusion.139
  3.4 0.7 compare_and_fusion
  4.1 0.7 fusion.146
  4.8 0.7 add_select_fusion
  5.5 0.9 concatenate.41
  6.4 1.0 copy.102
  7.5 0.1 copy.101
  7.6 0.1 fusion.107
  7.7 6.1 %multiply_reduce_fusion.1 = f32[9,3072]{1,0:T(8,128)S(1)} fusion(f32[64,3072]{1,0:T(8,128)S(1)} %get-tuple-element.243, s32[3072]{0:T(1024)S(1)} %get-tuple-element.235, f32[3,64,384]{2,1,0:T(8,128)S(1)} %bitcast.249, f32[1,64,384]{2,1,0:T(8,128)S(1)} %concatenate.41, f32[5,64,384]{2,1,0:T(8,128)S(1)} %bitcast.247), kind=kOutput, calls=%fused_computation.163 | convolution fusion | flops 8158860288 | bytes 1794048 | tf_op jit(solution)/shard_map/chl,le->che/dot_general | solution.py:110
  14.0 8.1 %while.20 = (s32[]{:T(128)}, f32[12,4,256]{2,1,0:T(4,128)S(1)}, s32[]{:T(128)}, f32[9,12,256]{2,1,0:T(8,128)S(1)}, f32[12,256]{1,0:T(8,128)S(1)}, /*index=5*/f32...) while((s32[]{:T(128)}, f32[12,4,256]{2,1,0:T(4,128)S(1)}, ...), condition=%wide.region_4.5_spmd, body=%wide.region_2.4_spmd.sunk | while | flops 825316352 | bytes 2339135 | solution.py:134
  14.2 1.0 fusion.172
  15.2 1.8 %fusion.173 = f32[4,256,256]{2,1,0:T(8,128)S(1)} fusion(f32[4,256]{1,0:T(4,128)S(1)} %get-tuple-element.357, f32[4,256]{1,0:T(4,128)S(1)} %get-tuple-element.358, f32[4,256]{1,0:T(4,128)S(1)} %get-tuple-element.359, f32[4,256]{1,0:T(4,128)S(1)} %get-tuple-element.360, f32[4,256]{1,0:T(4,128)S(1)} %get-tuple-element.361, ...), kind=kOutput, calls=%fused_computation.10.clone.1 | convolution fusion | flops 812187648 | bytes 1081344 | tf_op jit(solution)/shard_map/while/body/kpg,gh->kph/dot_general | solution.py:34
  17.1 1.0 fusion.174
  18.2 1.0 fusion.172
  19.3 1.8 %fusion.173 = f32[4,256,256]{2,1,0:T(8,128)S(1)} fusion(f32[4,256]{1,0:T(4,128)S(1)} %get-tuple-element.357, f32[4,256]{1,0:T(4,128)S(1)} %get-tuple-element.358, f32[4,256]{1,0:T(4,128)S(1)} %get-tuple-element.359, f32[4,256]{1,0:T(4,128)S(1)} %get-tuple-element.360, f32[4,256]{1,0:T(4,128)S(1)} %get-tuple-element.361, ...), kind=kOutput, calls=%fused_computation.10.clone.1 | convolution fusion | flops 812187648 | bytes 1081344 | tf_op jit(solution)/shard_map/while/body/kpg,gh->kph/dot_general | solution.py:34
  21.1 1.0 fusion.174
  22.2 1.0 scatter_fusion
  23.2 0.6 scatter_custom_fusion.1
  23.9 0.9 all_to_all.14
  24.9 17.4 %all-to-all-start = ((f32[64,1,1152]{2,1,0:T(1,128)}), f32[64,1,1152]{2,1,0:T(1,128)S(1)}, u32[]{:S(2)}, u32[]{:S(2)}) async-start(f32[64,1,1152]{2,1,0:T(1,128)} %all_to_all.14), calls=%async_computation | async-start | bytes 589824 | tf_op jit(solution)/shard_map/all_to_all | solution.py:156
  42.3 14.3 %all-to-all-done = f32[64,1,1152]{2,1,0:T(1,128)S(1)} async-done(((f32[64,1,1152]{2,1,0:T(1,128)}), f32[64,1,1152]{2,1,0:T(1,128)S(1)}, u32[]{:S(2)}, u32[]{:S(2)}) %all-to-all-start) | async-done | bytes 294944 | tf_op jit(solution)/shard_map/all_to_all | solution.py:156
  56.6 0.1 fusion.125
  56.7 0.1 reshape.670
  56.9 0.1 copy_select_fusion.1
  57.0 0.5 fusion.109
  58.1 0.1 reduce_window.9
  58.3 0.1 slice.258
  58.5 0.1 slice.254
  58.6 0.1 slice.262
  59.0 0.1 slice.271
  59.1 0.1 slice.269
  59.2 0.1 slice.265
  60.2 0.1 slice.257
  60.3 0.1 slice.255
  61.5 0.1 pad.98
  61.6 0.1 pad.164
  61.8 0.2 slice.303
  62.1 0.4 convolution_bitcast_fusion
  62.6 0.9 copy.68
  63.4 5.7 %all-to-all-start.1 = ((f32[64,4,256]{2,1,0:T(4,128)}), f32[64,4,256]{2,1,0:T(4,128)S(1)}, u32[]{:S(2)}, u32[]{:S(2)}) async-start(f32[64,4,256]{2,1,0:T(4,128)} %copy.68), calls=%async_computation.1 | async-start | bytes 524288 | tf_op jit(solution)/shard_map/all_to_all | solution.py:169
  69.2 12.8 %all-to-all-done.1 = f32[64,4,256]{2,1,0:T(4,128)S(1)} async-done(((f32[64,4,256]{2,1,0:T(4,128)}), f32[64,4,256]{2,1,0:T(4,128)S(1)}, u32[]{:S(2)}, u32[]{:S(2)}) %all-to-all-start.1) | async-done | bytes 262176 | tf_op jit(solution)/shard_map/all_to_all | solution.py:169
  82.0 0.6 gather_fusion
  82.7 16.3 %while.21 = (s32[]{:T(128)}, f32[9,12,256]{2,1,0:T(8,128)S(1)}, s32[]{:T(128)}, f32[12,4,256]{2,1,0:T(4,128)S(1)}, f32[9,12,256]{2,1,0:T(8,128)S(1)}, /*index=5*...) while((s32[]{:T(128)}, f32[9,12,256]{2,1,0:T(8,128)S(1)}, ...), condition=%wide.region_18.19_spmd, body=%wide.region_10.18_spmd.sunk | while | flops 1655438336 | bytes 5755247 | solution.py:180
  82.8 1.0 log-plus-one_reduce_fusion.2
  83.9 1.1 fusion.181
  84.9 1.5 %convolution_exponential_fusion.3 = f32[4,256,256]{2,1,0:T(8,128)S(1)} fusion(f32[4,256]{1,0:T(4,128)S(1)} %get-tuple-element.375, f32[4,256]{1,0:T(4,128)S(1)} %get-tuple-element.372, f32[4,256]{1,0:T(4,128)S(1)} %get-tuple-element.373, f32[4,256]{1,0:T(4,128)S(1)} %get-tuple-element.376, f32[4,256]{1,0:T(4,128)S(1)} %get-tuple-element.374, ...), kind=kOutput, calls=%fused_computation.60.clone.1 | convolution fusion | flops 808779776 | bytes 1081344 | tf_op jit(solution)/shard_map/while/body/jvp(kpg,gh->kph)/dot_general | solution.py:34
  86.4 2.9 %fusion.182 = (f32[4,256]{1,0:T(4,128)S(1)}, f32[4,256]{1,0:T(4,128)S(1)}, f32[4,256]{1,0:T(4,128)S(1)}, f32[4,256]{1,0:T(4,128)S(1)}, f32[4,256]{1,0:T(4,128)S(1)}, /*index=5*/f32[4,256]{1,0:T(4,128)S(1)}) fusion(f32[4,256]{1,0:T(4,128)S(1)} %get-tuple-element.372, f32[4,256]{1,0:T(4,128)S(1)} %get-tuple-element.373, ...), kind=kOutput, calls=%fused_computation.73.clone.1 | convolution fusion | flops 820570112 | bytes 2158592 | tf_op jit(solution)/shard_map/while/body/transpose(jvp(kpg,gh->kph))/dot_general | solution.py:34
  89.3 1.2 fusion.185
  90.9 1.0 log-plus-one_reduce_fusion.2
  91.9 1.1 fusion.181
  93.0 1.5 %convolution_exponential_fusion.3 = f32[4,256,256]{2,1,0:T(8,128)S(1)} fusion(f32[4,256]{1,0:T(4,128)S(1)} %get-tuple-element.375, f32[4,256]{1,0:T(4,128)S(1)} %get-tuple-element.372, f32[4,256]{1,0:T(4,128)S(1)} %get-tuple-element.373, f32[4,256]{1,0:T(4,128)S(1)} %get-tuple-element.376, f32[4,256]{1,0:T(4,128)S(1)} %get-tuple-element.374, ...), kind=kOutput, calls=%fused_computation.60.clone.1 | convolution fusion | flops 808779776 | bytes 1081344 | tf_op jit(solution)/shard_map/while/body/jvp(kpg,gh->kph)/dot_general | solution.py:34
  94.4 2.9 %fusion.182 = (f32[4,256]{1,0:T(4,128)S(1)}, f32[4,256]{1,0:T(4,128)S(1)}, f32[4,256]{1,0:T(4,128)S(1)}, f32[4,256]{1,0:T(4,128)S(1)}, f32[4,256]{1,0:T(4,128)S(1)}, /*index=5*/f32[4,256]{1,0:T(4,128)S(1)}) fusion(f32[4,256]{1,0:T(4,128)S(1)} %get-tuple-element.372, f32[4,256]{1,0:T(4,128)S(1)} %get-tuple-element.373, ...), kind=kOutput, calls=%fused_computation.73.clone.1 | convolution fusion | flops 820570112 | bytes 2158592 | tf_op jit(solution)/shard_map/while/body/transpose(jvp(kpg,gh->kph))/dot_general | solution.py:34
  97.4 1.2 fusion.185
  99.0 0.1 copy.82
  99.2 6.1 %fusion.92 = f32[9,64,384]{2,1,0:T(8,128)S(1)} fusion(f32[64,3072]{1,0:T(8,128)S(1)} %get-tuple-element.244, f32[9,3072]{1,0:T(8,128)S(1)} %bitcast.250, s32[3072]{0:T(1024)S(1)} %get-tuple-element.232), kind=kOutput, calls=%fused_computation.161 | convolution fusion | flops 8156676096 | bytes 1794048 | tf_op jit(solution)/shard_map/che,le->chl/dot_general | solution.py:194
  105.3 1.7 %copy.69 = f32[9,64,384]{2,0,1:T(8,128)} copy(f32[9,64,384]{2,1,0:T(8,128)S(1)} %fusion.92) | data formatting | bytes 1769472 | tf_op jit(solution)/shard_map/che,le->chl/dot_general | solution.py:194
  107.0 4.3 %all-to-all-start.2 = ((f32[9,64,384]{2,0,1:T(8,128)}), f32[9,64,384]{2,0,1:T(8,128)S(1)}, u32[]{:S(2)}, u32[]{:S(2)}) async-start(f32[9,64,384]{2,0,1:T(8,128)} %copy.69), calls=%async_computation.2 | async-start | bytes 3145728 | tf_op jit(solution)/shard_map/all_to_all | solution.py:195
  111.2 0.6 copy.70
  111.8 21.0 %all-to-all-done.2 = f32[9,64,384]{2,0,1:T(8,128)S(1)} async-done(((f32[9,64,384]{2,0,1:T(8,128)}), f32[9,64,384]{2,0,1:T(8,128)S(1)}, u32[]{:S(2)}, u32[]{:S(2)}) %all-to-all-start.2) | async-done | bytes 884768 | tf_op jit(solution)/shard_map/all_to_all | solution.py:195
  132.8 0.1 reduce_sum.141
  132.9 0.6 slice.342
  133.5 0.6 slice.343
  134.2 0.6 slice.341
  (138 shorter events, 4.0 us)
Async XLA Ops:
  0.6 6.8 %copy-start = (f32[5,24576]{1,0:T(8,128)S(1)}, f32[5,24576]{1,0:T(8,128)}, u32[]{:S(2)}) copy-start(f32[5,24576]{1,0:T(8,128)} %param.11) | copy-start | bytes 1474564
  7.7 6.3 %copy-start.1 = (f32[4,256]{1,0:T(4,128)S(1)}, f32[4,256]{1,0:T(4,128)}, u32[]{:S(2)}) copy-start(f32[4,256]{1,0:T(4,128)} %constant.180.clone.1) | copy-start | bytes 12292
  22.1 20.1 %copy-start.2 = (f32[3,2,256]{2,1,0:T(2,128)S(1)}, f32[3,2,256]{2,1,0:T(2,128)}, u32[]{:S(2)}) copy-start(f32[3,2,256]{2,1,0:T(2,128)} %param.17) | copy-start | bytes 18436
  24.9 32.1 %copy-start.3 = (s32[2,64]{1,0:T(2,128)S(1)}, s32[2,64]{1,0:T(2,128)}, u32[]{:S(2)}) copy-start(s32[2,64]{1,0:T(2,128)} %param.16) | copy-start | bytes 1540
  24.9 31.7 %all-to-all-start = ((f32[64,1,1152]{2,1,0:T(1,128)}), f32[64,1,1152]{2,1,0:T(1,128)S(1)}, u32[]{:S(2)}, u32[]{:S(2)}) async-start(f32[64,1,1152]{2,1,0:T(1,128)} %all_to_all.14), calls=%async_computation | async-start | bytes 589824 | tf_op jit(solution)/shard_map/all_to_all | solution.py:156
  63.4 18.5 %all-to-all-start.1 = ((f32[64,4,256]{2,1,0:T(4,128)}), f32[64,4,256]{2,1,0:T(4,128)S(1)}, u32[]{:S(2)}, u32[]{:S(2)}) async-start(f32[64,4,256]{2,1,0:T(4,128)} %copy.68), calls=%async_computation.1 | async-start | bytes 524288 | tf_op jit(solution)/shard_map/all_to_all | solution.py:169
  107.0 25.8 %all-to-all-start.2 = ((f32[9,64,384]{2,0,1:T(8,128)}), f32[9,64,384]{2,0,1:T(8,128)S(1)}, u32[]{:S(2)}, u32[]{:S(2)}) async-start(f32[9,64,384]{2,0,1:T(8,128)} %copy.69), calls=%async_computation.2 | async-start | bytes 3145728 | tf_op jit(solution)/shard_map/all_to_all | solution.py:195

commit v7 on v6

--- a/solution.py
+++ b/solution.py
@@ -102,18 +102,18 @@
     safe_index = jnp.where(live_all, entries, 0).reshape(-1)
     hi_pick = (
         safe_index[None, None, :] // lo_size
-        == jnp.arange(hi_size, dtype=jnp.int32)[None, :, None]
+        == jnp.arange(hi_size, dtype=jnp.int32)[:, None, None]
     ).astype(jnp.float32)
     lo_pick = (
         safe_index[None, :] % lo_size == jnp.arange(lo_size, dtype=jnp.int32)[:, None]
     ).astype(jnp.float32)
     by_row = jnp.einsum(
-        "chl,le->che",
+        "chl,le->hce",
         params.reshape(params.shape[0], hi_size, lo_size),
         lo_pick,
         precision=lax.Precision.HIGHEST,
     )
-    chosen_all = jnp.sum(by_row * hi_pick, axis=1).reshape((params.shape[0],) + entries.shape)
+    chosen_all = jnp.sum(by_row * hi_pick, axis=0).reshape((params.shape[0],) + entries.shape)
     live_all_f = live_all.astype(jnp.float32)
 
     def gather_turn(first_row):

time: 135 us -> 136 us (level)
  the two profiles are of different devices: /device:TPU:16 before, /device:TPU:240 now
where the time goes in v7:
time: 136 us; the launch traced here: 135 us
  matrix products  41.6 us (31%)
  waiting for transfers between devices  40.8 us (30%)
  starting transfers between devices  23.1 us (17%)
  local copies, waits for them, and re-layouts  14.2 us (10%)
  other arithmetic  12.8 us (9%)
  between operations  2.16 us (2%)
    all_to_all x1, waiting for transfers between devices, local(): lax.all_to_all(placed, 'tile', split_axis=1, concat_axis=1, tiled=True)  21 us
    dot_general x9, matrix products, render(): jnp.einsum('kpg,gh->kph', log_keep, ahead, precision=lax.Precision.HIGHEST)  18.7 us
    all_to_all x1, waiting for transfers between devices, local(): lax.all_to_all(payload, 'dom', split_axis=0, concat_axis=0, tiled=True)  10.8 us
    dot_general x9, matrix products, render(): jnp.einsum('kpg,ckg->kcp', weight, params[6:9], precision=lax.Precision.H...  9.63 us
    all_to_all x1, starting transfers between devices, local(): lax.all_to_all(payload, 'dom', split_axis=0, concat_axis=0, tiled=True)  9.45 us
    all_to_all x1, starting transfers between devices, local(): lax.all_to_all(sent_back, 'dom', split_axis=0, concat_axis=0, tiled=True)  9.37 us
    all_to_all x1, waiting for transfers between devices, local(): lax.all_to_all(sent_back, 'dom', split_axis=0, concat_axis=0, tiled=True)  9.09 us
    dot_general x1, matrix products, local(): jnp.einsum('chl,le->hce', params.reshape(params.shape[0], hi_size, lo_siz...  6.22 us
  transfers between devices with their start and end apart: 3, of which 3 were waited for; matrix products, arithmetic and copies ran while one was open for 0% of the time, Pallas kernels for 0%

profile of v7, /device:TPU:240, one launch (start us, length us, event | category | flops | bytes accessed | tf_op | source)
XLA Modules:
  0.0 135.4 jit_solution(12182489142588650170)
XLA Ops:
  0.7 1.4 %fusion.136 = (s32[12]{0:T(128)S(1)}, f32[12]{0:T(128)S(1)}, s32[]{:T(128)}) fusion(s32[1,1,12]{2,1,0:T(1,128)} %param.14, s32[]{:T(128)S(6)} %mul.711), kind=kLoop, calls=%fused_computation.281 | loop fusion | flops 287 | bytes 152 | tf_op jit(solution)/shard_map/mul | solution.py:46
  2.7 0.7 fusion.140
  3.4 0.7 compare_and_fusion
  4.1 0.7 fusion.147
  4.8 0.7 add_select_fusion
  5.5 0.9 concatenate.41
  6.4 1.0 copy.102
  7.7 6.2 %fusion.92 = f32[9,3072]{1,0:T(8,128)S(1)} fusion(f32[64,3072]{1,0:T(8,128)S(1)} %get-tuple-element.243, s32[3072]{0:T(1024)S(1)} %get-tuple-element.235, f32[3,64,384]{2,1,0:T(8,128)S(1)} %bitcast.253, f32[1,64,384]{2,1,0:T(8,128)S(1)} %concatenate.41, f32[5,64,384]{2,1,0:T(8,128)S(1)} %bitcast.251), kind=kOutput, calls=%fused_computation.162 | convolution fusion | flops 8158860288 | bytes 1794048 | tf_op jit(solution)/shard_map/chl,le->hce/dot_general | solution.py:110
  14.1 12.2 %while.20 = (s32[]{:T(128)}, f32[12,4,256]{2,1,0:T(4,128)S(1)}, s32[]{:T(128)}, f32[9,12,256]{2,1,0:T(8,128)S(1)}, f32[12,256]{1,0:T(8,128)S(1)}, /*index=5*/f32...) while((s32[]{:T(128)}, f32[12,4,256]{2,1,0:T(4,128)S(1)}, ...), condition=%wide.region_4.5_spmd, body=%wide.region_2.4_spmd.sunk | while | flops 825316352 | bytes 2339135 | solution.py:134
  14.2 1.0 fusion.173
  15.3 1.8 %fusion.174 = f32[4,256,256]{2,1,0:T(8,128)S(1)} fusion(f32[4,256]{1,0:T(4,128)S(1)} %get-tuple-element.357, f32[4,256]{1,0:T(4,128)S(1)} %get-tuple-element.358, f32[4,256]{1,0:T(4,128)S(1)} %get-tuple-element.359, f32[4,256]{1,0:T(4,128)S(1)} %get-tuple-element.360, f32[4,256]{1,0:T(4,128)S(1)} %get-tuple-element.361, ...), kind=kOutput, calls=%fused_computation.10.clone.1 | convolution fusion | flops 812187648 | bytes 1081344 | tf_op jit(solution)/shard_map/while/body/kpg,gh->kph/dot_general | solution.py:34
  17.1 1.0 fusion.175
  18.3 1.0 fusion.173
  19.3 1.8 %fusion.174 = f32[4,256,256]{2,1,0:T(8,128)S(1)} fusion(f32[4,256]{1,0:T(4,128)S(1)} %get-tuple-element.357, f32[4,256]{1,0:T(4,128)S(1)} %get-tuple-element.358, f32[4,256]{1,0:T(4,128)S(1)} %get-tuple-element.359, f32[4,256]{1,0:T(4,128)S(1)} %get-tuple-element.360, f32[4,256]{1,0:T(4,128)S(1)} %get-tuple-element.361, ...), kind=kOutput, calls=%fused_computation.10.clone.1 | convolution fusion | flops 812187648 | bytes 1081344 | tf_op jit(solution)/shard_map/while/body/kpg,gh->kph/dot_general | solution.py:34
  21.2 1.0 fusion.175
  22.4 1.0 fusion.173
  23.4 1.8 %fusion.174 = f32[4,256,256]{2,1,0:T(8,128)S(1)} fusion(f32[4,256]{1,0:T(4,128)S(1)} %get-tuple-element.357, f32[4,256]{1,0:T(4,128)S(1)} %get-tuple-element.358, f32[4,256]{1,0:T(4,128)S(1)} %get-tuple-element.359, f32[4,256]{1,0:T(4,128)S(1)} %get-tuple-element.360, f32[4,256]{1,0:T(4,128)S(1)} %get-tuple-element.361, ...), kind=kOutput, calls=%fused_computation.10.clone.1 | convolution fusion | flops 812187648 | bytes 1081344 | tf_op jit(solution)/shard_map/while/body/kpg,gh->kph/dot_general | solution.py:34
  25.3 1.0 fusion.175
  26.3 1.0 scatter_fusion
  27.3 0.6 scatter_custom_fusion.1
  28.1 0.9 all_to_all.14
  29.0 9.5 %all-to-all-start = ((f32[64,1,1152]{2,1,0:T(1,128)}), f32[64,1,1152]{2,1,0:T(1,128)S(1)}, u32[]{:S(2)}, u32[]{:S(2)}) async-start(f32[64,1,1152]{2,1,0:T(1,128)} %all_to_all.14), calls=%async_computation | async-start | bytes 589824 | tf_op jit(solution)/shard_map/all_to_all | solution.py:156
  38.4 10.8 %all-to-all-done = f32[64,1,1152]{2,1,0:T(1,128)S(1)} async-done(((f32[64,1,1152]{2,1,0:T(1,128)}), f32[64,1,1152]{2,1,0:T(1,128)S(1)}, u32[]{:S(2)}, u32[]{:S(2)}) %all-to-all-start) | async-done | bytes 294944 | tf_op jit(solution)/shard_map/all_to_all | solution.py:156
  49.4 0.1 reshape.671
  49.5 0.1 copy_select_fusion.1
  49.6 0.5 fusion.110
  50.7 0.1 reduce_window.9
  51.0 0.1 slice.258
  51.1 0.1 slice.254
  51.2 0.1 slice.262
  52.9 0.1 slice.255
  54.1 0.1 pad.98
  54.2 0.1 pad.164
  54.4 0.2 slice.303
  54.7 0.4 convolution_bitcast_fusion
  55.2 0.9 copy.68
  56.1 9.4 %all-to-all-start.1 = ((f32[64,4,256]{2,1,0:T(4,128)}), f32[64,4,256]{2,1,0:T(4,128)S(1)}, u32[]{:S(2)}, u32[]{:S(2)}) async-start(f32[64,4,256]{2,1,0:T(4,128)} %copy.68), calls=%async_computation.1 | async-start | bytes 524288 | tf_op jit(solution)/shard_map/all_to_all | solution.py:169
  65.5 9.1 %all-to-all-done.1 = f32[64,4,256]{2,1,0:T(4,128)S(1)} async-done(((f32[64,4,256]{2,1,0:T(4,128)}), f32[64,4,256]{2,1,0:T(4,128)S(1)}, u32[]{:S(2)}, u32[]{:S(2)}) %all-to-all-start.1) | async-done | bytes 262176 | tf_op jit(solution)/shard_map/all_to_all | solution.py:169
  74.6 0.6 gather_fusion
  75.3 24.4 %while.21 = (s32[]{:T(128)}, f32[9,12,256]{2,1,0:T(8,128)S(1)}, s32[]{:T(128)}, f32[12,4,256]{2,1,0:T(4,128)S(1)}, f32[9,12,256]{2,1,0:T(8,128)S(1)}, /*index=5*...) while((s32[]{:T(128)}, f32[9,12,256]{2,1,0:T(8,128)S(1)}, ...), condition=%wide.region_18.19_spmd, body=%wide.region_10.18_spmd.sunk | while | flops 1655438336 | bytes 5755247 | solution.py:180
  75.4 1.0 log-plus-one_reduce_fusion.2
  76.5 1.1 fusion.182
  77.5 1.5 %convolution_exponential_fusion.3 = f32[4,256,256]{2,1,0:T(8,128)S(1)} fusion(f32[4,256]{1,0:T(4,128)S(1)} %get-tuple-element.375, f32[4,256]{1,0:T(4,128)S(1)} %get-tuple-element.372, f32[4,256]{1,0:T(4,128)S(1)} %get-tuple-element.373, f32[4,256]{1,0:T(4,128)S(1)} %get-tuple-element.376, f32[4,256]{1,0:T(4,128)S(1)} %get-tuple-element.374, ...), kind=kOutput, calls=%fused_computation.60.clone.1 | convolution fusion | flops 808779776 | bytes 1081344 | tf_op jit(solution)/shard_map/while/body/jvp(kpg,gh->kph)/dot_general | solution.py:34
  79.0 2.9 %fusion.183 = (f32[4,256]{1,0:T(4,128)S(1)}, f32[4,256]{1,0:T(4,128)S(1)}, f32[4,256]{1,0:T(4,128)S(1)}, f32[4,256]{1,0:T(4,128)S(1)}, f32[4,256]{1,0:T(4,128)S(1)}, /*index=5*/f32[4,256]{1,0:T(4,128)S(1)}) fusion(f32[4,256]{1,0:T(4,128)S(1)} %get-tuple-element.372, f32[4,256]{1,0:T(4,128)S(1)} %get-tuple-element.373, ...), kind=kOutput, calls=%fused_computation.73.clone.1 | convolution fusion | flops 820570112 | bytes 2158592 | tf_op jit(solution)/shard_map/while/body/transpose(jvp(kpg,gh->kph))/dot_general | solution.py:34
  82.0 1.2 fusion.186
  83.5 1.0 log-plus-one_reduce_fusion.2
  84.5 1.1 fusion.182
  85.6 1.5 %convolution_exponential_fusion.3 = f32[4,256,256]{2,1,0:T(8,128)S(1)} fusion(f32[4,256]{1,0:T(4,128)S(1)} %get-tuple-element.375, f32[4,256]{1,0:T(4,128)S(1)} %get-tuple-element.372, f32[4,256]{1,0:T(4,128)S(1)} %get-tuple-element.373, f32[4,256]{1,0:T(4,128)S(1)} %get-tuple-element.376, f32[4,256]{1,0:T(4,128)S(1)} %get-tuple-element.374, ...), kind=kOutput, calls=%fused_computation.60.clone.1 | convolution fusion | flops 808779776 | bytes 1081344 | tf_op jit(solution)/shard_map/while/body/jvp(kpg,gh->kph)/dot_general | solution.py:34
  87.0 2.9 %fusion.183 = (f32[4,256]{1,0:T(4,128)S(1)}, f32[4,256]{1,0:T(4,128)S(1)}, f32[4,256]{1,0:T(4,128)S(1)}, f32[4,256]{1,0:T(4,128)S(1)}, f32[4,256]{1,0:T(4,128)S(1)}, /*index=5*/f32[4,256]{1,0:T(4,128)S(1)}) fusion(f32[4,256]{1,0:T(4,128)S(1)} %get-tuple-element.372, f32[4,256]{1,0:T(4,128)S(1)} %get-tuple-element.373, ...), kind=kOutput, calls=%fused_computation.73.clone.1 | convolution fusion | flops 820570112 | bytes 2158592 | tf_op jit(solution)/shard_map/while/body/transpose(jvp(kpg,gh->kph))/dot_general | solution.py:34
  90.0 1.2 fusion.186
  91.5 1.0 log-plus-one_reduce_fusion.2
  92.6 1.1 fusion.182
  93.6 1.5 %convolution_exponential_fusion.3 = f32[4,256,256]{2,1,0:T(8,128)S(1)} fusion(f32[4,256]{1,0:T(4,128)S(1)} %get-tuple-element.375, f32[4,256]{1,0:T(4,128)S(1)} %get-tuple-element.372, f32[4,256]{1,0:T(4,128)S(1)} %get-tuple-element.373, f32[4,256]{1,0:T(4,128)S(1)} %get-tuple-element.376, f32[4,256]{1,0:T(4,128)S(1)} %get-tuple-element.374, ...), kind=kOutput, calls=%fused_computation.60.clone.1 | convolution fusion | flops 808779776 | bytes 1081344 | tf_op jit(solution)/shard_map/while/body/jvp(kpg,gh->kph)/dot_general | solution.py:34
  95.1 2.9 %fusion.183 = (f32[4,256]{1,0:T(4,128)S(1)}, f32[4,256]{1,0:T(4,128)S(1)}, f32[4,256]{1,0:T(4,128)S(1)}, f32[4,256]{1,0:T(4,128)S(1)}, f32[4,256]{1,0:T(4,128)S(1)}, /*index=5*/f32[4,256]{1,0:T(4,128)S(1)}) fusion(f32[4,256]{1,0:T(4,128)S(1)} %get-tuple-element.372, f32[4,256]{1,0:T(4,128)S(1)} %get-tuple-element.373, ...), kind=kOutput, calls=%fused_computation.73.clone.1 | convolution fusion | flops 820570112 | bytes 2158592 | tf_op jit(solution)/shard_map/while/body/transpose(jvp(kpg,gh->kph))/dot_general | solution.py:34
  98.0 1.2 fusion.186
  99.7 0.1 copy.82
  99.8 6.1 %fusion.93 = f32[9,64,384]{2,1,0:T(8,128)S(1)} fusion(f32[64,3072]{1,0:T(8,128)S(1)} %get-tuple-element.244, f32[9,3072]{1,0:T(8,128)S(1)} %bitcast.254, s32[3072]{0:T(1024)S(1)} %get-tuple-element.232), kind=kOutput, calls=%fused_computation.163 | convolution fusion | flops 8156676096 | bytes 1794048 | tf_op jit(solution)/shard_map/che,le->chl/dot_general | solution.py:194
  105.9 1.7 %copy.69 = f32[9,64,384]{2,0,1:T(8,128)} copy(f32[9,64,384]{2,1,0:T(8,128)S(1)} %fusion.93) | data formatting | bytes 1769472 | tf_op jit(solution)/shard_map/che,le->chl/dot_general | solution.py:194
  107.6 4.3 %all-to-all-start.2 = ((f32[9,64,384]{2,0,1:T(8,128)}), f32[9,64,384]{2,0,1:T(8,128)S(1)}, u32[]{:S(2)}, u32[]{:S(2)}) async-start(f32[9,64,384]{2,0,1:T(8,128)} %copy.69), calls=%async_computation.2 | async-start | bytes 3145728 | tf_op jit(solution)/shard_map/all_to_all | solution.py:195
  111.9 0.6 copy.70
  112.5 21.0 %all-to-all-done.2 = f32[9,64,384]{2,0,1:T(8,128)S(1)} async-done(((f32[9,64,384]{2,0,1:T(8,128)}), f32[9,64,384]{2,0,1:T(8,128)S(1)}, u32[]{:S(2)}, u32[]{:S(2)}) %all-to-all-start.2) | async-done | bytes 884768 | tf_op jit(solution)/shard_map/all_to_all | solution.py:195
  133.5 0.6 slice.342
  134.1 0.6 slice.343
  134.8 0.6 slice.341
  (165 shorter events, 5.3 us)
Async XLA Ops:
  0.6 6.8 %copy-start = (f32[5,24576]{1,0:T(8,128)S(1)}, f32[5,24576]{1,0:T(8,128)}, u32[]{:S(2)}) copy-start(f32[5,24576]{1,0:T(8,128)} %param.11) | copy-start | bytes 1474564
  7.7 6.4 %copy-start.1 = (f32[4,256]{1,0:T(4,128)S(1)}, f32[4,256]{1,0:T(4,128)}, u32[]{:S(2)}) copy-start(f32[4,256]{1,0:T(4,128)} %constant.180.clone.1) | copy-start | bytes 12292
  26.3 12.2 %copy-start.2 = (f32[3,2,256]{2,1,0:T(2,128)S(1)}, f32[3,2,256]{2,1,0:T(2,128)}, u32[]{:S(2)}) copy-start(f32[3,2,256]{2,1,0:T(2,128)} %param.17) | copy-start | bytes 18436
  29.0 20.7 %copy-start.3 = (s32[2,64]{1,0:T(2,128)S(1)}, s32[2,64]{1,0:T(2,128)}, u32[]{:S(2)}) copy-start(s32[2,64]{1,0:T(2,128)} %param.16) | copy-start | bytes 1540
  29.0 20.3 %all-to-all-start = ((f32[64,1,1152]{2,1,0:T(1,128)}), f32[64,1,1152]{2,1,0:T(1,128)S(1)}, u32[]{:S(2)}, u32[]{:S(2)}) async-start(f32[64,1,1152]{2,1,0:T(1,128)} %all_to_all.14), calls=%async_computation | async-start | bytes 589824 | tf_op jit(solution)/shard_map/all_to_all | solution.py:156
  56.1 18.5 %all-to-all-start.1 = ((f32[64,4,256]{2,1,0:T(4,128)}), f32[64,4,256]{2,1,0:T(4,128)S(1)}, u32[]{:S(2)}, u32[]{:S(2)}) async-start(f32[64,4,256]{2,1,0:T(4,128)} %copy.68), calls=%async_computation.1 | async-start | bytes 524288 | tf_op jit(solution)/shard_map/all_to_all | solution.py:169
  107.6 25.8 %all-to-all-start.2 = ((f32[9,64,384]{2,0,1:T(8,128)}), f32[9,64,384]{2,0,1:T(8,128)S(1)}, u32[]{:S(2)}, u32[]{:S(2)}) async-start(f32[9,64,384]{2,0,1:T(8,128)} %copy.69), calls=%async_computation.2 | async-start | bytes 3145728 | tf_op jit(solution)/shard_map/all_to_all | solution.py:195

commit v8 on v7

--- a/solution.py
+++ b/solution.py
@@ -56,19 +56,19 @@
     ordered = jnp.einsum("irk,kicp->ircp", ranks_onehot, arrived, precision=lax.Precision.HIGHEST)
     colour = ordered[:, :, :3]
     transmit = ordered[:, :, 3]
-    running = jnp.cumprod(transmit, axis=1)
-    prefix = jnp.concatenate([jnp.ones_like(running[:, :1]), running[:, :-1]], axis=1)
+    ahead = (
+        jnp.arange(parts_count, dtype=jnp.int32)[:, None]
+        < jnp.arange(parts_count, dtype=jnp.int32)[None, :]
+    ).astype(jnp.float32)
+    prefix = jnp.exp(
+        jnp.einsum("iqp,qr->irp", jnp.log(transmit), ahead, precision=lax.Precision.HIGHEST)
+    )
     rendered = jnp.sum(prefix[:, :, None, :] * colour, axis=1)
-
-    def compose(earlier, later):
-        return (earlier[0] * later[0], later[1] + later[0][:, :, None, :] * earlier[1])
-
-    flipped = lax.associative_scan(compose, (transmit[:, ::-1], colour[:, ::-1]), axis=1)
-    suffix = flipped[1][:, ::-1]
-    behind = jnp.concatenate([suffix[:, 1:], jnp.zeros_like(suffix[:, :1])], axis=1)
     upstream_cot = jnp.transpose(cotangent, (1, 0, 2))
     grad_colour = prefix[:, :, None, :] * upstream_cot[:, None]
-    grad_transmit = prefix * jnp.sum(upstream_cot[:, None] * behind, axis=2)
+    weighted = prefix * jnp.sum(upstream_cot[:, None] * colour, axis=2)
+    behind = jnp.einsum("iqp,rq->irp", weighted, ahead, precision=lax.Precision.HIGHEST)
+    grad_transmit = behind / transmit
     grad_ordered = jnp.concatenate([grad_colour, grad_transmit[:, :, None, :]], axis=2)
     upstream = jnp.einsum(
         "irk,ircp->kicp", ranks_onehot, grad_ordered, precision=lax.Precision.HIGHEST
@@ -191,7 +191,7 @@
     lo_hot = (lo_index[None, :] == jnp.arange(lo_size, dtype=jnp.int32)[:, None]).astype(
         jnp.float32
     )
-    placed = jnp.einsum("che,le->chl", spread, lo_hot, precision=lax.Precision.HIGHEST)
+    placed = jnp.einsum("che,le->chl", spread, lo_hot, precision=lax.Precision.HIGH)
     gathered = lax.all_to_all(placed, "tile", split_axis=1, concat_axis=1, tiled=True)
     total = jnp.sum(
         gathered.reshape(rows_count, groups_count, hi_size // groups_count, lo_size), axis=1

time: 136 us -> 136 us (level)
  the two profiles are of different devices: /device:TPU:240 before, /device:TPU:16 now
where the time goes in v8:
time: 136 us
  waiting for transfers between devices  48.1 us (35%)
  matrix products  39.9 us (29%)
  starting transfers between devices  22.5 us (17%)
  other arithmetic  12.1 us (9%)
  local copies, waits for them, and re-layouts  10.9 us (8%)
  between operations  1.66 us (1%)
    all_to_all x1, waiting for transfers between devices, local(): lax.all_to_all(placed, 'tile', split_axis=1, concat_axis=1, tiled=True)  21 us
    dot_general x9, matrix products, render(): jnp.einsum('kpg,gh->kph', log_keep, ahead, precision=lax.Precision.HIGHEST)  18.7 us
    all_to_all x1, waiting for transfers between devices, local(): lax.all_to_all(payload, 'dom', split_axis=0, concat_axis=0, tiled=True)  14.3 us
    all_to_all x1, waiting for transfers between devices, local(): lax.all_to_all(sent_back, 'dom', split_axis=0, concat_axis=0, tiled=True)  12.8 us
    all_to_all x1, starting transfers between devices, local(): lax.all_to_all(payload, 'dom', split_axis=0, concat_axis=0, tiled=True)  12.5 us
    dot_general x9, matrix products, render(): jnp.einsum('kpg,ckg->kcp', weight, params[6:9], precision=lax.Precision.H...  9.63 us
    dot_general x1, matrix products, local(): jnp.einsum('chl,le->hce', params.reshape(params.shape[0], hi_size, lo_siz...  6.22 us
    reduce_sum x6, other arithmetic, render(): transmit = jnp.exp(jnp.sum(log_keep, axis=2))  6.11 us
  transfers between devices with their start and end apart: 3, of which 3 were waited for; matrix products, arithmetic and copies ran while one was open for 0% of the time, Pallas kernels for 0%

profile of v8, /device:TPU:16, one launch (start us, length us, event | category | flops | bytes accessed | tf_op | source)
XLA Modules:
  0.0 135.8 jit_solution(17931611360987150856)
XLA Ops:
  0.7 1.4 %fusion.139 = (s32[12]{0:T(128)S(1)}, f32[12]{0:T(128)S(1)}, s32[]{:T(128)}) fusion(s32[1,1,12]{2,1,0:T(1,128)} %param.14, s32[]{:T(128)S(6)} %mul.602), kind=kLoop, calls=%fused_computation.262 | loop fusion | flops 287 | bytes 152 | tf_op jit(solution)/shard_map/mul | solution.py:46
  2.7 0.7 fusion.143
  3.4 0.7 compare_and_fusion
  4.1 0.7 fusion.150
  4.8 0.7 add_select_fusion
  5.5 0.9 concatenate.20
  6.4 1.0 copy.113
  7.5 0.1 copy.112
  7.6 0.1 fusion.111
  7.7 6.2 %fusion.92 = f32[9,3072]{1,0:T(8,128)S(1)} fusion(f32[64,3072]{1,0:T(8,128)S(1)} %get-tuple-element.239, s32[3072]{0:T(1024)S(1)} %get-tuple-element.233, f32[3,64,384]{2,1,0:T(8,128)S(1)} %bitcast.264, f32[1,64,384]{2,1,0:T(8,128)S(1)} %concatenate.20, f32[5,64,384]{2,1,0:T(8,128)S(1)} %bitcast.262), kind=kOutput, calls=%fused_computation.162 | convolution fusion | flops 8158860288 | bytes 1794048 | tf_op jit(solution)/shard_map/chl,le->hce/dot_general | solution.py:110
  14.1 12.2 %while.20 = (s32[]{:T(128)}, f32[12,4,256]{2,1,0:T(4,128)S(1)}, s32[]{:T(128)}, f32[9,12,256]{2,1,0:T(8,128)S(1)}, f32[12,256]{1,0:T(8,128)S(1)}, /*index=5*/f32...) while((s32[]{:T(128)}, f32[12,4,256]{2,1,0:T(4,128)S(1)}, ...), condition=%wide.region_4.5_spmd, body=%wide.region_2.4_spmd.sunk | while | flops 825316352 | bytes 2339135 | solution.py:134
  14.2 1.0 fusion.173
  15.3 1.8 %fusion.174 = f32[4,256,256]{2,1,0:T(8,128)S(1)} fusion(f32[4,256]{1,0:T(4,128)S(1)} %get-tuple-element.353, f32[4,256]{1,0:T(4,128)S(1)} %get-tuple-element.354, f32[4,256]{1,0:T(4,128)S(1)} %get-tuple-element.355, f32[4,256]{1,0:T(4,128)S(1)} %get-tuple-element.356, f32[4,256]{1,0:T(4,128)S(1)} %get-tuple-element.357, ...), kind=kOutput, calls=%fused_computation.10.clone.1 | convolution fusion | flops 812187648 | bytes 1081344 | tf_op jit(solution)/shard_map/while/body/kpg,gh->kph/dot_general | solution.py:34
  17.1 1.0 fusion.175
  18.3 1.0 fusion.173
  19.3 1.8 %fusion.174 = f32[4,256,256]{2,1,0:T(8,128)S(1)} fusion(f32[4,256]{1,0:T(4,128)S(1)} %get-tuple-element.353, f32[4,256]{1,0:T(4,128)S(1)} %get-tuple-element.354, f32[4,256]{1,0:T(4,128)S(1)} %get-tuple-element.355, f32[4,256]{1,0:T(4,128)S(1)} %get-tuple-element.356, f32[4,256]{1,0:T(4,128)S(1)} %get-tuple-element.357, ...), kind=kOutput, calls=%fused_computation.10.clone.1 | convolution fusion | flops 812187648 | bytes 1081344 | tf_op jit(solution)/shard_map/while/body/kpg,gh->kph/dot_general | solution.py:34
  21.2 1.0 fusion.175
  22.4 1.0 fusion.173
  23.4 1.8 %fusion.174 = f32[4,256,256]{2,1,0:T(8,128)S(1)} fusion(f32[4,256]{1,0:T(4,128)S(1)} %get-tuple-element.353, f32[4,256]{1,0:T(4,128)S(1)} %get-tuple-element.354, f32[4,256]{1,0:T(4,128)S(1)} %get-tuple-element.355, f32[4,256]{1,0:T(4,128)S(1)} %get-tuple-element.356, f32[4,256]{1,0:T(4,128)S(1)} %get-tuple-element.357, ...), kind=kOutput, calls=%fused_computation.10.clone.1 | convolution fusion | flops 812187648 | bytes 1081344 | tf_op jit(solution)/shard_map/while/body/kpg,gh->kph/dot_general | solution.py:34
  25.3 1.0 fusion.175
  26.3 1.0 scatter_fusion
  27.3 0.6 scatter_custom_fusion.1
  28.1 0.9 all_to_all.14
  29.0 12.5 %all-to-all-start = ((f32[64,1,1152]{2,1,0:T(1,128)}), f32[64,1,1152]{2,1,0:T(1,128)S(1)}, u32[]{:S(2)}, u32[]{:S(2)}) async-start(f32[64,1,1152]{2,1,0:T(1,128)} %all_to_all.14), calls=%async_computation | async-start | bytes 589824 | tf_op jit(solution)/shard_map/all_to_all | solution.py:156
  41.5 14.3 %all-to-all-done = f32[64,1,1152]{2,1,0:T(1,128)S(1)} async-done(((f32[64,1,1152]{2,1,0:T(1,128)}), f32[64,1,1152]{2,1,0:T(1,128)S(1)}, u32[]{:S(2)}, u32[]{:S(2)}) %all-to-all-start) | async-done | bytes 294944 | tf_op jit(solution)/shard_map/all_to_all | solution.py:156
  55.9 0.1 fusion.131
  56.0 0.1 reshape.656
  56.2 0.1 copy_select_fusion.1
  56.3 0.5 fusion.113
  56.8 0.3 fusion.105
  57.0 0.1 multiply_reduce_fusion.1
  57.1 0.2 fusion.104
  57.4 0.4 convolution_bitcast_fusion
  57.8 0.1 fusion.120
  57.9 0.9 copy.80
  58.8 5.7 %all-to-all-start.1 = ((f32[64,4,256]{2,1,0:T(4,128)}), f32[64,4,256]{2,1,0:T(4,128)S(1)}, u32[]{:S(2)}, u32[]{:S(2)}) async-start(f32[64,4,256]{2,1,0:T(4,128)} %copy.80), calls=%async_computation.1 | async-start | bytes 524288 | tf_op jit(solution)/shard_map/all_to_all | solution.py:169
  64.5 12.8 %all-to-all-done.1 = f32[64,4,256]{2,1,0:T(4,128)S(1)} async-done(((f32[64,4,256]{2,1,0:T(4,128)}), f32[64,4,256]{2,1,0:T(4,128)S(1)}, u32[]{:S(2)}, u32[]{:S(2)}) %all-to-all-start.1) | async-done | bytes 262176 | tf_op jit(solution)/shard_map/all_to_all | solution.py:169
  77.3 0.6 gather_fusion
  78.0 24.2 %while.21 = (s32[]{:T(128)}, f32[9,12,256]{2,1,0:T(8,128)S(1)}, s32[]{:T(128)}, f32[12,4,256]{2,1,0:T(4,128)S(1)}, f32[9,12,256]{2,1,0:T(8,128)S(1)}, /*index=5*...) while((s32[]{:T(128)}, f32[9,12,256]{2,1,0:T(8,128)S(1)}, ...), condition=%wide.region_17.18_spmd, body=%wide.region_9.17_spmd.sunk | while | flops 1655438336 | bytes 5755247 | solution.py:180
  78.2 1.0 log-plus-one_reduce_fusion.2
  79.2 1.1 fusion.182
  80.3 1.5 %convolution_exponential_fusion.4 = f32[4,256,256]{2,1,0:T(8,128)S(1)} fusion(f32[4,256]{1,0:T(4,128)S(1)} %get-tuple-element.371, f32[4,256]{1,0:T(4,128)S(1)} %get-tuple-element.368, f32[4,256]{1,0:T(4,128)S(1)} %get-tuple-element.369, f32[4,256]{1,0:T(4,128)S(1)} %get-tuple-element.372, f32[4,256]{1,0:T(4,128)S(1)} %get-tuple-element.370, ...), kind=kOutput, calls=%fused_computation.60.clone.1 | convolution fusion | flops 808779776 | bytes 1081344 | tf_op jit(solution)/shard_map/while/body/jvp(kpg,gh->kph)/dot_general | solution.py:34
  81.7 2.9 %fusion.183 = (f32[4,256]{1,0:T(4,128)S(1)}, f32[4,256]{1,0:T(4,128)S(1)}, f32[4,256]{1,0:T(4,128)S(1)}, f32[4,256]{1,0:T(4,128)S(1)}, f32[4,256]{1,0:T(4,128)S(1)}, /*index=5*/f32[4,256]{1,0:T(4,128)S(1)}) fusion(f32[4,256]{1,0:T(4,128)S(1)} %get-tuple-element.368, f32[4,256]{1,0:T(4,128)S(1)} %get-tuple-element.369, ...), kind=kOutput, calls=%fused_computation.73.clone.1 | convolution fusion | flops 820570112 | bytes 2158592 | tf_op jit(solution)/shard_map/while/body/transpose(jvp(kpg,gh->kph))/dot_general | solution.py:34
  84.7 1.2 fusion.186
  86.2 1.0 log-plus-one_reduce_fusion.2
  87.2 1.1 fusion.182
  88.3 1.5 %convolution_exponential_fusion.4 = f32[4,256,256]{2,1,0:T(8,128)S(1)} fusion(f32[4,256]{1,0:T(4,128)S(1)} %get-tuple-element.371, f32[4,256]{1,0:T(4,128)S(1)} %get-tuple-element.368, f32[4,256]{1,0:T(4,128)S(1)} %get-tuple-element.369, f32[4,256]{1,0:T(4,128)S(1)} %get-tuple-element.372, f32[4,256]{1,0:T(4,128)S(1)} %get-tuple-element.370, ...), kind=kOutput, calls=%fused_computation.60.clone.1 | convolution fusion | flops 808779776 | bytes 1081344 | tf_op jit(solution)/shard_map/while/body/jvp(kpg,gh->kph)/dot_general | solution.py:34
  89.8 2.9 %fusion.183 = (f32[4,256]{1,0:T(4,128)S(1)}, f32[4,256]{1,0:T(4,128)S(1)}, f32[4,256]{1,0:T(4,128)S(1)}, f32[4,256]{1,0:T(4,128)S(1)}, f32[4,256]{1,0:T(4,128)S(1)}, /*index=5*/f32[4,256]{1,0:T(4,128)S(1)}) fusion(f32[4,256]{1,0:T(4,128)S(1)} %get-tuple-element.368, f32[4,256]{1,0:T(4,128)S(1)} %get-tuple-element.369, ...), kind=kOutput, calls=%fused_computation.73.clone.1 | convolution fusion | flops 820570112 | bytes 2158592 | tf_op jit(solution)/shard_map/while/body/transpose(jvp(kpg,gh->kph))/dot_general | solution.py:34
  92.7 1.2 fusion.186
  94.3 1.0 log-plus-one_reduce_fusion.2
  95.3 1.1 fusion.182
  96.4 1.5 %convolution_exponential_fusion.4 = f32[4,256,256]{2,1,0:T(8,128)S(1)} fusion(f32[4,256]{1,0:T(4,128)S(1)} %get-tuple-element.371, f32[4,256]{1,0:T(4,128)S(1)} %get-tuple-element.368, f32[4,256]{1,0:T(4,128)S(1)} %get-tuple-element.369, f32[4,256]{1,0:T(4,128)S(1)} %get-tuple-element.372, f32[4,256]{1,0:T(4,128)S(1)} %get-tuple-element.370, ...), kind=kOutput, calls=%fused_computation.60.clone.1 | convolution fusion | flops 808779776 | bytes 1081344 | tf_op jit(solution)/shard_map/while/body/jvp(kpg,gh->kph)/dot_general | solution.py:34
  97.8 2.9 %fusion.183 = (f32[4,256]{1,0:T(4,128)S(1)}, f32[4,256]{1,0:T(4,128)S(1)}, f32[4,256]{1,0:T(4,128)S(1)}, f32[4,256]{1,0:T(4,128)S(1)}, f32[4,256]{1,0:T(4,128)S(1)}, /*index=5*/f32[4,256]{1,0:T(4,128)S(1)}) fusion(f32[4,256]{1,0:T(4,128)S(1)} %get-tuple-element.368, f32[4,256]{1,0:T(4,128)S(1)} %get-tuple-element.369, ...), kind=kOutput, calls=%fused_computation.73.clone.1 | convolution fusion | flops 820570112 | bytes 2158592 | tf_op jit(solution)/shard_map/while/body/transpose(jvp(kpg,gh->kph))/dot_general | solution.py:34
  100.8 1.2 fusion.186
  102.2 0.1 copy.95
  102.3 3.9 %fusion.93 = f32[9,64,384]{2,1,0:T(8,128)S(1)} fusion(f32[64,3072]{1,0:T(8,128)S(1)} %get-tuple-element.240, f32[9,3072]{1,0:T(8,128)S(1)} %bitcast.265, s32[3072]{0:T(1024)S(1)} %get-tuple-element.230), kind=kOutput, calls=%fused_computation.163 | convolution fusion | flops 4079812608 | bytes 1794048 | tf_op jit(solution)/shard_map/che,le->chl/dot_general | solution.py:194
  106.2 1.7 %copy.81 = f32[9,64,384]{2,0,1:T(8,128)} copy(f32[9,64,384]{2,1,0:T(8,128)S(1)} %fusion.93) | data formatting | bytes 1769472 | tf_op jit(solution)/shard_map/che,le->chl/dot_general | solution.py:194
  107.9 4.3 %all-to-all-start.2 = ((f32[9,64,384]{2,0,1:T(8,128)}), f32[9,64,384]{2,0,1:T(8,128)S(1)}, u32[]{:S(2)}, u32[]{:S(2)}) async-start(f32[9,64,384]{2,0,1:T(8,128)} %copy.81), calls=%async_computation.2 | async-start | bytes 3145728 | tf_op jit(solution)/shard_map/all_to_all | solution.py:195
  112.2 0.6 copy.82
  112.8 21.0 %all-to-all-done.2 = f32[9,64,384]{2,0,1:T(8,128)S(1)} async-done(((f32[9,64,384]{2,0,1:T(8,128)}), f32[9,64,384]{2,0,1:T(8,128)S(1)}, u32[]{:S(2)}, u32[]{:S(2)}) %all-to-all-start.2) | async-done | bytes 884768 | tf_op jit(solution)/shard_map/all_to_all | solution.py:195
  133.8 0.1 reduce_sum.141
  133.9 0.6 slice.104
  134.5 0.6 slice.105
  135.1 0.6 slice.103
  (83 shorter events, 1.8 us)
Async XLA Ops:
  0.6 6.8 %copy-start = (f32[5,24576]{1,0:T(8,128)S(1)}, f32[5,24576]{1,0:T(8,128)}, u32[]{:S(2)}) copy-start(f32[5,24576]{1,0:T(8,128)} %param.11) | copy-start | bytes 1474564
  7.7 6.4 %copy-start.1 = (f32[4,256]{1,0:T(4,128)S(1)}, f32[4,256]{1,0:T(4,128)}, u32[]{:S(2)}) copy-start(f32[4,256]{1,0:T(4,128)} %constant.175.clone.1) | copy-start | bytes 12292
  26.3 15.3 %copy-start.2 = (f32[3,2,256]{2,1,0:T(2,128)S(1)}, f32[3,2,256]{2,1,0:T(2,128)}, u32[]{:S(2)}) copy-start(f32[3,2,256]{2,1,0:T(2,128)} %param.17) | copy-start | bytes 18436
  29.0 27.3 %copy-start.3 = (s32[2,64]{1,0:T(2,128)S(1)}, s32[2,64]{1,0:T(2,128)}, u32[]{:S(2)}) copy-start(s32[2,64]{1,0:T(2,128)} %param.16) | copy-start | bytes 1540
  29.0 26.9 %all-to-all-start = ((f32[64,1,1152]{2,1,0:T(1,128)}), f32[64,1,1152]{2,1,0:T(1,128)S(1)}, u32[]{:S(2)}, u32[]{:S(2)}) async-start(f32[64,1,1152]{2,1,0:T(1,128)} %all_to_all.14), calls=%async_computation | async-start | bytes 589824 | tf_op jit(solution)/shard_map/all_to_all | solution.py:156
  58.8 18.5 %all-to-all-start.1 = ((f32[64,4,256]{2,1,0:T(4,128)}), f32[64,4,256]{2,1,0:T(4,128)S(1)}, u32[]{:S(2)}, u32[]{:S(2)}) async-start(f32[64,4,256]{2,1,0:T(4,128)} %copy.80), calls=%async_computation.1 | async-start | bytes 524288 | tf_op jit(solution)/shard_map/all_to_all | solution.py:169
  107.9 25.8 %all-to-all-start.2 = ((f32[9,64,384]{2,0,1:T(8,128)}), f32[9,64,384]{2,0,1:T(8,128)S(1)}, u32[]{:S(2)}, u32[]{:S(2)}) async-start(f32[9,64,384]{2,0,1:T(8,128)} %copy.81), calls=%async_computation.2 | async-start | bytes 3145728 | tf_op jit(solution)/shard_map/all_to_all | solution.py:195

commit v9 on v8

--- a/solution.py
+++ b/solution.py
@@ -135,23 +135,26 @@
         0, turn_count, forward_turn, jnp.broadcast_to(default, (slots_count, 4, pixels))
     )
     target = jnp.where(tile_ids >= 0, tile_ids // tiles_per, parts_count)
-    dense = (
-        jnp.broadcast_to(default, (parts_count, 4, pixels))
-        .at[target]
-        .set(partial_value, mode="drop")
-    )
-    offset = (
-        jnp.zeros((parts_count,), jnp.float32)
-        .at[target]
-        .set((tile_ids % tiles_per).astype(jnp.float32), mode="drop")
-    )
     tag_width = 128
-    payload = jnp.concatenate(
+    rows_out = jnp.concatenate(
         [
-            dense.reshape(parts_count, 4 * pixels),
-            jnp.broadcast_to(offset[:, None], (parts_count, tag_width)),
+            partial_value.reshape(slots_count, 4 * pixels),
+            jnp.broadcast_to(
+                (tile_ids % tiles_per).astype(jnp.float32)[:, None], (slots_count, tag_width)
+            ),
         ],
         axis=1,
+    )
+    route = (
+        target[None, :] == jnp.arange(parts_count, dtype=jnp.int32)[:, None]
+    ).astype(jnp.float32)
+    unrouted = 1.0 - jnp.sum(route, axis=1)
+    blank_row = jnp.concatenate(
+        [default.reshape(4 * pixels), jnp.zeros((tag_width,), jnp.float32)], axis=0
+    )
+    payload = (
+        jnp.einsum("ds,sz->dz", route, rows_out, precision=lax.Precision.HIGHEST)
+        + unrouted[:, None] * blank_row[None, :]
     )
     landed = lax.all_to_all(payload, "dom", split_axis=0, concat_axis=0, tiled=True)
     second_here = landed[:, 4 * pixels] > 0.5

time: 136 us -> 128 us (0.941)
  the two profiles are of different devices: /device:TPU:16 before, /device:TPU:264 now
where the time goes in v9:
time: 128 us; the launch traced here: 127 us
  waiting for transfers between devices  41 us (32%)
  matrix products  40.3 us (31%)
  starting transfers between devices  22.7 us (18%)
  other arithmetic  11.5 us (9%)
  local copies, waits for them, and re-layouts  9.42 us (7%)
  between operations  1.67 us (1%)
    all_to_all x1, waiting for transfers between devices, local(): lax.all_to_all(placed, 'tile', split_axis=1, concat_axis=1, tiled=True)  21 us
    dot_general x9, matrix products, render(): jnp.einsum('kpg,gh->kph', log_keep, ahead, precision=lax.Precision.HIGHEST)  18.8 us
    all_to_all x1, waiting for transfers between devices, local(): lax.all_to_all(payload, 'dom', split_axis=0, concat_axis=0, tiled=True)  10.9 us
    dot_general x9, matrix products, render(): jnp.einsum('kpg,ckg->kcp', weight, params[6:9], precision=lax.Precision.H...  9.63 us
    all_to_all x1, starting transfers between devices, local(): lax.all_to_all(sent_back, 'dom', split_axis=0, concat_axis=0, tiled=True)  9.24 us
    all_to_all x1, waiting for transfers between devices, local(): lax.all_to_all(sent_back, 'dom', split_axis=0, concat_axis=0, tiled=True)  9.18 us
    all_to_all x1, starting transfers between devices, local(): lax.all_to_all(payload, 'dom', split_axis=0, concat_axis=0, tiled=True)  9.11 us
    dot_general x1, matrix products, local(): jnp.einsum('chl,le->hce', params.reshape(params.shape[0], hi_size, lo_siz...  6.22 us
  transfers between devices with their start and end apart: 3, of which 3 were waited for; matrix products, arithmetic and copies ran while one was open for 0% of the time, Pallas kernels for 0%

profile of v9, /device:TPU:264, one launch (start us, length us, event | category | flops | bytes accessed | tf_op | source)
XLA Modules:
  0.0 127.3 jit_solution(14453939369667779178)
XLA Ops:
  0.7 0.7 compare_and_fusion
  1.4 1.3 %fusion.144 = (s32[12]{0:T(128)S(1)}, f32[12]{0:T(128)S(1)}, s32[]{:T(128)}, s32[12]{0:T(128)S(1)}) fusion(s32[1,1,12]{2,1,0:T(1,128)} %param.14, s32[]{:T(128)S(6)} %mul.615), kind=kLoop, calls=%fused_computation.264 | loop fusion | flops 395 | bytes 200 | tf_op jit(solution)/shard_map/mul | solution.py:46
  3.4 0.1 convert_reduce_fusion
  3.5 0.7 fusion.152
  4.2 0.7 add_select_fusion
  4.9 0.9 concatenate.20
  5.9 1.0 copy.134
  6.9 0.1 copy.133
  7.0 0.1 fusion.112
  7.1 6.2 %fusion.92 = f32[9,3072]{1,0:T(8,128)S(1)} fusion(f32[64,3072]{1,0:T(8,128)S(1)} %get-tuple-element.261, s32[3072]{0:T(1024)S(1)} %get-tuple-element.256, f32[3,64,384]{2,1,0:T(8,128)S(1)} %bitcast.267, f32[1,64,384]{2,1,0:T(8,128)S(1)} %concatenate.20, f32[5,64,384]{2,1,0:T(8,128)S(1)} %bitcast.265), kind=kOutput, calls=%fused_computation.160 | convolution fusion | flops 8158860288 | bytes 1794048 | tf_op jit(solution)/shard_map/chl,le->hce/dot_general | solution.py:110
  13.5 12.2 %while.20 = (s32[]{:T(128)}, f32[12,4,256]{2,1,0:T(4,128)S(1)}, s32[]{:T(128)}, f32[9,12,256]{2,1,0:T(8,128)S(1)}, f32[12,256]{1,0:T(8,128)S(1)}, /*index=5*/f32...) while((s32[]{:T(128)}, f32[12,4,256]{2,1,0:T(4,128)S(1)}, ...), condition=%wide.region_4.5_spmd, body=%wide.region_2.4_spmd.sunk | while | flops 825316352 | bytes 2339135 | solution.py:134
  13.7 1.0 fusion.175
  14.7 1.9 %fusion.176 = f32[4,256,256]{2,1,0:T(8,128)S(1)} fusion(f32[4,256]{1,0:T(4,128)S(1)} %get-tuple-element.375, f32[4,256]{1,0:T(4,128)S(1)} %get-tuple-element.376, f32[4,256]{1,0:T(4,128)S(1)} %get-tuple-element.377, f32[4,256]{1,0:T(4,128)S(1)} %get-tuple-element.378, f32[4,256]{1,0:T(4,128)S(1)} %get-tuple-element.379, ...), kind=kOutput, calls=%fused_computation.8.clone.1 | convolution fusion | flops 812187648 | bytes 1081344 | tf_op jit(solution)/shard_map/while/body/kpg,gh->kph/dot_general | solution.py:34
  16.6 1.0 fusion.177
  17.7 1.0 fusion.175
  18.8 1.9 %fusion.176 = f32[4,256,256]{2,1,0:T(8,128)S(1)} fusion(f32[4,256]{1,0:T(4,128)S(1)} %get-tuple-element.375, f32[4,256]{1,0:T(4,128)S(1)} %get-tuple-element.376, f32[4,256]{1,0:T(4,128)S(1)} %get-tuple-element.377, f32[4,256]{1,0:T(4,128)S(1)} %get-tuple-element.378, f32[4,256]{1,0:T(4,128)S(1)} %get-tuple-element.379, ...), kind=kOutput, calls=%fused_computation.8.clone.1 | convolution fusion | flops 812187648 | bytes 1081344 | tf_op jit(solution)/shard_map/while/body/kpg,gh->kph/dot_general | solution.py:34
  20.6 1.0 fusion.177
  21.8 1.0 fusion.175
  22.8 1.9 %fusion.176 = f32[4,256,256]{2,1,0:T(8,128)S(1)} fusion(f32[4,256]{1,0:T(4,128)S(1)} %get-tuple-element.375, f32[4,256]{1,0:T(4,128)S(1)} %get-tuple-element.376, f32[4,256]{1,0:T(4,128)S(1)} %get-tuple-element.377, f32[4,256]{1,0:T(4,128)S(1)} %get-tuple-element.378, f32[4,256]{1,0:T(4,128)S(1)} %get-tuple-element.379, ...), kind=kOutput, calls=%fused_computation.8.clone.1 | convolution fusion | flops 812187648 | bytes 1081344 | tf_op jit(solution)/shard_map/while/body/kpg,gh->kph/dot_general | solution.py:34
  24.7 1.0 fusion.177
  25.8 0.4 fusion.103
  26.2 1.0 copy.94
  27.3 9.1 %all-to-all-start = ((f32[64,1,1152]{2,1,0:T(1,128)}), f32[64,1,1152]{2,1,0:T(1,128)S(1)}, u32[]{:S(2)}, u32[]{:S(2)}) async-start(f32[64,1,1152]{2,1,0:T(1,128)} %copy.94), calls=%async_computation | async-start | bytes 589824 | tf_op jit(solution)/shard_map/all_to_all | solution.py:159
  36.4 10.9 %all-to-all-done = f32[64,1,1152]{2,1,0:T(1,128)S(1)} async-done(((f32[64,1,1152]{2,1,0:T(1,128)}), f32[64,1,1152]{2,1,0:T(1,128)S(1)}, u32[]{:S(2)}, u32[]{:S(2)}) %all-to-all-start) | async-done | bytes 294944 | tf_op jit(solution)/shard_map/all_to_all | solution.py:159
  47.3 0.1 fusion.135
  47.5 0.1 reshape.634
  47.6 0.1 copy_select_fusion.1
  47.7 0.5 fusion.114
  48.2 0.3 fusion.106
  48.5 0.1 multiply_reduce_fusion.1
  48.6 0.2 fusion.105
  48.8 0.4 convolution_bitcast_fusion
  49.2 0.1 fusion.121
  49.3 0.9 copy.101
  50.2 9.2 %all-to-all-start.1 = ((f32[64,4,256]{2,1,0:T(4,128)}), f32[64,4,256]{2,1,0:T(4,128)S(1)}, u32[]{:S(2)}, u32[]{:S(2)}) async-start(f32[64,4,256]{2,1,0:T(4,128)} %copy.101), calls=%async_computation.1 | async-start | bytes 524288 | tf_op jit(solution)/shard_map/all_to_all | solution.py:172
  59.5 9.2 %all-to-all-done.1 = f32[64,4,256]{2,1,0:T(4,128)S(1)} async-done(((f32[64,4,256]{2,1,0:T(4,128)}), f32[64,4,256]{2,1,0:T(4,128)S(1)}, u32[]{:S(2)}, u32[]{:S(2)}) %all-to-all-start.1) | async-done | bytes 262176 | tf_op jit(solution)/shard_map/all_to_all | solution.py:172
  68.6 0.6 gather_fusion
  69.2 0.1 broadcast_select_fusion.1
  69.3 24.4 %while.21 = (s32[]{:T(128)}, f32[9,12,256]{2,1,0:T(8,128)S(1)}, s32[]{:T(128)}, f32[12,4,256]{2,1,0:T(4,128)S(1)}, f32[9,12,256]{2,1,0:T(8,128)S(1)}, /*index=5*...) while((s32[]{:T(128)}, f32[9,12,256]{2,1,0:T(8,128)S(1)}, ...), condition=%wide.region_16.17_spmd, body=%wide.region_8.16_spmd.sunk | while | flops 1655438336 | bytes 5755247 | solution.py:183
  69.7 1.0 log-plus-one_reduce_fusion.2
  70.7 1.1 fusion.184
  71.8 1.5 %convolution_exponential_fusion.4 = f32[4,256,256]{2,1,0:T(8,128)S(1)} fusion(f32[4,256]{1,0:T(4,128)S(1)} %get-tuple-element.393, f32[4,256]{1,0:T(4,128)S(1)} %get-tuple-element.390, f32[4,256]{1,0:T(4,128)S(1)} %get-tuple-element.391, f32[4,256]{1,0:T(4,128)S(1)} %get-tuple-element.394, f32[4,256]{1,0:T(4,128)S(1)} %get-tuple-element.392, ...), kind=kOutput, calls=%fused_computation.58.clone.1 | convolution fusion | flops 808779776 | bytes 1081344 | tf_op jit(solution)/shard_map/while/body/jvp(kpg,gh->kph)/dot_general | solution.py:34
  73.3 2.9 %fusion.185 = (f32[4,256]{1,0:T(4,128)S(1)}, f32[4,256]{1,0:T(4,128)S(1)}, f32[4,256]{1,0:T(4,128)S(1)}, f32[4,256]{1,0:T(4,128)S(1)}, f32[4,256]{1,0:T(4,128)S(1)}, /*index=5*/f32[4,256]{1,0:T(4,128)S(1)}) fusion(f32[4,256]{1,0:T(4,128)S(1)} %get-tuple-element.390, f32[4,256]{1,0:T(4,128)S(1)} %get-tuple-element.391, ...), kind=kOutput, calls=%fused_computation.71.clone.1 | convolution fusion | flops 820570112 | bytes 2158592 | tf_op jit(solution)/shard_map/while/body/transpose(jvp(kpg,gh->kph))/dot_general | solution.py:34
  76.2 1.2 fusion.188
  77.8 1.0 log-plus-one_reduce_fusion.2
  78.8 1.1 fusion.184
  79.9 1.5 %convolution_exponential_fusion.4 = f32[4,256,256]{2,1,0:T(8,128)S(1)} fusion(f32[4,256]{1,0:T(4,128)S(1)} %get-tuple-element.393, f32[4,256]{1,0:T(4,128)S(1)} %get-tuple-element.390, f32[4,256]{1,0:T(4,128)S(1)} %get-tuple-element.391, f32[4,256]{1,0:T(4,128)S(1)} %get-tuple-element.394, f32[4,256]{1,0:T(4,128)S(1)} %get-tuple-element.392, ...), kind=kOutput, calls=%fused_computation.58.clone.1 | convolution fusion | flops 808779776 | bytes 1081344 | tf_op jit(solution)/shard_map/while/body/jvp(kpg,gh->kph)/dot_general | solution.py:34
  81.3 2.9 %fusion.185 = (f32[4,256]{1,0:T(4,128)S(1)}, f32[4,256]{1,0:T(4,128)S(1)}, f32[4,256]{1,0:T(4,128)S(1)}, f32[4,256]{1,0:T(4,128)S(1)}, f32[4,256]{1,0:T(4,128)S(1)}, /*index=5*/f32[4,256]{1,0:T(4,128)S(1)}) fusion(f32[4,256]{1,0:T(4,128)S(1)} %get-tuple-element.390, f32[4,256]{1,0:T(4,128)S(1)} %get-tuple-element.391, ...), kind=kOutput, calls=%fused_computation.71.clone.1 | convolution fusion | flops 820570112 | bytes 2158592 | tf_op jit(solution)/shard_map/while/body/transpose(jvp(kpg,gh->kph))/dot_general | solution.py:34
  84.3 1.2 fusion.188
  85.8 1.0 log-plus-one_reduce_fusion.2
  86.8 1.1 fusion.184
  87.9 1.5 %convolution_exponential_fusion.4 = f32[4,256,256]{2,1,0:T(8,128)S(1)} fusion(f32[4,256]{1,0:T(4,128)S(1)} %get-tuple-element.393, f32[4,256]{1,0:T(4,128)S(1)} %get-tuple-element.390, f32[4,256]{1,0:T(4,128)S(1)} %get-tuple-element.391, f32[4,256]{1,0:T(4,128)S(1)} %get-tuple-element.394, f32[4,256]{1,0:T(4,128)S(1)} %get-tuple-element.392, ...), kind=kOutput, calls=%fused_computation.58.clone.1 | convolution fusion | flops 808779776 | bytes 1081344 | tf_op jit(solution)/shard_map/while/body/jvp(kpg,gh->kph)/dot_general | solution.py:34
  89.4 2.9 %fusion.185 = (f32[4,256]{1,0:T(4,128)S(1)}, f32[4,256]{1,0:T(4,128)S(1)}, f32[4,256]{1,0:T(4,128)S(1)}, f32[4,256]{1,0:T(4,128)S(1)}, f32[4,256]{1,0:T(4,128)S(1)}, /*index=5*/f32[4,256]{1,0:T(4,128)S(1)}) fusion(f32[4,256]{1,0:T(4,128)S(1)} %get-tuple-element.390, f32[4,256]{1,0:T(4,128)S(1)} %get-tuple-element.391, ...), kind=kOutput, calls=%fused_computation.71.clone.1 | convolution fusion | flops 820570112 | bytes 2158592 | tf_op jit(solution)/shard_map/while/body/transpose(jvp(kpg,gh->kph))/dot_general | solution.py:34
  92.3 1.2 fusion.188
  93.7 0.1 copy.116
  93.9 3.9 %fusion.93 = f32[9,64,384]{2,1,0:T(8,128)S(1)} fusion(f32[64,3072]{1,0:T(8,128)S(1)} %get-tuple-element.262, f32[9,3072]{1,0:T(8,128)S(1)} %bitcast.270, s32[3072]{0:T(1024)S(1)} %get-tuple-element.253), kind=kOutput, calls=%fused_computation.161 | convolution fusion | flops 4079812608 | bytes 1794048 | tf_op jit(solution)/shard_map/che,le->chl/dot_general | solution.py:197
  97.8 1.7 %copy.102 = f32[9,64,384]{2,0,1:T(8,128)} copy(f32[9,64,384]{2,1,0:T(8,128)S(1)} %fusion.93) | data formatting | bytes 1769472 | tf_op jit(solution)/shard_map/che,le->chl/dot_general | solution.py:197
  99.5 4.3 %all-to-all-start.2 = ((f32[9,64,384]{2,0,1:T(8,128)}), f32[9,64,384]{2,0,1:T(8,128)S(1)}, u32[]{:S(2)}, u32[]{:S(2)}) async-start(f32[9,64,384]{2,0,1:T(8,128)} %copy.102), calls=%async_computation.2 | async-start | bytes 3145728 | tf_op jit(solution)/shard_map/all_to_all | solution.py:198
  103.8 0.6 copy.103
  104.4 21.0 %all-to-all-done.2 = f32[9,64,384]{2,0,1:T(8,128)S(1)} async-done(((f32[9,64,384]{2,0,1:T(8,128)}), f32[9,64,384]{2,0,1:T(8,128)S(1)}, u32[]{:S(2)}, u32[]{:S(2)}) %all-to-all-start.2) | async-done | bytes 884768 | tf_op jit(solution)/shard_map/all_to_all | solution.py:198
  125.3 0.1 reduce_sum.153
  125.4 0.6 slice.104
  126.0 0.6 slice.105
  126.7 0.6 slice.103
  (87 shorter events, 1.7 us)
Async XLA Ops:
  0.6 6.3 %copy-start = (f32[5,24576]{1,0:T(8,128)S(1)}, f32[5,24576]{1,0:T(8,128)}, u32[]{:S(2)}) copy-start(f32[5,24576]{1,0:T(8,128)} %param.11) | copy-start | bytes 1474564
  7.1 6.4 %copy-start.1 = (f32[4,256]{1,0:T(4,128)S(1)}, f32[4,256]{1,0:T(4,128)}, u32[]{:S(2)}) copy-start(f32[4,256]{1,0:T(4,128)} %constant.180.clone.1) | copy-start | bytes 12292
  13.5 12.3 %copy-start.2 = (f32[1152]{0:T(1024)S(1)}, f32[1152]{0:T(1024)}, u32[]{:S(2)}) copy-start(f32[1152]{0:T(1024)} %constant.191.clone.1) | copy-start | bytes 13828
  25.7 10.7 %copy-start.3 = (f32[3,2,256]{2,1,0:T(2,128)S(1)}, f32[3,2,256]{2,1,0:T(2,128)}, u32[]{:S(2)}) copy-start(f32[3,2,256]{2,1,0:T(2,128)} %param.17) | copy-start | bytes 18436
  27.3 20.4 %copy-start.4 = (s32[2,64]{1,0:T(2,128)S(1)}, s32[2,64]{1,0:T(2,128)}, u32[]{:S(2)}) copy-start(s32[2,64]{1,0:T(2,128)} %param.16) | copy-start | bytes 1540
  27.3 20.0 %all-to-all-start = ((f32[64,1,1152]{2,1,0:T(1,128)}), f32[64,1,1152]{2,1,0:T(1,128)S(1)}, u32[]{:S(2)}, u32[]{:S(2)}) async-start(f32[64,1,1152]{2,1,0:T(1,128)} %copy.94), calls=%async_computation | async-start | bytes 589824 | tf_op jit(solution)/shard_map/all_to_all | solution.py:159
  48.8 10.7 %copy-start.5 = (s32[1,1,12]{2,1,0:T(1,128)S(1)}, s32[1,1,12]{2,1,0:T(1,128)}, u32[]{:S(2)}) copy-start(s32[1,1,12]{2,1,0:T(1,128)} %param.14) | copy-start | bytes 148
  50.2 18.5 %all-to-all-start.1 = ((f32[64,4,256]{2,1,0:T(4,128)}), f32[64,4,256]{2,1,0:T(4,128)S(1)}, u32[]{:S(2)}, u32[]{:S(2)}) async-start(f32[64,4,256]{2,1,0:T(4,128)} %copy.101), calls=%async_computation.1 | async-start | bytes 524288 | tf_op jit(solution)/shard_map/all_to_all | solution.py:172
  99.5 25.8 %all-to-all-start.2 = ((f32[9,64,384]{2,0,1:T(8,128)}), f32[9,64,384]{2,0,1:T(8,128)S(1)}, u32[]{:S(2)}, u32[]{:S(2)}) async-start(f32[9,64,384]{2,0,1:T(8,128)} %copy.102), calls=%async_computation.2 | async-start | bytes 3145728 | tf_op jit(solution)/shard_map/all_to_all | solution.py:198

commit v10 on v9

--- a/solution.py
+++ b/solution.py
@@ -8,7 +8,29 @@
 TSIDE = 16
 
 
-def render(params, pixel_x, pixel_y, live_mask):
+@jax.custom_vjp
+def reuse_before(log_keep, saved):
+    return saved
+
+
+def reuse_before_fwd(log_keep, saved):
+    return saved, None
+
+
+def reuse_before_bwd(_, grad):
+    entries_count = grad.shape[2]
+    ahead = (
+        jnp.arange(entries_count, dtype=jnp.int32)[:, None]
+        < jnp.arange(entries_count, dtype=jnp.int32)[None, :]
+    ).astype(jnp.float32)
+    grad_keep = jnp.einsum("kph,gh->kpg", grad, ahead, precision=lax.Precision.HIGHEST)
+    return (grad_keep, jnp.zeros_like(grad))
+
+
+reuse_before.defvjp(reuse_before_fwd, reuse_before_bwd)
+
+
+def render(params, pixel_x, pixel_y, live_mask, saved_before=None):
     centre_x = params[0][:, None, :]
     centre_y = params[1][:, None, :]
     inv_one = jnp.exp(-2.0 * params[2])
@@ -31,11 +53,14 @@
         jnp.arange(entries_count, dtype=jnp.int32)[:, None]
         < jnp.arange(entries_count, dtype=jnp.int32)[None, :]
     ).astype(jnp.float32)
-    before = jnp.einsum("kpg,gh->kph", log_keep, ahead, precision=lax.Precision.HIGHEST)
+    if saved_before is None:
+        before = jnp.einsum("kpg,gh->kph", log_keep, ahead, precision=lax.Precision.HIGHEST)
+    else:
+        before = reuse_before(log_keep, saved_before)
     weight = opaque_part * jnp.exp(before)
     colour = jnp.einsum("kpg,ckg->kcp", weight, params[6:9], precision=lax.Precision.HIGHEST)
     transmit = jnp.exp(jnp.sum(log_keep, axis=2))
-    return (colour, transmit)
+    return (colour, transmit, before)
 
 
 def pixel_grid(tile_ids, group_index, tiles_per, pixels):
@@ -124,15 +149,25 @@
         rows_y = lax.dynamic_slice_in_dim(pixel_y, first_row, turn_rows, 0)
         return (index_rows, live, chosen, rows_x, rows_y)
 
-    def forward_turn(turn_index, partial_value):
+    def forward_turn(turn_index, carried):
+        partial_value, saved = carried
         first_row = turn_index * turn_rows
         index_rows, live_mask, chosen, rows_x, rows_y = gather_turn(first_row)
-        colour, transmit = render(chosen, rows_x, rows_y, live_mask)
+        colour, transmit, before = render(chosen, rows_x, rows_y, live_mask)
         packed = jnp.concatenate([colour, transmit[:, None, :]], axis=1)
-        return lax.dynamic_update_slice_in_dim(partial_value, packed, first_row, 0)
-
-    partial_value = lax.fori_loop(
-        0, turn_count, forward_turn, jnp.broadcast_to(default, (slots_count, 4, pixels))
+        return (
+            lax.dynamic_update_slice_in_dim(partial_value, packed, first_row, 0),
+            lax.dynamic_update_slice_in_dim(saved, before, first_row, 0),
+        )
+
+    partial_value, saved_all = lax.fori_loop(
+        0,
+        turn_count,
+        forward_turn,
+        (
+            jnp.broadcast_to(default, (slots_count, 4, pixels)),
+            jnp.zeros((slots_count, pixels, entries.shape[1]), jnp.float32),
+        ),
     )
     target = jnp.where(tile_ids >= 0, tile_ids // tiles_per, parts_count)
     tag_width = 128
@@ -176,7 +211,10 @@
         first_row = turn_index * turn_rows
         index_rows, live_mask, chosen, rows_x, rows_y = gather_turn(first_row)
         upper_cot = lax.dynamic_slice_in_dim(slot_grads, first_row, turn_rows, 0)
-        _, pullback = jax.vjp(lambda values: render(values, rows_x, rows_y, live_mask), chosen)
+        saved = lax.dynamic_slice_in_dim(saved_all, first_row, turn_rows, 0)
+        _, pullback = jax.vjp(
+            lambda values: render(values, rows_x, rows_y, live_mask, saved)[:2], chosen
+        )
         grad_chosen = pullback((upper_cot[:, :3], upper_cot[:, 3]))[0]
         return lax.dynamic_update_slice_in_dim(compact, grad_chosen, first_row, 1)
 

time: 128 us -> 150 us (1.17)
  the two profiles are of different devices: /device:TPU:264 before, /device:TPU:232 now
where the time goes in v10:
time: 150 us; the launch traced here: 148 us
  matrix products  45.4 us (30%)
  waiting for transfers between devices  37.1 us (25%)
  starting transfers between devices  24.4 us (16%)
  other arithmetic  23.3 us (16%)
  local copies, waits for them, and re-layouts  16.1 us (11%)
  between operations  1.66 us (1%)
    all_to_all x1, waiting for transfers between devices, local(): lax.all_to_all(placed, 'tile', split_axis=1, concat_axis=1, tiled=True)  20.9 us
    dot_general x9, matrix products, render(): jnp.einsum('kpg,ckg->kcp', weight, params[6:9], precision=lax.Precision.H...  15.2 us
    all_to_all x1, starting transfers between devices, local(): lax.all_to_all(sent_back, 'dom', split_axis=0, concat_axis=0, tiled=True)  10.3 us
    all_to_all x1, starting transfers between devices, local(): lax.all_to_all(payload, 'dom', split_axis=0, concat_axis=0, tiled=True)  9.81 us
    all_to_all x1, waiting for transfers between devices, local(): lax.all_to_all(payload, 'dom', split_axis=0, concat_axis=0, tiled=True)  9.37 us
    dot_general x3, matrix products, render(): before = reuse_before(log_keep, saved_before)  9.19 us
    dot_general x3, matrix products, render(): jnp.einsum('kpg,gh->kph', log_keep, ahead, precision=lax.Precision.HIGHEST)  7.36 us
    all_to_all x1, waiting for transfers between devices, local(): lax.all_to_all(sent_back, 'dom', split_axis=0, concat_axis=0, tiled=True)  6.75 us
  transfers between devices with their start and end apart: 3, of which 3 were waited for; matrix products, arithmetic and copies ran while one was open for 2% of the time, Pallas kernels for 0%

profile of v10, /device:TPU:232, one launch (start us, length us, event | category | flops | bytes accessed | tf_op | source)
XLA Modules:
  0.0 148.4 jit_solution(5719989625166934113)
XLA Ops:
  0.6 1.3 fusion.142
  2.6 1.3 compare_and_fusion
  3.9 1.3 fusion.150
  5.2 1.3 add_select_fusion
  6.5 1.2 copy.133
  7.7 1.0 copy.134
  8.7 0.9 concatenate.20
  9.7 1.0 fusion.110
  10.7 6.2 %fusion.90 = f32[9,3072]{1,0:T(8,128)S(1)} fusion(f32[64,3072]{1,0:T(8,128)S(1)} %get-tuple-element.290, s32[3072]{0:T(1024)S(1)} %get-tuple-element.285, f32[3,64,384]{2,1,0:T(8,128)S(1)} %bitcast.263, f32[1,64,384]{2,1,0:T(8,128)S(1)} %concatenate.20, f32[5,64,384]{2,1,0:T(8,128)S(1)} %bitcast.261), kind=kOutput, calls=%fused_computation.160 | convolution fusion | flops 8158860288 | bytes 1794048 | tf_op jit(solution)/shard_map/chl,le->hce/dot_general | solution.py:135
  17.6 19.3 %while.22 = (s32[]{:T(128)}, f32[12,4,256]{2,1,0:T(4,128)S(1)}, f32[12,256,256]{2,1,0:T(8,128)S(1)}, s32[]{:T(128)}, f32[9,12,256]{2,1,0:T(8,128)S(1)}, /*index=...) while((s32[]{:T(128)}, f32[12,4,256]{2,1,0:T(4,128)S(1)}, ...), condition=%wide.region_4.5_spmd, body=%wide.region_2.4_spmd.sunk | while | flops 825316352 | bytes 3420491 | solution.py:163
  17.8 2.5 %constant_dynamic-update-slice_fusion.2 = (f32[12,256,256]{2,1,0:T(8,128)S(1)}, f32[4,256,256]{2,1,0:T(8,128)}) fusion(f32[12,256,256]{2,1,0:T(8,128)S(1)} %get-tuple-element.472, s32[]{:T(128)S(6)} %select_n.293, f32[4,256]{1,0:T(4,128)S(1)} %get-tuple-element.417, f32[4,256]{1,0:T(4,128)S(1)} %get-tuple-element.418, ...), kind=kOutput, calls=%fused_computation.39.clone.1 | convolution fusion | flops 808779776 | bytes 2129924 | tf_op jit(solution)/shard_map/while/body/kpg,gh->kph/dot_general | solution.py:57
  20.2 2.8 %fusion.168 = f32[4,3,256]{2,1,0:T(4,128)S(1)} fusion(f32[4,256,256]{2,1,0:T(8,128)} %get-tuple-element.424, f32[4,256]{1,0:T(4,128)S(1)} %get-tuple-element.417, f32[4,256]{1,0:T(4,128)S(1)} %get-tuple-element.418, f32[4,256]{1,0:T(4,128)S(1)} %get-tuple-element.419, f32[4,256]{1,0:T(4,128)S(1)} %get-tuple-element.420, ...), kind=kOutput, calls=%fused_computation.12.clone.1 | convolution fusion | flops 12845056 | bytes 1105920 | tf_op jit(solution)/shard_map/while/body/kpg,ckg->kcp/dot_general | solution.py:61
  23.0 1.0 fusion.167
  24.2 2.5 %constant_dynamic-update-slice_fusion.2 = (f32[12,256,256]{2,1,0:T(8,128)S(1)}, f32[4,256,256]{2,1,0:T(8,128)}) fusion(f32[12,256,256]{2,1,0:T(8,128)S(1)} %get-tuple-element.472, s32[]{:T(128)S(6)} %select_n.293, f32[4,256]{1,0:T(4,128)S(1)} %get-tuple-element.417, f32[4,256]{1,0:T(4,128)S(1)} %get-tuple-element.418, ...), kind=kOutput, calls=%fused_computation.39.clone.1 | convolution fusion | flops 808779776 | bytes 2129924 | tf_op jit(solution)/shard_map/while/body/kpg,gh->kph/dot_general | solution.py:57
  26.7 2.8 %fusion.168 = f32[4,3,256]{2,1,0:T(4,128)S(1)} fusion(f32[4,256,256]{2,1,0:T(8,128)} %get-tuple-element.424, f32[4,256]{1,0:T(4,128)S(1)} %get-tuple-element.417, f32[4,256]{1,0:T(4,128)S(1)} %get-tuple-element.418, f32[4,256]{1,0:T(4,128)S(1)} %get-tuple-element.419, f32[4,256]{1,0:T(4,128)S(1)} %get-tuple-element.420, ...), kind=kOutput, calls=%fused_computation.12.clone.1 | convolution fusion | flops 12845056 | bytes 1105920 | tf_op jit(solution)/shard_map/while/body/kpg,ckg->kcp/dot_general | solution.py:61
  29.4 1.0 fusion.167
  30.7 2.5 %constant_dynamic-update-slice_fusion.2 = (f32[12,256,256]{2,1,0:T(8,128)S(1)}, f32[4,256,256]{2,1,0:T(8,128)}) fusion(f32[12,256,256]{2,1,0:T(8,128)S(1)} %get-tuple-element.472, s32[]{:T(128)S(6)} %select_n.293, f32[4,256]{1,0:T(4,128)S(1)} %get-tuple-element.417, f32[4,256]{1,0:T(4,128)S(1)} %get-tuple-element.418, ...), kind=kOutput, calls=%fused_computation.39.clone.1 | convolution fusion | flops 808779776 | bytes 2129924 | tf_op jit(solution)/shard_map/while/body/kpg,gh->kph/dot_general | solution.py:57
  33.1 2.8 %fusion.168 = f32[4,3,256]{2,1,0:T(4,128)S(1)} fusion(f32[4,256,256]{2,1,0:T(8,128)} %get-tuple-element.424, f32[4,256]{1,0:T(4,128)S(1)} %get-tuple-element.417, f32[4,256]{1,0:T(4,128)S(1)} %get-tuple-element.418, f32[4,256]{1,0:T(4,128)S(1)} %get-tuple-element.419, f32[4,256]{1,0:T(4,128)S(1)} %get-tuple-element.420, ...), kind=kOutput, calls=%fused_computation.12.clone.1 | convolution fusion | flops 12845056 | bytes 1105920 | tf_op jit(solution)/shard_map/while/body/kpg,ckg->kcp/dot_general | solution.py:61
  35.9 1.0 fusion.167
  37.6 1.0 copy.94
  38.6 9.8 %all-to-all-start = ((f32[64,1,1152]{2,1,0:T(1,128)}), f32[64,1,1152]{2,1,0:T(1,128)}, u32[]{:S(2)}, u32[]{:S(2)}) async-start(f32[64,1,1152]{2,1,0:T(1,128)} %copy.94), calls=%async_computation | async-start | bytes 589824 | tf_op jit(solution)/shard_map/all_to_all | solution.py:194
  48.5 0.6 copy.100
  49.1 9.4 %all-to-all-done = f32[64,1,1152]{2,1,0:T(1,128)} async-done(((f32[64,1,1152]{2,1,0:T(1,128)}), f32[64,1,1152]{2,1,0:T(1,128)}, u32[]{:S(2)}, u32[]{:S(2)}) %all-to-all-start) | async-done | bytes 294944 | tf_op jit(solution)/shard_map/all_to_all | solution.py:194
  58.4 1.0 copy.135
  59.5 0.7 fusion.133
  60.2 0.8 reshape.634
  61.0 1.1 copy_select_fusion.1
  62.1 1.2 fusion.112
  63.5 1.4 multiply_reduce_fusion.1
  65.7 0.9 copy.101
  66.5 10.3 %all-to-all-start.1 = ((f32[64,4,256]{2,1,0:T(4,128)}), f32[64,4,256]{2,1,0:T(4,128)S(1)}, u32[]{:S(2)}, u32[]{:S(2)}) async-start(f32[64,4,256]{2,1,0:T(4,128)} %copy.101), calls=%async_computation.1 | async-start | bytes 524288 | tf_op jit(solution)/shard_map/all_to_all | solution.py:207
  76.8 0.7 fusion.144
  78.1 6.8 %all-to-all-done.1 = f32[64,4,256]{2,1,0:T(4,128)S(1)} async-done(((f32[64,4,256]{2,1,0:T(4,128)}), f32[64,4,256]{2,1,0:T(4,128)S(1)}, u32[]{:S(2)}, u32[]{:S(2)}) %all-to-all-start.1) | async-done | bytes 262176 | tf_op jit(solution)/shard_map/all_to_all | solution.py:207
  84.8 1.3 gather_fusion
  86.2 0.9 broadcast_select_fusion.1
  87.1 26.6 %while.23 = (s32[]{:T(128)}, f32[9,12,256]{2,1,0:T(8,128)S(1)}, s32[]{:T(128)}, f32[12,4,256]{2,1,0:T(4,128)S(1)}, f32[9,12,256]{2,1,0:T(8,128)S(1)}, /*index=5*...) while((s32[]{:T(128)}, f32[9,12,256]{2,1,0:T(8,128)S(1)}, ...), condition=%wide.region_16.17_spmd, body=%wide.region_8.16_spmd.sunk | while | flops 846658560 | bytes 6805875 | solution.py:221
  87.2 0.7 bitcast_multiply_fusion.18
  87.9 0.7 constant_dynamic-slice_fusion.16
  88.6 1.0 log-plus-one_reduce_fusion.2
  89.7 1.1 fusion.173
  90.8 3.1 %fusion.174 = (f32[4,256]{1,0:T(4,128)S(1)}, f32[4,256]{1,0:T(4,128)S(1)}, f32[4,256]{1,0:T(4,128)S(1)}, f32[4,256]{1,0:T(4,128)S(1)}, f32[4,256]{1,0:T(4,128)S(1)}, /*index=5*/f32[4,256]{1,0:T(4,128)S(1)}) fusion(f32[4,256]{1,0:T(4,128)S(1)} %get-tuple-element.435, f32[4,256]{1,0:T(4,128)S(1)} %get-tuple-element.436, ...), kind=kOutput, calls=%fused_computation.73.clone.1 | convolution fusion | flops 820570112 | bytes 4289536 | tf_op jit(solution)/shard_map/while/body/transpose(jvp(kph,gh->kpg))/dot_general | solution.py:59
  93.9 0.7 fusion.176
  94.6 1.3 fusion.177
  96.0 0.7 bitcast_multiply_fusion.18
  96.8 0.7 constant_dynamic-slice_fusion.16
  97.5 1.0 log-plus-one_reduce_fusion.2
  98.5 1.1 fusion.173
  99.6 3.1 %fusion.174 = (f32[4,256]{1,0:T(4,128)S(1)}, f32[4,256]{1,0:T(4,128)S(1)}, f32[4,256]{1,0:T(4,128)S(1)}, f32[4,256]{1,0:T(4,128)S(1)}, f32[4,256]{1,0:T(4,128)S(1)}, /*index=5*/f32[4,256]{1,0:T(4,128)S(1)}) fusion(f32[4,256]{1,0:T(4,128)S(1)} %get-tuple-element.435, f32[4,256]{1,0:T(4,128)S(1)} %get-tuple-element.436, ...), kind=kOutput, calls=%fused_computation.73.clone.1 | convolution fusion | flops 820570112 | bytes 4289536 | tf_op jit(solution)/shard_map/while/body/transpose(jvp(kph,gh->kpg))/dot_general | solution.py:59
  102.8 0.7 fusion.176
  103.5 1.3 fusion.177
  104.9 0.7 bitcast_multiply_fusion.18
  105.6 0.7 constant_dynamic-slice_fusion.16
  106.3 1.0 log-plus-one_reduce_fusion.2
  107.4 1.1 fusion.173
  108.5 3.1 %fusion.174 = (f32[4,256]{1,0:T(4,128)S(1)}, f32[4,256]{1,0:T(4,128)S(1)}, f32[4,256]{1,0:T(4,128)S(1)}, f32[4,256]{1,0:T(4,128)S(1)}, f32[4,256]{1,0:T(4,128)S(1)}, /*index=5*/f32[4,256]{1,0:T(4,128)S(1)}) fusion(f32[4,256]{1,0:T(4,128)S(1)} %get-tuple-element.435, f32[4,256]{1,0:T(4,128)S(1)} %get-tuple-element.436, ...), kind=kOutput, calls=%fused_computation.73.clone.1 | convolution fusion | flops 820570112 | bytes 4289536 | tf_op jit(solution)/shard_map/while/body/transpose(jvp(kph,gh->kpg))/dot_general | solution.py:59
  111.6 0.7 fusion.176
  112.4 1.3 fusion.177
  113.8 5.0 %fusion.91 = f32[9,64,384]{2,1,0:T(8,128)S(1)} fusion(f32[64,3072]{1,0:T(8,128)} %get-tuple-element.291, f32[9,3072]{1,0:T(8,128)S(1)} %bitcast.266, s32[3072]{0:T(1024)S(1)} %copy-done.6), kind=kOutput, calls=%fused_computation.161 | convolution fusion | flops 4079812608 | bytes 1794048 | tf_op jit(solution)/shard_map/che,le->chl/dot_general | solution.py:235
  118.9 1.7 %copy.102 = f32[9,64,384]{2,0,1:T(8,128)} copy(f32[9,64,384]{2,1,0:T(8,128)S(1)} %fusion.91) | data formatting | bytes 1769472 | tf_op jit(solution)/shard_map/che,le->chl/dot_general | solution.py:235
  120.6 4.3 %all-to-all-start.2 = ((f32[9,64,384]{2,0,1:T(8,128)}), f32[9,64,384]{2,0,1:T(8,128)S(1)}, u32[]{:S(2)}, u32[]{:S(2)}) async-start(f32[9,64,384]{2,0,1:T(8,128)} %copy.102), calls=%async_computation.2 | async-start | bytes 3145728 | tf_op jit(solution)/shard_map/all_to_all | solution.py:236
  125.5 20.9 %all-to-all-done.2 = f32[9,64,384]{2,0,1:T(8,128)S(1)} async-done(((f32[9,64,384]{2,0,1:T(8,128)}), f32[9,64,384]{2,0,1:T(8,128)S(1)}, u32[]{:S(2)}, u32[]{:S(2)}) %all-to-all-start.2) | async-done | bytes 884768 | tf_op jit(solution)/shard_map/all_to_all | solution.py:236
  146.6 0.6 slice.103
  147.2 0.6 slice.105
  147.8 0.6 slice.104
  (95 shorter events, 4.8 us)
Async XLA Ops:
  16.9 0.7 copy-start.5
  17.6 19.6 %copy-start.7 = (f32[1152]{0:T(1024)S(1)}, f32[1152]{0:T(1024)}, u32[]{:S(2)}) copy-start(f32[1152]{0:T(1024)} %constant.192.clone.1) | copy-start | bytes 13828
  17.6 30.8 %copy-start.8 = (f32[3,2,256]{2,1,0:T(2,128)S(1)}, f32[3,2,256]{2,1,0:T(2,128)}, u32[]{:S(2)}) copy-start(f32[3,2,256]{2,1,0:T(2,128)} %param.17) | copy-start | bytes 18436
  37.0 22.5 %copy-start = (f32[12,256]{1,0:T(8,128)}, f32[12,256]{1,0:T(8,128)S(1)}, u32[]{:S(2)}) copy-start(f32[12,256]{1,0:T(8,128)S(1)} %get-tuple-element.568) | copy-start | bytes 36868
  37.0 22.5 %copy-start.1 = (f32[12,256]{1,0:T(8,128)}, f32[12,256]{1,0:T(8,128)S(1)}, u32[]{:S(2)}) copy-start(f32[12,256]{1,0:T(8,128)S(1)} %get-tuple-element.569) | copy-start | bytes 36868
  37.0 22.5 %copy-start.2 = (f32[12,256]{1,0:T(8,128)}, f32[12,256]{1,0:T(8,128)S(1)}, u32[]{:S(2)}) copy-start(f32[12,256]{1,0:T(8,128)S(1)} %get-tuple-element.570) | copy-start | bytes 36868
  38.6 19.8 %all-to-all-start = ((f32[64,1,1152]{2,1,0:T(1,128)}), f32[64,1,1152]{2,1,0:T(1,128)}, u32[]{:S(2)}, u32[]{:S(2)}) async-start(f32[64,1,1152]{2,1,0:T(1,128)} %copy.94), calls=%async_computation | async-start | bytes 589824 | tf_op jit(solution)/shard_map/all_to_all | solution.py:194
  61.0 4.1 %copy-start.10 = (s32[2,64]{1,0:T(2,128)S(1)}, s32[2,64]{1,0:T(2,128)}, u32[]{:S(2)}) copy-start(s32[2,64]{1,0:T(2,128)} %param.16) | copy-start | bytes 1540
  61.0 4.6 %copy-start.9 = (pred[64]{0:T(512)(128)(4,1)S(1)}, pred[64]{0:T(512)(128)(4,1)}, u32[]{:S(2)}) copy-start(pred[64]{0:T(512)(128)(4,1)} %fusion.133) | copy-start | bytes 196
  66.5 18.3 %all-to-all-start.1 = ((f32[64,4,256]{2,1,0:T(4,128)}), f32[64,4,256]{2,1,0:T(4,128)S(1)}, u32[]{:S(2)}, u32[]{:S(2)}) async-start(f32[64,4,256]{2,1,0:T(4,128)} %copy.101), calls=%async_computation.1 | async-start | bytes 524288 | tf_op jit(solution)/shard_map/all_to_all | solution.py:207
  87.1 26.6 %copy-start.4 = (pred[12,256]{1,0:T(8,128)(4,1)S(1)}, pred[12,256]{1,0:T(8,128)(4,1)}, u32[]{:S(2)}) copy-start(pred[12,256]{1,0:T(8,128)(4,1)} %get-tuple-element.258) | copy-start | bytes 9220
  87.1 26.8 %copy-start.6 = (s32[3072]{0:T(1024)S(1)}, s32[3072]{0:T(1024)}, u32[]{:S(2)}) copy-start(s32[3072]{0:T(1024)} %get-tuple-element.282) | copy-start | bytes 36868
  118.9 6.0 %copy-start.3 = (f32[2,3,256]{2,1,0:T(4,128)S(1)}, f32[2,3,256]{2,1,0:T(4,128)}, u32[]{:S(2)}) copy-start(f32[2,3,256]{2,1,0:T(4,128)} %get-tuple-element.220) | copy-start | bytes 18436
  120.6 25.8 %all-to-all-start.2 = ((f32[9,64,384]{2,0,1:T(8,128)}), f32[9,64,384]{2,0,1:T(8,128)S(1)}, u32[]{:S(2)}, u32[]{:S(2)}) async-start(f32[9,64,384]{2,0,1:T(8,128)} %copy.102), calls=%async_computation.2 | async-start | bytes 3145728 | tf_op jit(solution)/shard_map/all_to_all | solution.py:236

commit v11 on v9

--- a/solution.py
+++ b/solution.py
@@ -196,11 +196,12 @@
     )
     placed = jnp.einsum("che,le->chl", spread, lo_hot, precision=lax.Precision.HIGH)
     gathered = lax.all_to_all(placed, "tile", split_axis=1, concat_axis=1, tiled=True)
-    total = jnp.sum(
-        gathered.reshape(rows_count, groups_count, hi_size // groups_count, lo_size), axis=1
-    )
-    shares = total.reshape(rows_count, shard)
-    return (rendered, shares[:5], shares[5], shares[6:])
+    arrived_grads = gathered.reshape(rows_count, groups_count, hi_size // groups_count, lo_size)
+
+    def share_of(first, last):
+        return jnp.sum(arrived_grads[first:last], axis=1).reshape(last - first, shard)
+
+    return (rendered, share_of(0, 5), share_of(5, 6)[0], share_of(6, rows_count))
 
 
 def solution(mesh):

time: 128 us -> 133 us (1.039)
  the two profiles are of different devices: /device:TPU:264 before, /device:TPU:136 now
where the time goes in v11:
time: 133 us; the launch traced here: 132 us
  waiting for transfers between devices  47 us (35%)
  matrix products  40.3 us (30%)
  starting transfers between devices  21.4 us (16%)
  other arithmetic  12.8 us (10%)
  local copies, waits for them, and re-layouts  8.36 us (6%)
  between operations  1.69 us (1%)
    all_to_all x1, waiting for transfers between devices, local(): lax.all_to_all(placed, 'tile', split_axis=1, concat_axis=1, tiled=True)  21 us
    dot_general x9, matrix products, render(): jnp.einsum('kpg,gh->kph', log_keep, ahead, precision=lax.Precision.HIGHEST)  18.8 us
    all_to_all x1, waiting for transfers between devices, local(): lax.all_to_all(payload, 'dom', split_axis=0, concat_axis=0, tiled=True)  13.9 us
    all_to_all x1, waiting for transfers between devices, local(): lax.all_to_all(sent_back, 'dom', split_axis=0, concat_axis=0, tiled=True)  12.2 us
    all_to_all x1, starting transfers between devices, local(): lax.all_to_all(payload, 'dom', split_axis=0, concat_axis=0, tiled=True)  10.8 us
    dot_general x9, matrix products, render(): jnp.einsum('kpg,ckg->kcp', weight, params[6:9], precision=lax.Precision.H...  9.63 us
    all_to_all x1, starting transfers between devices, local(): lax.all_to_all(sent_back, 'dom', split_axis=0, concat_axis=0, tiled=True)  6.26 us
    dot_general x1, matrix products, local(): jnp.einsum('chl,le->hce', params.reshape(params.shape[0], hi_size, lo_siz...  6.21 us
  transfers between devices with their start and end apart: 3, of which 3 were waited for; matrix products, arithmetic and copies ran while one was open for 0% of the time, Pallas kernels for 0%

profile of v11, /device:TPU:136, one launch (start us, length us, event | category | flops | bytes accessed | tf_op | source)
XLA Modules:
  0.0 132.3 jit_solution(3961145270785493691)
XLA Ops:
  0.7 0.7 compare_and_fusion
  1.4 1.3 fusion.144
  3.4 0.1 convert_reduce_fusion
  3.5 0.7 fusion.152
  4.2 0.7 add_select_fusion
  4.9 0.9 concatenate.20
  5.9 1.0 copy.136
  6.9 0.1 copy.135
  7.0 0.1 fusion.112
  7.1 6.2 %fusion.92 = f32[9,3072]{1,0:T(8,128)S(1)} fusion(f32[64,3072]{1,0:T(8,128)S(1)} %get-tuple-element.261, s32[3072]{0:T(1024)S(1)} %get-tuple-element.256, f32[3,64,384]{2,1,0:T(8,128)S(1)} %bitcast.270, f32[1,64,384]{2,1,0:T(8,128)S(1)} %concatenate.20, f32[5,64,384]{2,1,0:T(8,128)S(1)} %bitcast.268), kind=kOutput, calls=%fused_computation.160 | convolution fusion | flops 8158860288 | bytes 1794048 | tf_op jit(solution)/shard_map/chl,le->hce/dot_general | solution.py:110
  13.5 12.2 %while.20 = (s32[]{:T(128)}, f32[12,4,256]{2,1,0:T(4,128)S(1)}, s32[]{:T(128)}, f32[9,12,256]{2,1,0:T(8,128)S(1)}, f32[12,256]{1,0:T(8,128)S(1)}, /*index=5*/f32...) while((s32[]{:T(128)}, f32[12,4,256]{2,1,0:T(4,128)S(1)}, ...), condition=%wide.region_4.5_spmd, body=%wide.region_2.4_spmd.sunk | while | flops 825316352 | bytes 2339135 | solution.py:134
  13.7 1.0 fusion.175
  14.7 1.9 %fusion.176 = f32[4,256,256]{2,1,0:T(8,128)S(1)} fusion(f32[4,256]{1,0:T(4,128)S(1)} %get-tuple-element.375, f32[4,256]{1,0:T(4,128)S(1)} %get-tuple-element.376, f32[4,256]{1,0:T(4,128)S(1)} %get-tuple-element.377, f32[4,256]{1,0:T(4,128)S(1)} %get-tuple-element.378, f32[4,256]{1,0:T(4,128)S(1)} %get-tuple-element.379, ...), kind=kOutput, calls=%fused_computation.8.clone.1 | convolution fusion | flops 812187648 | bytes 1081344 | tf_op jit(solution)/shard_map/while/body/kpg,gh->kph/dot_general | solution.py:34
  16.6 1.0 fusion.177
  17.7 1.0 fusion.175
  18.8 1.9 %fusion.176 = f32[4,256,256]{2,1,0:T(8,128)S(1)} fusion(f32[4,256]{1,0:T(4,128)S(1)} %get-tuple-element.375, f32[4,256]{1,0:T(4,128)S(1)} %get-tuple-element.376, f32[4,256]{1,0:T(4,128)S(1)} %get-tuple-element.377, f32[4,256]{1,0:T(4,128)S(1)} %get-tuple-element.378, f32[4,256]{1,0:T(4,128)S(1)} %get-tuple-element.379, ...), kind=kOutput, calls=%fused_computation.8.clone.1 | convolution fusion | flops 812187648 | bytes 1081344 | tf_op jit(solution)/shard_map/while/body/kpg,gh->kph/dot_general | solution.py:34
  20.6 1.0 fusion.177
  21.8 1.0 fusion.175
  22.8 1.9 %fusion.176 = f32[4,256,256]{2,1,0:T(8,128)S(1)} fusion(f32[4,256]{1,0:T(4,128)S(1)} %get-tuple-element.375, f32[4,256]{1,0:T(4,128)S(1)} %get-tuple-element.376, f32[4,256]{1,0:T(4,128)S(1)} %get-tuple-element.377, f32[4,256]{1,0:T(4,128)S(1)} %get-tuple-element.378, f32[4,256]{1,0:T(4,128)S(1)} %get-tuple-element.379, ...), kind=kOutput, calls=%fused_computation.8.clone.1 | convolution fusion | flops 812187648 | bytes 1081344 | tf_op jit(solution)/shard_map/while/body/kpg,gh->kph/dot_general | solution.py:34
  24.7 1.0 fusion.177
  25.8 0.4 fusion.103
  26.2 1.0 copy.94
  27.2 10.8 %all-to-all-start = ((f32[64,1,1152]{2,1,0:T(1,128)}), f32[64,1,1152]{2,1,0:T(1,128)S(1)}, u32[]{:S(2)}, u32[]{:S(2)}) async-start(f32[64,1,1152]{2,1,0:T(1,128)} %copy.94), calls=%async_computation | async-start | bytes 589824 | tf_op jit(solution)/shard_map/all_to_all | solution.py:159
  38.1 13.9 %all-to-all-done = f32[64,1,1152]{2,1,0:T(1,128)S(1)} async-done(((f32[64,1,1152]{2,1,0:T(1,128)}), f32[64,1,1152]{2,1,0:T(1,128)S(1)}, u32[]{:S(2)}, u32[]{:S(2)}) %all-to-all-start) | async-done | bytes 294944 | tf_op jit(solution)/shard_map/all_to_all | solution.py:159
  52.0 0.1 fusion.135
  52.1 0.1 reshape.638
  52.3 0.1 copy_select_fusion.1
  52.4 0.5 fusion.114
  52.9 0.3 fusion.106
  53.2 0.1 multiply_reduce_fusion.1
  53.2 0.2 fusion.105
  53.5 0.4 convolution_bitcast_fusion
  53.9 0.1 fusion.121
  54.0 0.9 copy.101
  54.9 6.3 %all-to-all-start.1 = ((f32[64,4,256]{2,1,0:T(4,128)}), f32[64,4,256]{2,1,0:T(4,128)S(1)}, u32[]{:S(2)}, u32[]{:S(2)}) async-start(f32[64,4,256]{2,1,0:T(4,128)} %copy.101), calls=%async_computation.1 | async-start | bytes 524288 | tf_op jit(solution)/shard_map/all_to_all | solution.py:172
  61.2 12.2 %all-to-all-done.1 = f32[64,4,256]{2,1,0:T(4,128)S(1)} async-done(((f32[64,4,256]{2,1,0:T(4,128)}), f32[64,4,256]{2,1,0:T(4,128)S(1)}, u32[]{:S(2)}, u32[]{:S(2)}) %all-to-all-start.1) | async-done | bytes 262176 | tf_op jit(solution)/shard_map/all_to_all | solution.py:172
  73.3 0.6 gather_fusion
  74.0 24.4 %while.21 = (s32[]{:T(128)}, f32[9,12,256]{2,1,0:T(8,128)S(1)}, s32[]{:T(128)}, f32[12,4,256]{2,1,0:T(4,128)S(1)}, f32[9,12,256]{2,1,0:T(8,128)S(1)}, /*index=5*...) while((s32[]{:T(128)}, f32[9,12,256]{2,1,0:T(8,128)S(1)}, ...), condition=%wide.region_16.17_spmd, body=%wide.region_8.16_spmd.sunk | while | flops 1655438336 | bytes 5755247 | solution.py:183
  74.4 1.0 log-plus-one_reduce_fusion.2
  75.4 1.1 fusion.184
  76.5 1.5 %convolution_exponential_fusion.4 = f32[4,256,256]{2,1,0:T(8,128)S(1)} fusion(f32[4,256]{1,0:T(4,128)S(1)} %get-tuple-element.393, f32[4,256]{1,0:T(4,128)S(1)} %get-tuple-element.390, f32[4,256]{1,0:T(4,128)S(1)} %get-tuple-element.391, f32[4,256]{1,0:T(4,128)S(1)} %get-tuple-element.394, f32[4,256]{1,0:T(4,128)S(1)} %get-tuple-element.392, ...), kind=kOutput, calls=%fused_computation.58.clone.1 | convolution fusion | flops 808779776 | bytes 1081344 | tf_op jit(solution)/shard_map/while/body/jvp(kpg,gh->kph)/dot_general | solution.py:34
  78.0 2.9 %fusion.185 = (f32[4,256]{1,0:T(4,128)S(1)}, f32[4,256]{1,0:T(4,128)S(1)}, f32[4,256]{1,0:T(4,128)S(1)}, f32[4,256]{1,0:T(4,128)S(1)}, f32[4,256]{1,0:T(4,128)S(1)}, /*index=5*/f32[4,256]{1,0:T(4,128)S(1)}) fusion(f32[4,256]{1,0:T(4,128)S(1)} %get-tuple-element.390, f32[4,256]{1,0:T(4,128)S(1)} %get-tuple-element.391, ...), kind=kOutput, calls=%fused_computation.71.clone.1 | convolution fusion | flops 820570112 | bytes 2158592 | tf_op jit(solution)/shard_map/while/body/transpose(jvp(kpg,gh->kph))/dot_general | solution.py:34
  80.9 1.2 fusion.188
  82.5 1.0 log-plus-one_reduce_fusion.2
  83.5 1.1 fusion.184
  84.5 1.5 %convolution_exponential_fusion.4 = f32[4,256,256]{2,1,0:T(8,128)S(1)} fusion(f32[4,256]{1,0:T(4,128)S(1)} %get-tuple-element.393, f32[4,256]{1,0:T(4,128)S(1)} %get-tuple-element.390, f32[4,256]{1,0:T(4,128)S(1)} %get-tuple-element.391, f32[4,256]{1,0:T(4,128)S(1)} %get-tuple-element.394, f32[4,256]{1,0:T(4,128)S(1)} %get-tuple-element.392, ...), kind=kOutput, calls=%fused_computation.58.clone.1 | convolution fusion | flops 808779776 | bytes 1081344 | tf_op jit(solution)/shard_map/while/body/jvp(kpg,gh->kph)/dot_general | solution.py:34
  86.0 2.9 %fusion.185 = (f32[4,256]{1,0:T(4,128)S(1)}, f32[4,256]{1,0:T(4,128)S(1)}, f32[4,256]{1,0:T(4,128)S(1)}, f32[4,256]{1,0:T(4,128)S(1)}, f32[4,256]{1,0:T(4,128)S(1)}, /*index=5*/f32[4,256]{1,0:T(4,128)S(1)}) fusion(f32[4,256]{1,0:T(4,128)S(1)} %get-tuple-element.390, f32[4,256]{1,0:T(4,128)S(1)} %get-tuple-element.391, ...), kind=kOutput, calls=%fused_computation.71.clone.1 | convolution fusion | flops 820570112 | bytes 2158592 | tf_op jit(solution)/shard_map/while/body/transpose(jvp(kpg,gh->kph))/dot_general | solution.py:34
  89.0 1.2 fusion.188
  90.5 1.0 log-plus-one_reduce_fusion.2
  91.5 1.1 fusion.184
  92.6 1.5 %convolution_exponential_fusion.4 = f32[4,256,256]{2,1,0:T(8,128)S(1)} fusion(f32[4,256]{1,0:T(4,128)S(1)} %get-tuple-element.393, f32[4,256]{1,0:T(4,128)S(1)} %get-tuple-element.390, f32[4,256]{1,0:T(4,128)S(1)} %get-tuple-element.391, f32[4,256]{1,0:T(4,128)S(1)} %get-tuple-element.394, f32[4,256]{1,0:T(4,128)S(1)} %get-tuple-element.392, ...), kind=kOutput, calls=%fused_computation.58.clone.1 | convolution fusion | flops 808779776 | bytes 1081344 | tf_op jit(solution)/shard_map/while/body/jvp(kpg,gh->kph)/dot_general | solution.py:34
  94.1 2.9 %fusion.185 = (f32[4,256]{1,0:T(4,128)S(1)}, f32[4,256]{1,0:T(4,128)S(1)}, f32[4,256]{1,0:T(4,128)S(1)}, f32[4,256]{1,0:T(4,128)S(1)}, f32[4,256]{1,0:T(4,128)S(1)}, /*index=5*/f32[4,256]{1,0:T(4,128)S(1)}) fusion(f32[4,256]{1,0:T(4,128)S(1)} %get-tuple-element.390, f32[4,256]{1,0:T(4,128)S(1)} %get-tuple-element.391, ...), kind=kOutput, calls=%fused_computation.71.clone.1 | convolution fusion | flops 820570112 | bytes 2158592 | tf_op jit(solution)/shard_map/while/body/transpose(jvp(kpg,gh->kph))/dot_general | solution.py:34
  97.0 1.2 fusion.188
  98.4 0.1 copy.117
  98.6 3.9 %fusion.93 = f32[9,64,384]{2,1,0:T(8,128)S(1)} fusion(f32[64,3072]{1,0:T(8,128)S(1)} %get-tuple-element.262, f32[9,3072]{1,0:T(8,128)S(1)} %bitcast.273, s32[3072]{0:T(1024)S(1)} %get-tuple-element.253), kind=kOutput, calls=%fused_computation.161 | convolution fusion | flops 4079812608 | bytes 1794048 | tf_op jit(solution)/shard_map/che,le->chl/dot_general | solution.py:197
  102.5 1.7 %copy.102 = f32[9,64,384]{2,0,1:T(8,128)} copy(f32[9,64,384]{2,1,0:T(8,128)S(1)} %fusion.93) | data formatting | bytes 1769472 | tf_op jit(solution)/shard_map/che,le->chl/dot_general | solution.py:197
  104.2 4.3 %all-to-all-start.2 = ((f32[9,64,384]{2,0,1:T(8,128)}), f32[9,64,384]{2,0,1:T(8,128)S(1)}, u32[]{:S(2)}, u32[]{:S(2)}) async-start(f32[9,64,384]{2,0,1:T(8,128)} %copy.102), calls=%async_computation.2 | async-start | bytes 3145728 | tf_op jit(solution)/shard_map/all_to_all | solution.py:198
  108.5 0.6 copy.103
  109.1 21.0 %all-to-all-done.2 = f32[9,64,384]{2,0,1:T(8,128)S(1)} async-done(((f32[9,64,384]{2,0,1:T(8,128)}), f32[9,64,384]{2,0,1:T(8,128)S(1)}, u32[]{:S(2)}, u32[]{:S(2)}) %all-to-all-start.2) | async-done | bytes 884768 | tf_op jit(solution)/shard_map/all_to_all | solution.py:198
  130.0 0.1 slice.107
  130.1 0.6 squeeze_reshape.3
  130.8 0.7 reduce_sum.177
  131.5 0.1 slice.108
  131.6 0.7 reduce_sum.179
  (90 shorter events, 1.8 us)
Async XLA Ops:
  0.6 6.3 %copy-start = (f32[5,24576]{1,0:T(8,128)S(1)}, f32[5,24576]{1,0:T(8,128)}, u32[]{:S(2)}) copy-start(f32[5,24576]{1,0:T(8,128)} %param.11) | copy-start | bytes 1474564
  7.1 6.4 %copy-start.1 = (f32[4,256]{1,0:T(4,128)S(1)}, f32[4,256]{1,0:T(4,128)}, u32[]{:S(2)}) copy-start(f32[4,256]{1,0:T(4,128)} %constant.180.clone.1) | copy-start | bytes 12292
  13.5 12.3 %copy-start.2 = (f32[1152]{0:T(1024)S(1)}, f32[1152]{0:T(1024)}, u32[]{:S(2)}) copy-start(f32[1152]{0:T(1024)} %constant.191.clone.1) | copy-start | bytes 13828
  25.7 12.4 %copy-start.3 = (f32[3,2,256]{2,1,0:T(2,128)S(1)}, f32[3,2,256]{2,1,0:T(2,128)}, u32[]{:S(2)}) copy-start(f32[3,2,256]{2,1,0:T(2,128)} %param.17) | copy-start | bytes 18436
  27.2 25.2 %copy-start.4 = (s32[2,64]{1,0:T(2,128)S(1)}, s32[2,64]{1,0:T(2,128)}, u32[]{:S(2)}) copy-start(s32[2,64]{1,0:T(2,128)} %param.16) | copy-start | bytes 1540
  27.2 24.7 %all-to-all-start = ((f32[64,1,1152]{2,1,0:T(1,128)}), f32[64,1,1152]{2,1,0:T(1,128)S(1)}, u32[]{:S(2)}, u32[]{:S(2)}) async-start(f32[64,1,1152]{2,1,0:T(1,128)} %copy.94), calls=%async_computation | async-start | bytes 589824 | tf_op jit(solution)/shard_map/all_to_all | solution.py:159
  53.5 7.7 %copy-start.5 = (s32[1,1,12]{2,1,0:T(1,128)S(1)}, s32[1,1,12]{2,1,0:T(1,128)}, u32[]{:S(2)}) copy-start(s32[1,1,12]{2,1,0:T(1,128)} %param.14) | copy-start | bytes 148
  54.9 18.5 %all-to-all-start.1 = ((f32[64,4,256]{2,1,0:T(4,128)}), f32[64,4,256]{2,1,0:T(4,128)S(1)}, u32[]{:S(2)}, u32[]{:S(2)}) async-start(f32[64,4,256]{2,1,0:T(4,128)} %copy.101), calls=%async_computation.1 | async-start | bytes 524288 | tf_op jit(solution)/shard_map/all_to_all | solution.py:172
  104.2 25.8 %all-to-all-start.2 = ((f32[9,64,384]{2,0,1:T(8,128)}), f32[9,64,384]{2,0,1:T(8,128)S(1)}, u32[]{:S(2)}, u32[]{:S(2)}) async-start(f32[9,64,384]{2,0,1:T(8,128)} %copy.102), calls=%async_computation.2 | async-start | bytes 3145728 | tf_op jit(solution)/shard_map/all_to_all | solution.py:198

commit v12 on v11

--- a/solution.py
+++ b/solution.py
@@ -170,7 +170,12 @@
     rendered, upstream = composite(arrived, orders, cotangent)
     sent_back = jnp.where(second_here[:, None, None], upstream[:, 1], upstream[:, 0])
     returned = lax.all_to_all(sent_back, "dom", split_axis=0, concat_axis=0, tiled=True)
-    slot_grads = jnp.take(returned, jnp.maximum(tile_ids, 0) // tiles_per, axis=0)
+    slot_grads = jnp.einsum(
+        "ds,dz->sz",
+        route,
+        returned.reshape(parts_count, 4 * pixels),
+        precision=lax.Precision.HIGHEST,
+    ).reshape(slots_count, 4, pixels)
 
     def backward_turn(turn_index, compact):
         first_row = turn_index * turn_rows

time: 133 us -> 130 us (0.977)
  the two profiles are of different devices: /device:TPU:136 before, /device:TPU:1 now
where the time goes in v12:
time: 130 us; the launch traced here: 129 us
  waiting for transfers between devices  45.8 us (35%)
  starting transfers between devices  32.5 us (25%)
  matrix products  31 us (24%)
  other arithmetic  9.68 us (7%)
  local copies, waits for them, and re-layouts  7.69 us (6%)
  between operations  1.63 us (1%)
    all_to_all x1, waiting for transfers between devices, local(): lax.all_to_all(placed, 'tile', split_axis=1, concat_axis=1, tiled=True)  20 us
    all_to_all x1, starting transfers between devices, local(): lax.all_to_all(payload, 'dom', split_axis=0, concat_axis=0, tiled=True)  18.9 us
    all_to_all x1, waiting for transfers between devices, local(): lax.all_to_all(payload, 'dom', split_axis=0, concat_axis=0, tiled=True)  13.2 us
    all_to_all x1, waiting for transfers between devices, local(): lax.all_to_all(sent_back, 'dom', split_axis=0, concat_axis=0, tiled=True)  12.6 us
    dot_general x6, matrix products, render(): jnp.einsum('kpg,gh->kph', log_keep, ahead, precision=lax.Precision.HIGHEST)  12.5 us
    all_to_all x1, starting transfers between devices, local(): lax.all_to_all(placed, 'tile', split_axis=1, concat_axis=1, tiled=True)  7.69 us
    dot_general x6, matrix products, render(): jnp.einsum('kpg,ckg->kcp', weight, params[6:9], precision=lax.Precision.H...  6.39 us
    dot_general x1, matrix products, local(): jnp.einsum('chl,le->hce', params.reshape(params.shape[0], hi_size, lo_siz...  6.22 us
  transfers between devices with their start and end apart: 3, of which 3 were waited for; matrix products, arithmetic and copies ran while one was open for 0% of the time, Pallas kernels for 0%

profile of v12, /device:TPU:1, one launch (start us, length us, event | category | flops | bytes accessed | tf_op | source)
XLA Modules:
  0.0 128.9 jit_solution(16427230962536710368)
XLA Ops:
  0.7 1.4 %fusion.151 = (s32[12]{0:T(128)S(1)}, f32[12]{0:T(128)S(1)}, s32[]{:T(128)}, s32[12]{0:T(128)S(1)}, s32[12]{0:T(128)S(1)}) fusion(s32[1,1,12]{2,1,0:T(1,128)} %param.14, s32[]{:T(128)S(6)} %mul.615), kind=kLoop, calls=%fused_computation.266 | loop fusion | flops 479 | bytes 248 | tf_op jit(solution)/shard_map/mul | solution.py:47
  2.7 0.1 convert_reduce_fusion
  2.8 0.7 fusion.157
  3.5 0.7 add_select_fusion
  4.2 0.9 concatenate.20
  5.2 1.0 copy.146
  6.2 0.1 copy.145
  6.3 0.1 fusion.111
  6.4 6.2 %fusion.91 = f32[9,3072]{1,0:T(8,128)S(1)} fusion(f32[64,3072]{1,0:T(8,128)S(1)} %get-tuple-element.251, s32[3072]{0:T(1024)S(1)} %get-tuple-element.243, f32[3,64,384]{2,1,0:T(8,128)S(1)} %bitcast.276, f32[1,64,384]{2,1,0:T(8,128)S(1)} %concatenate.20, f32[5,64,384]{2,1,0:T(8,128)S(1)} %bitcast.274), kind=kOutput, calls=%fused_computation.158 | convolution fusion | flops 8158860288 | bytes 1794048 | tf_op jit(solution)/shard_map/chl,le->hce/dot_general | solution.py:110
  12.7 0.1 convert_add_fusion
  12.8 8.1 %while.20 = (s32[]{:T(128)}, f32[12,4,256]{2,1,0:T(4,128)S(1)}, s32[]{:T(128)}, f32[9,12,256]{2,1,0:T(8,128)S(1)}, f32[12,256]{1,0:T(8,128)S(1)}, /*index=5*/f32...) while((s32[]{:T(128)}, f32[12,4,256]{2,1,0:T(4,128)S(1)}, ...), condition=%wide.region_4.5_spmd, body=%wide.region_2.4_spmd.sunk | while | flops 825316352 | bytes 2339135 | solution.py:134
  12.9 0.1 add_bitcast_fusion.6
  13.0 1.0 fusion.181
  14.0 1.9 %fusion.182 = f32[4,256,256]{2,1,0:T(8,128)S(1)} fusion(f32[4,256]{1,0:T(4,128)S(1)} %get-tuple-element.363, f32[4,256]{1,0:T(4,128)S(1)} %get-tuple-element.364, f32[4,256]{1,0:T(4,128)S(1)} %get-tuple-element.365, f32[4,256]{1,0:T(4,128)S(1)} %get-tuple-element.366, f32[4,256]{1,0:T(4,128)S(1)} %get-tuple-element.367, ...), kind=kOutput, calls=%fused_computation.7.clone.1 | convolution fusion | flops 812187648 | bytes 1081344 | tf_op jit(solution)/shard_map/while/body/kpg,gh->kph/dot_general | solution.py:34
  15.9 1.0 fusion.183
  17.0 0.1 add_bitcast_fusion.6
  17.0 1.0 fusion.181
  18.1 1.9 %fusion.182 = f32[4,256,256]{2,1,0:T(8,128)S(1)} fusion(f32[4,256]{1,0:T(4,128)S(1)} %get-tuple-element.363, f32[4,256]{1,0:T(4,128)S(1)} %get-tuple-element.364, f32[4,256]{1,0:T(4,128)S(1)} %get-tuple-element.365, f32[4,256]{1,0:T(4,128)S(1)} %get-tuple-element.366, f32[4,256]{1,0:T(4,128)S(1)} %get-tuple-element.367, ...), kind=kOutput, calls=%fused_computation.7.clone.1 | convolution fusion | flops 812187648 | bytes 1081344 | tf_op jit(solution)/shard_map/while/body/kpg,gh->kph/dot_general | solution.py:34
  19.9 1.0 fusion.183
  21.0 0.1 broadcast_in_dim.57
  21.1 0.4 fusion.102
  21.5 1.0 copy.87
  22.5 18.9 %all-to-all-start = ((f32[64,1,1152]{2,1,0:T(1,128)}), f32[64,1,1152]{2,1,0:T(1,128)S(1)}, u32[]{:S(2)}, u32[]{:S(2)}) async-start(f32[64,1,1152]{2,1,0:T(1,128)} %copy.87), calls=%async_computation | async-start | bytes 589824 | tf_op jit(solution)/shard_map/all_to_all | solution.py:159
  41.5 13.2 %all-to-all-done = f32[64,1,1152]{2,1,0:T(1,128)S(1)} async-done(((f32[64,1,1152]{2,1,0:T(1,128)}), f32[64,1,1152]{2,1,0:T(1,128)S(1)}, u32[]{:S(2)}, u32[]{:S(2)}) %all-to-all-start) | async-done | bytes 294944 | tf_op jit(solution)/shard_map/all_to_all | solution.py:159
  54.7 0.1 fusion.137
  54.9 0.1 reshape.592
  55.0 0.1 copy_select_fusion.1
  55.1 0.5 fusion.113
  55.6 0.3 fusion.105
  55.9 0.1 multiply_reduce_fusion.1
  56.0 0.2 fusion.104
  56.2 0.4 convolution_bitcast_fusion
  56.6 0.1 fusion.123
  56.7 0.9 copy.94
  57.6 5.9 %all-to-all-start.1 = ((f32[64,4,256]{2,1,0:T(4,128)}), f32[64,4,256]{2,1,0:T(4,128)S(1)}, u32[]{:S(2)}, u32[]{:S(2)}) async-start(f32[64,4,256]{2,1,0:T(4,128)} %copy.94), calls=%async_computation.1 | async-start | bytes 524288 | tf_op jit(solution)/shard_map/all_to_all | solution.py:172
  63.5 12.6 %all-to-all-done.1 = f32[64,4,256]{2,1,0:T(4,128)S(1)} async-done(((f32[64,4,256]{2,1,0:T(4,128)}), f32[64,4,256]{2,1,0:T(4,128)S(1)}, u32[]{:S(2)}, u32[]{:S(2)}) %all-to-all-start.1) | async-done | bytes 262176 | tf_op jit(solution)/shard_map/all_to_all | solution.py:172
  76.1 0.2 fusion.120
  76.3 16.3 %while.21 = (s32[]{:T(128)}, f32[9,12,256]{2,1,0:T(8,128)S(1)}, s32[]{:T(128)}, f32[12,4,256]{2,0,1:T(8,128)S(1)}, f32[9,12,256]{2,1,0:T(8,128)S(1)}, /*index=5*...) while((s32[]{:T(128)}, f32[9,12,256]{2,1,0:T(8,128)S(1)}, ...), condition=%wide.region_16.17_spmd, body=%wide.region_8.16_spmd.sunk | while | flops 1655438336 | bytes 5763435 | solution.py:188
  76.6 0.1 add_bitcast_fusion.7
  76.7 1.0 log-plus-one_reduce_fusion.2
  77.8 1.0 fusion.190
  78.8 1.5 %convolution_exponential_fusion.4 = f32[4,256,256]{2,1,0:T(8,128)S(1)} fusion(f32[4,256]{1,0:T(4,128)S(1)} %get-tuple-element.381, f32[4,256]{1,0:T(4,128)S(1)} %get-tuple-element.378, f32[4,256]{1,0:T(4,128)S(1)} %get-tuple-element.379, f32[4,256]{1,0:T(4,128)S(1)} %get-tuple-element.382, f32[4,256]{1,0:T(4,128)S(1)} %get-tuple-element.380, ...), kind=kOutput, calls=%fused_computation.57.clone.1 | convolution fusion | flops 808779776 | bytes 1081344 | tf_op jit(solution)/shard_map/while/body/jvp(kpg,gh->kph)/dot_general | solution.py:34
  80.3 3.0 %fusion.192 = (f32[4,256]{1,0:T(4,128)S(1)}, f32[4,256]{1,0:T(4,128)S(1)}, f32[4,256]{1,0:T(4,128)S(1)}, f32[4,256]{1,0:T(4,128)S(1)}, f32[4,256]{1,0:T(4,128)S(1)}, /*index=5*/f32[4,256]{1,0:T(4,128)S(1)}) fusion(f32[4,256]{1,0:T(4,128)S(1)} %get-tuple-element.378, f32[4,256]{1,0:T(4,128)S(1)} %get-tuple-element.379, ...), kind=kOutput, calls=%fused_computation.70.clone.1 | convolution fusion | flops 820570112 | bytes 2158592 | tf_op jit(solution)/shard_map/while/body/transpose(jvp(kpg,gh->kph))/dot_general | solution.py:34
  83.2 1.2 fusion.195
  84.5 0.1 fusion.193
  84.7 0.1 add_bitcast_fusion.7
  84.8 1.0 log-plus-one_reduce_fusion.2
  85.8 1.0 fusion.190
  86.9 1.5 %convolution_exponential_fusion.4 = f32[4,256,256]{2,1,0:T(8,128)S(1)} fusion(f32[4,256]{1,0:T(4,128)S(1)} %get-tuple-element.381, f32[4,256]{1,0:T(4,128)S(1)} %get-tuple-element.378, f32[4,256]{1,0:T(4,128)S(1)} %get-tuple-element.379, f32[4,256]{1,0:T(4,128)S(1)} %get-tuple-element.382, f32[4,256]{1,0:T(4,128)S(1)} %get-tuple-element.380, ...), kind=kOutput, calls=%fused_computation.57.clone.1 | convolution fusion | flops 808779776 | bytes 1081344 | tf_op jit(solution)/shard_map/while/body/jvp(kpg,gh->kph)/dot_general | solution.py:34
  88.3 3.0 %fusion.192 = (f32[4,256]{1,0:T(4,128)S(1)}, f32[4,256]{1,0:T(4,128)S(1)}, f32[4,256]{1,0:T(4,128)S(1)}, f32[4,256]{1,0:T(4,128)S(1)}, f32[4,256]{1,0:T(4,128)S(1)}, /*index=5*/f32[4,256]{1,0:T(4,128)S(1)}) fusion(f32[4,256]{1,0:T(4,128)S(1)} %get-tuple-element.378, f32[4,256]{1,0:T(4,128)S(1)} %get-tuple-element.379, ...), kind=kOutput, calls=%fused_computation.70.clone.1 | convolution fusion | flops 820570112 | bytes 2158592 | tf_op jit(solution)/shard_map/while/body/transpose(jvp(kpg,gh->kph))/dot_general | solution.py:34
  91.3 1.2 fusion.195
  92.5 0.1 fusion.193
  92.7 0.1 copy.117
  92.8 3.9 %fusion.92 = f32[9,64,384]{2,1,0:T(8,128)S(1)} fusion(f32[64,3072]{1,0:T(8,128)S(1)} %get-tuple-element.252, f32[9,3072]{1,0:T(8,128)S(1)} %bitcast.279, s32[3072]{0:T(1024)S(1)} %get-tuple-element.240), kind=kOutput, calls=%fused_computation.159 | convolution fusion | flops 4079812608 | bytes 1794048 | tf_op jit(solution)/shard_map/che,le->chl/dot_general | solution.py:202
  96.7 1.7 %copy.97 = f32[9,64,384]{2,0,1:T(8,128)} copy(f32[9,64,384]{2,1,0:T(8,128)S(1)} %fusion.92) | data formatting | bytes 1769472 | tf_op jit(solution)/shard_map/che,le->chl/dot_general | solution.py:202
  98.4 7.7 %all-to-all-start.2 = ((f32[9,64,384]{2,0,1:T(8,128)}), f32[9,64,384]{2,0,1:T(8,128)S(1)}, u32[]{:S(2)}, u32[]{:S(2)}) async-start(f32[9,64,384]{2,0,1:T(8,128)} %copy.97), calls=%async_computation.2 | async-start | bytes 3145728 | tf_op jit(solution)/shard_map/all_to_all | solution.py:203
  106.1 0.6 copy.98
  106.7 20.0 %all-to-all-done.2 = f32[9,64,384]{2,0,1:T(8,128)S(1)} async-done(((f32[9,64,384]{2,0,1:T(8,128)}), f32[9,64,384]{2,0,1:T(8,128)S(1)}, u32[]{:S(2)}, u32[]{:S(2)}) %all-to-all-start.2) | async-done | bytes 884768 | tf_op jit(solution)/shard_map/all_to_all | solution.py:203
  126.7 0.1 slice.105
  126.8 0.6 squeeze_reshape.3
  127.4 0.1 slice.104
  127.5 0.7 reduce_sum.177
  128.2 0.1 slice.106
  128.3 0.7 reduce_sum.179
  (56 shorter events, 0.7 us)
Async XLA Ops:
  0.6 5.6 %copy-start = (f32[5,24576]{1,0:T(8,128)S(1)}, f32[5,24576]{1,0:T(8,128)}, u32[]{:S(2)}) copy-start(f32[5,24576]{1,0:T(8,128)} %param.11) | copy-start | bytes 1474564
  6.4 6.4 %copy-start.1 = (f32[4,256]{1,0:T(4,128)S(1)}, f32[4,256]{1,0:T(4,128)}, u32[]{:S(2)}) copy-start(f32[4,256]{1,0:T(4,128)} %constant.162.clone.1) | copy-start | bytes 12292
  12.8 8.3 %copy-start.2 = (f32[1152]{0:T(1024)S(1)}, f32[1152]{0:T(1024)}, u32[]{:S(2)}) copy-start(f32[1152]{0:T(1024)} %constant.173.clone.1) | copy-start | bytes 13828
  21.0 20.5 %copy-start.3 = (f32[3,2,256]{2,1,0:T(2,128)S(1)}, f32[3,2,256]{2,1,0:T(2,128)}, u32[]{:S(2)}) copy-start(f32[3,2,256]{2,1,0:T(2,128)} %param.17) | copy-start | bytes 18436
  22.5 32.6 %copy-start.4 = (s32[2,64]{1,0:T(2,128)S(1)}, s32[2,64]{1,0:T(2,128)}, u32[]{:S(2)}) copy-start(s32[2,64]{1,0:T(2,128)} %param.16) | copy-start | bytes 1540
  22.5 32.2 %all-to-all-start = ((f32[64,1,1152]{2,1,0:T(1,128)}), f32[64,1,1152]{2,1,0:T(1,128)S(1)}, u32[]{:S(2)}, u32[]{:S(2)}) async-start(f32[64,1,1152]{2,1,0:T(1,128)} %copy.87), calls=%async_computation | async-start | bytes 589824 | tf_op jit(solution)/shard_map/all_to_all | solution.py:159
  57.6 18.5 %all-to-all-start.1 = ((f32[64,4,256]{2,1,0:T(4,128)}), f32[64,4,256]{2,1,0:T(4,128)S(1)}, u32[]{:S(2)}, u32[]{:S(2)}) async-start(f32[64,4,256]{2,1,0:T(4,128)} %copy.94), calls=%async_computation.1 | async-start | bytes 524288 | tf_op jit(solution)/shard_map/all_to_all | solution.py:172
  98.4 28.3 %all-to-all-start.2 = ((f32[9,64,384]{2,0,1:T(8,128)}), f32[9,64,384]{2,0,1:T(8,128)S(1)}, u32[]{:S(2)}, u32[]{:S(2)}) async-start(f32[9,64,384]{2,0,1:T(8,128)} %copy.97), calls=%async_computation.2 | async-start | bytes 3145728 | tf_op jit(solution)/shard_map/all_to_all | solution.py:203

commit v13 on v12

--- a/solution.py
+++ b/solution.py
@@ -71,7 +71,7 @@
     grad_transmit = behind / transmit
     grad_ordered = jnp.concatenate([grad_colour, grad_transmit[:, :, None, :]], axis=2)
     upstream = jnp.einsum(
-        "irk,ircp->kicp", ranks_onehot, grad_ordered, precision=lax.Precision.HIGHEST
+        "irk,ircp->kicp", ranks_onehot, grad_ordered, precision=lax.Precision.HIGH
     )
     return (jnp.transpose(rendered, (1, 0, 2)), upstream)
 

time: 130 us -> 129 us (level)
  starting transfers between devices: 32.5 us -> 30.8 us
    all_to_all x1, starting transfers between devices: 18.9 us -> 17.2 us  [local(): lax.all_to_all(payload, 'dom', split_axis=0, concat_axis=0, tiled=True)]
where the time goes in v13:
time: 129 us; the launch traced here: 127 us
  waiting for transfers between devices  45.8 us (36%)
  matrix products  30.9 us (24%)
  starting transfers between devices  30.8 us (24%)
  other arithmetic  9.68 us (8%)
  local copies, waits for them, and re-layouts  7.69 us (6%)
  between operations  1.63 us (1%)
    all_to_all x1, waiting for transfers between devices, local(): lax.all_to_all(placed, 'tile', split_axis=1, concat_axis=1, tiled=True)  20 us
    all_to_all x1, starting transfers between devices, local(): lax.all_to_all(payload, 'dom', split_axis=0, concat_axis=0, tiled=True)  17.2 us
    all_to_all x1, waiting for transfers between devices, local(): lax.all_to_all(payload, 'dom', split_axis=0, concat_axis=0, tiled=True)  13.2 us
    all_to_all x1, waiting for transfers between devices, local(): lax.all_to_all(sent_back, 'dom', split_axis=0, concat_axis=0, tiled=True)  12.6 us
    dot_general x6, matrix products, render(): jnp.einsum('kpg,gh->kph', log_keep, ahead, precision=lax.Precision.HIGHEST)  12.5 us
    all_to_all x1, starting transfers between devices, local(): lax.all_to_all(placed, 'tile', split_axis=1, concat_axis=1, tiled=True)  7.69 us
    dot_general x6, matrix products, render(): jnp.einsum('kpg,ckg->kcp', weight, params[6:9], precision=lax.Precision.H...  6.4 us
    dot_general x1, matrix products, local(): jnp.einsum('chl,le->hce', params.reshape(params.shape[0], hi_size, lo_siz...  6.22 us
  transfers between devices with their start and end apart: 3, of which 3 were waited for; matrix products, arithmetic and copies ran while one was open for 0% of the time, Pallas kernels for 0%

profile of v13, /device:TPU:1, one launch (start us, length us, event | category | flops | bytes accessed | tf_op | source)
XLA Modules:
  0.0 127.1 jit_solution(14202906185547453091)
XLA Ops:
  0.7 1.4 %fusion.151 = (s32[12]{0:T(128)S(1)}, f32[12]{0:T(128)S(1)}, s32[]{:T(128)}, s32[12]{0:T(128)S(1)}, s32[12]{0:T(128)S(1)}) fusion(s32[1,1,12]{2,1,0:T(1,128)} %param.14, s32[]{:T(128)S(6)} %mul.615), kind=kLoop, calls=%fused_computation.266 | loop fusion | flops 479 | bytes 248 | tf_op jit(solution)/shard_map/mul | solution.py:47
  2.7 0.1 convert_reduce_fusion
  2.8 0.7 fusion.157
  3.5 0.7 add_select_fusion
  4.2 0.9 concatenate.20
  5.2 1.0 copy.146
  6.2 0.1 copy.145
  6.3 0.1 fusion.111
  6.4 6.2 %fusion.91 = f32[9,3072]{1,0:T(8,128)S(1)} fusion(f32[64,3072]{1,0:T(8,128)S(1)} %get-tuple-element.251, s32[3072]{0:T(1024)S(1)} %get-tuple-element.243, f32[3,64,384]{2,1,0:T(8,128)S(1)} %bitcast.276, f32[1,64,384]{2,1,0:T(8,128)S(1)} %concatenate.20, f32[5,64,384]{2,1,0:T(8,128)S(1)} %bitcast.274), kind=kOutput, calls=%fused_computation.158 | convolution fusion | flops 8158860288 | bytes 1794048 | tf_op jit(solution)/shard_map/chl,le->hce/dot_general | solution.py:110
  12.7 0.1 convert_add_fusion
  12.8 8.1 %while.20 = (s32[]{:T(128)}, f32[12,4,256]{2,1,0:T(4,128)S(1)}, s32[]{:T(128)}, f32[9,12,256]{2,1,0:T(8,128)S(1)}, f32[12,256]{1,0:T(8,128)S(1)}, /*index=5*/f32...) while((s32[]{:T(128)}, f32[12,4,256]{2,1,0:T(4,128)S(1)}, ...), condition=%wide.region_4.5_spmd, body=%wide.region_2.4_spmd.sunk | while | flops 825316352 | bytes 2339135 | solution.py:134
  12.9 0.1 add_bitcast_fusion.6
  13.0 1.0 fusion.181
  14.0 1.9 %fusion.182 = f32[4,256,256]{2,1,0:T(8,128)S(1)} fusion(f32[4,256]{1,0:T(4,128)S(1)} %get-tuple-element.363, f32[4,256]{1,0:T(4,128)S(1)} %get-tuple-element.364, f32[4,256]{1,0:T(4,128)S(1)} %get-tuple-element.365, f32[4,256]{1,0:T(4,128)S(1)} %get-tuple-element.366, f32[4,256]{1,0:T(4,128)S(1)} %get-tuple-element.367, ...), kind=kOutput, calls=%fused_computation.7.clone.1 | convolution fusion | flops 812187648 | bytes 1081344 | tf_op jit(solution)/shard_map/while/body/kpg,gh->kph/dot_general | solution.py:34
  15.9 1.0 fusion.183
  17.0 0.1 add_bitcast_fusion.6
  17.0 1.0 fusion.181
  18.1 1.9 %fusion.182 = f32[4,256,256]{2,1,0:T(8,128)S(1)} fusion(f32[4,256]{1,0:T(4,128)S(1)} %get-tuple-element.363, f32[4,256]{1,0:T(4,128)S(1)} %get-tuple-element.364, f32[4,256]{1,0:T(4,128)S(1)} %get-tuple-element.365, f32[4,256]{1,0:T(4,128)S(1)} %get-tuple-element.366, f32[4,256]{1,0:T(4,128)S(1)} %get-tuple-element.367, ...), kind=kOutput, calls=%fused_computation.7.clone.1 | convolution fusion | flops 812187648 | bytes 1081344 | tf_op jit(solution)/shard_map/while/body/kpg,gh->kph/dot_general | solution.py:34
  19.9 1.0 fusion.183
  21.0 0.1 broadcast_in_dim.57
  21.1 0.4 fusion.102
  21.5 1.0 copy.87
  22.5 17.2 %all-to-all-start = ((f32[64,1,1152]{2,1,0:T(1,128)}), f32[64,1,1152]{2,1,0:T(1,128)S(1)}, u32[]{:S(2)}, u32[]{:S(2)}) async-start(f32[64,1,1152]{2,1,0:T(1,128)} %copy.87), calls=%async_computation | async-start | bytes 589824 | tf_op jit(solution)/shard_map/all_to_all | solution.py:159
  39.8 13.2 %all-to-all-done = f32[64,1,1152]{2,1,0:T(1,128)S(1)} async-done(((f32[64,1,1152]{2,1,0:T(1,128)}), f32[64,1,1152]{2,1,0:T(1,128)S(1)}, u32[]{:S(2)}, u32[]{:S(2)}) %all-to-all-start) | async-done | bytes 294944 | tf_op jit(solution)/shard_map/all_to_all | solution.py:159
  53.0 0.1 fusion.137
  53.1 0.1 reshape.592
  53.3 0.1 copy_select_fusion.1
  53.4 0.5 fusion.113
  53.9 0.3 fusion.105
  54.2 0.1 multiply_reduce_fusion.1
  54.3 0.2 fusion.104
  54.5 0.3 convolution_bitcast_fusion
  54.8 0.1 fusion.123
  54.9 0.9 copy.94
  55.8 5.9 %all-to-all-start.1 = ((f32[64,4,256]{2,1,0:T(4,128)}), f32[64,4,256]{2,1,0:T(4,128)S(1)}, u32[]{:S(2)}, u32[]{:S(2)}) async-start(f32[64,4,256]{2,1,0:T(4,128)} %copy.94), calls=%async_computation.1 | async-start | bytes 524288 | tf_op jit(solution)/shard_map/all_to_all | solution.py:172
  61.7 12.6 %all-to-all-done.1 = f32[64,4,256]{2,1,0:T(4,128)S(1)} async-done(((f32[64,4,256]{2,1,0:T(4,128)}), f32[64,4,256]{2,1,0:T(4,128)S(1)}, u32[]{:S(2)}, u32[]{:S(2)}) %all-to-all-start.1) | async-done | bytes 262176 | tf_op jit(solution)/shard_map/all_to_all | solution.py:172
  74.3 0.2 fusion.120
  74.5 16.3 %while.21 = (s32[]{:T(128)}, f32[9,12,256]{2,1,0:T(8,128)S(1)}, s32[]{:T(128)}, f32[12,4,256]{2,0,1:T(8,128)S(1)}, f32[9,12,256]{2,1,0:T(8,128)S(1)}, /*index=5*...) while((s32[]{:T(128)}, f32[9,12,256]{2,1,0:T(8,128)S(1)}, ...), condition=%wide.region_16.17_spmd, body=%wide.region_8.16_spmd.sunk | while | flops 1655438336 | bytes 5763435 | solution.py:188
  74.8 0.1 add_bitcast_fusion.7
  74.9 1.0 log-plus-one_reduce_fusion.2
  75.9 1.0 fusion.190
  77.0 1.5 %convolution_exponential_fusion.4 = f32[4,256,256]{2,1,0:T(8,128)S(1)} fusion(f32[4,256]{1,0:T(4,128)S(1)} %get-tuple-element.381, f32[4,256]{1,0:T(4,128)S(1)} %get-tuple-element.378, f32[4,256]{1,0:T(4,128)S(1)} %get-tuple-element.379, f32[4,256]{1,0:T(4,128)S(1)} %get-tuple-element.382, f32[4,256]{1,0:T(4,128)S(1)} %get-tuple-element.380, ...), kind=kOutput, calls=%fused_computation.57.clone.1 | convolution fusion | flops 808779776 | bytes 1081344 | tf_op jit(solution)/shard_map/while/body/jvp(kpg,gh->kph)/dot_general | solution.py:34
  78.5 3.0 %fusion.192 = (f32[4,256]{1,0:T(4,128)S(1)}, f32[4,256]{1,0:T(4,128)S(1)}, f32[4,256]{1,0:T(4,128)S(1)}, f32[4,256]{1,0:T(4,128)S(1)}, f32[4,256]{1,0:T(4,128)S(1)}, /*index=5*/f32[4,256]{1,0:T(4,128)S(1)}) fusion(f32[4,256]{1,0:T(4,128)S(1)} %get-tuple-element.378, f32[4,256]{1,0:T(4,128)S(1)} %get-tuple-element.379, ...), kind=kOutput, calls=%fused_computation.70.clone.1 | convolution fusion | flops 820570112 | bytes 2158592 | tf_op jit(solution)/shard_map/while/body/transpose(jvp(kpg,gh->kph))/dot_general | solution.py:34
  81.4 1.2 fusion.195
  82.7 0.1 fusion.193
  82.9 0.1 add_bitcast_fusion.7
  83.0 1.0 log-plus-one_reduce_fusion.2
  84.0 1.0 fusion.190
  85.1 1.5 %convolution_exponential_fusion.4 = f32[4,256,256]{2,1,0:T(8,128)S(1)} fusion(f32[4,256]{1,0:T(4,128)S(1)} %get-tuple-element.381, f32[4,256]{1,0:T(4,128)S(1)} %get-tuple-element.378, f32[4,256]{1,0:T(4,128)S(1)} %get-tuple-element.379, f32[4,256]{1,0:T(4,128)S(1)} %get-tuple-element.382, f32[4,256]{1,0:T(4,128)S(1)} %get-tuple-element.380, ...), kind=kOutput, calls=%fused_computation.57.clone.1 | convolution fusion | flops 808779776 | bytes 1081344 | tf_op jit(solution)/shard_map/while/body/jvp(kpg,gh->kph)/dot_general | solution.py:34
  86.5 3.0 %fusion.192 = (f32[4,256]{1,0:T(4,128)S(1)}, f32[4,256]{1,0:T(4,128)S(1)}, f32[4,256]{1,0:T(4,128)S(1)}, f32[4,256]{1,0:T(4,128)S(1)}, f32[4,256]{1,0:T(4,128)S(1)}, /*index=5*/f32[4,256]{1,0:T(4,128)S(1)}) fusion(f32[4,256]{1,0:T(4,128)S(1)} %get-tuple-element.378, f32[4,256]{1,0:T(4,128)S(1)} %get-tuple-element.379, ...), kind=kOutput, calls=%fused_computation.70.clone.1 | convolution fusion | flops 820570112 | bytes 2158592 | tf_op jit(solution)/shard_map/while/body/transpose(jvp(kpg,gh->kph))/dot_general | solution.py:34
  89.5 1.2 fusion.195
  90.7 0.1 fusion.193
  90.9 0.1 copy.117
  91.0 3.9 %fusion.92 = f32[9,64,384]{2,1,0:T(8,128)S(1)} fusion(f32[64,3072]{1,0:T(8,128)S(1)} %get-tuple-element.252, f32[9,3072]{1,0:T(8,128)S(1)} %bitcast.279, s32[3072]{0:T(1024)S(1)} %get-tuple-element.240), kind=kOutput, calls=%fused_computation.159 | convolution fusion | flops 4079812608 | bytes 1794048 | tf_op jit(solution)/shard_map/che,le->chl/dot_general | solution.py:202
  94.9 1.7 %copy.97 = f32[9,64,384]{2,0,1:T(8,128)} copy(f32[9,64,384]{2,1,0:T(8,128)S(1)} %fusion.92) | data formatting | bytes 1769472 | tf_op jit(solution)/shard_map/che,le->chl/dot_general | solution.py:202
  96.6 7.7 %all-to-all-start.2 = ((f32[9,64,384]{2,0,1:T(8,128)}), f32[9,64,384]{2,0,1:T(8,128)S(1)}, u32[]{:S(2)}, u32[]{:S(2)}) async-start(f32[9,64,384]{2,0,1:T(8,128)} %copy.97), calls=%async_computation.2 | async-start | bytes 3145728 | tf_op jit(solution)/shard_map/all_to_all | solution.py:203
  104.3 0.6 copy.98
  104.9 20.0 %all-to-all-done.2 = f32[9,64,384]{2,0,1:T(8,128)S(1)} async-done(((f32[9,64,384]{2,0,1:T(8,128)}), f32[9,64,384]{2,0,1:T(8,128)S(1)}, u32[]{:S(2)}, u32[]{:S(2)}) %all-to-all-start.2) | async-done | bytes 884768 | tf_op jit(solution)/shard_map/all_to_all | solution.py:203
  124.9 0.1 slice.105
  125.0 0.6 squeeze_reshape.3
  125.6 0.1 slice.104
  125.7 0.7 reduce_sum.177
  126.4 0.1 slice.106
  126.5 0.7 reduce_sum.179
  (56 shorter events, 0.7 us)
Async XLA Ops:
  0.6 5.6 %copy-start = (f32[5,24576]{1,0:T(8,128)S(1)}, f32[5,24576]{1,0:T(8,128)}, u32[]{:S(2)}) copy-start(f32[5,24576]{1,0:T(8,128)} %param.11) | copy-start | bytes 1474564
  6.4 6.4 %copy-start.1 = (f32[4,256]{1,0:T(4,128)S(1)}, f32[4,256]{1,0:T(4,128)}, u32[]{:S(2)}) copy-start(f32[4,256]{1,0:T(4,128)} %constant.162.clone.1) | copy-start | bytes 12292
  12.8 8.3 %copy-start.2 = (f32[1152]{0:T(1024)S(1)}, f32[1152]{0:T(1024)}, u32[]{:S(2)}) copy-start(f32[1152]{0:T(1024)} %constant.173.clone.1) | copy-start | bytes 13828
  21.0 18.8 %copy-start.3 = (f32[3,2,256]{2,1,0:T(2,128)S(1)}, f32[3,2,256]{2,1,0:T(2,128)}, u32[]{:S(2)}) copy-start(f32[3,2,256]{2,1,0:T(2,128)} %param.17) | copy-start | bytes 18436
  22.5 30.9 %copy-start.4 = (s32[2,64]{1,0:T(2,128)S(1)}, s32[2,64]{1,0:T(2,128)}, u32[]{:S(2)}) copy-start(s32[2,64]{1,0:T(2,128)} %param.16) | copy-start | bytes 1540
  22.5 30.5 %all-to-all-start = ((f32[64,1,1152]{2,1,0:T(1,128)}), f32[64,1,1152]{2,1,0:T(1,128)S(1)}, u32[]{:S(2)}, u32[]{:S(2)}) async-start(f32[64,1,1152]{2,1,0:T(1,128)} %copy.87), calls=%async_computation | async-start | bytes 589824 | tf_op jit(solution)/shard_map/all_to_all | solution.py:159
  55.8 18.5 %all-to-all-start.1 = ((f32[64,4,256]{2,1,0:T(4,128)}), f32[64,4,256]{2,1,0:T(4,128)S(1)}, u32[]{:S(2)}, u32[]{:S(2)}) async-start(f32[64,4,256]{2,1,0:T(4,128)} %copy.94), calls=%async_computation.1 | async-start | bytes 524288 | tf_op jit(solution)/shard_map/all_to_all | solution.py:172
  96.6 28.3 %all-to-all-start.2 = ((f32[9,64,384]{2,0,1:T(8,128)}), f32[9,64,384]{2,0,1:T(8,128)S(1)}, u32[]{:S(2)}, u32[]{:S(2)}) async-start(f32[9,64,384]{2,0,1:T(8,128)} %copy.97), calls=%async_computation.2 | async-start | bytes 3145728 | tf_op jit(solution)/shard_map/all_to_all | solution.py:203
